TPU v7x, 256 devices: a whole 4x4x8 slice. The times are simulated.
256 devices in a mesh: row: 8 (over x_lo, y), col: 32 (over z, x_hi, core).
Axes of the slice: x: 4 (x_hi: 2, x_lo: 2; x = x_hi * 2 + x_lo), y: 4, z: 8, core: 2. Of those that a mesh axis runs over, the one named last changes fastest.
Arguments:
- a_blocks: float32 [32, 8, 32, 4096], P('col', 'row'), may hold values from -0.25 to 0.25
- a_rows: int32 [32, 8, 32], P('col', 'row'), may hold values from 0 to 32, as said below
- a_slots: int32 [32, 8, 32], P('col', 'row'), may hold values from 0 to 23, as said below
- b_stripes: float32 [192, 64, 1024], P('col', None, 'row'), may hold values from -6 to 6
Outputs:
- product: float32 [65536, 1024], P('col', 'row')
Inputs may be any that keep to these rules, and one draw needn't show every extreme that they name: `a_rows`: in each group and panel the used slots (row below 32) come first, in rising order of the pair (row, stripe), no pair twice; the remaining slots hold 32. In every draw one group has all 32 slots of all its panels used; in the others each panel uses between a quarter and five eighths of them. `a_slots`: stripe of each slot within its panel; empty slots hold 0.
All inputs are finite; a program needn't handle non-finite values.
Results may differ from a plain program's by a relative error of at most 0.0003.
Values sent between devices are 32-bit elements; how exact they have to be, the bound alone decides.
No kernel may reach another device: no remote copies, remote signals or barrier semaphores. Data moves between devices by JAX's collectives and lax.ppermute only.
A program may use at most 64 MiB of HBM per device.

v0:
```python
import jax
import jax.numpy as jnp
from jax import lax
from jax.sharding import Mesh
from jax.sharding import PartitionSpec as P

BLK = 64
MB = 32

AXES = ("xl", "y", "z", "xh", "core")
ROW = ("xl", "y")
COL = ("z", "xh", "core")


def swap(block, axis):
    return lax.ppermute(block, axis, [(0, 1), (1, 0)])


def shift(block, axis, distance):
    n = lax.axis_size(axis)
    return lax.ppermute(block, axis, [(i, (i + distance) % n) for i in range(n)])


def gather_a(a_own):
    n_y = lax.axis_size("y")
    xl = lax.axis_index("xl")
    y = lax.axis_index("y")
    a_x = swap(a_own, "xl")
    bundle = jnp.stack([a_own, a_x])
    from_minus = shift(bundle, "y", 1)
    from_plus = shift(bundle, "y", -1)
    far_a = shift(from_plus[0], "y", -1)
    far_b = shift(from_minus[1], "y", 1)
    panels = [a_own, a_x, from_minus[0], from_minus[1], from_plus[0], from_plus[1], far_a, far_b]
    ys = [y, y, y - 1, y - 1, y + 1, y + 1, y + 2, y + 2]
    xls = [xl, 1 - xl] * 4
    pid = jnp.stack([xls[k] * n_y + (ys[k] % n_y) for k in range(8)]).astype(jnp.int32)
    return jnp.stack(panels), pid


def gather_b(b_own):
    n_z = lax.axis_size("z")
    xh = lax.axis_index("xh")
    core = lax.axis_index("core")
    b_h = swap(b_own, "xh")
    pair = jnp.where(xh == 0, jnp.stack([b_own, b_h]), jnp.stack([b_h, b_own]))
    by_offset = [None] * n_z
    by_offset[0] = pair
    up = pair
    down = pair
    half = n_z // 2
    for d in range(1, half):
        up = shift(up, "z", -1)
        down = shift(down, "z", 1)
        by_offset[d] = up
        by_offset[n_z - d] = down
    far_up = shift(up[0], "z", -1)
    far_down = shift(down[1], "z", 1)
    by_offset[half] = jnp.stack([far_up, far_down])
    mine = jnp.stack(by_offset)
    other = swap(mine, "core")
    return jnp.where(core == 0, jnp.stack([mine, other]), jnp.stack([other, mine]))


def shards(a_blocks, a_rows, a_slots, b_stripes):
    n_z = lax.axis_size("z")
    z = lax.axis_index("z")
    columns = b_stripes.shape[2]
    highest = lax.Precision.HIGHEST

    ints = jnp.stack([a_rows[0, 0], a_slots[0, 0]])
    all_ints = lax.all_gather(ints, ROW, axis=0, tiled=False)

    a_all, pid = gather_a(a_blocks[0, 0])
    table = gather_b(b_stripes)
    table = table.reshape(-1, BLK, columns)

    ints_k = jnp.take(all_ints, pid, axis=0)
    rows = ints_k[:, 0]
    slots = ints_k[:, 1]
    d = (pid[:, None] - z) % n_z
    index = (((slots // 6) % 2 * n_z + d) * 2 + slots // 12) * 6 + slots % 6
    chosen = jnp.take(table, index.reshape(-1), axis=0)
    left = a_all.reshape(-1, BLK, BLK)
    terms = jnp.einsum("gij,gjc->gic", left, chosen, precision=highest)
    place = (rows.reshape(-1)[:, None] == jnp.arange(MB, dtype=jnp.int32)[None, :]).astype(jnp.float32)
    out = jnp.einsum("gm,gic->mic", place, terms, precision=highest)
    return out.reshape(MB * BLK, columns)


def solution(mesh):
    fine = Mesh(mesh.devices.reshape(2, 4, 8, 2, 2), AXES)
    return jax.shard_map(
        shards,
        mesh=fine,
        in_specs=(
            P(COL, ROW, None, None),
            P(COL, ROW, None),
            P(COL, ROW, None),
            P(COL, None, ROW),
        ),
        out_specs=P(COL, ROW),
        check_vma=False,
    )
```

profile of v0, /device:TPU:2, one launch (start us, length us, event | category | flops | bytes accessed | tf_op | source)
XLA Modules:
  0.0 137.3 jit_solution(8136391173583100333)
XLA Ops:
  0.0 2.1 %collective-permute-start.5 = (f32[6,64,128]{2,1,0:T(8,128)}, f32[6,64,128]{2,1,0:T(8,128)S(1)}, u32[]{:S(2)}, u32[]{:S(2)}) collective-permute-start(f32[6,64,128]{2,1,0:T(8,128)} %param.7), channel_id=1, source_target_pairs={{0,2},{2,0},{1,3},{3,1},{4,6},{6,4},{5,7},{7,5},{8,10},{10,8},{9,1... | collective-permute-start | bytes 589832 | tf_op jit(solution)/shard_map/ppermute | solution.py:16
  2.1 1.4 %collective-permute-start = (f32[32,4096]{1,0:T(8,128)}, f32[32,4096]{1,0:T(8,128)}, u32[]{:S(2)}, u32[]{:S(2)}) collective-permute-start(f32[32,4096]{1,0:T(8,128)} %bitcast.75), channel_id=1, source_target_pairs={{0,128},{128,0},{1,129},{129,1},{2,130},{130,2},{3,131},{131,3},{4... | collective-permute-start | bytes 1572872 | tf_op jit(solution)/shard_map/ppermute | solution.py:16
  3.6 2.0 %constant_dynamic-update-slice_fusion.3 = f32[8,32,4096]{2,1,0:T(8,128)} fusion(f32[1,1,32,4096]{3,2,1,0:T(8,128)} %param.4), kind=kLoop, calls=%fused_computation.32 | loop fusion | bytes 1048576
  6.6 24.6 %all-gather.1 = s32[8,2,32]{2,1,0:T(2,128)S(1)} all-gather(s32[1,2,32]{2,1,0:T(2,128)S(1)} %add_bitcast_fusion), channel_id=2, replica_groups=mesh['xl'=2,'y'=4,'z'=8,'xh'=2,'core'=2] {'xl','y'}, dimensions={0}, use_global_device_ids=true | all-gather | bytes 2304 | tf_op jit(solution)/shard_map/all_gather | solution.py:72
  35.2 2.0 %collective-permute-start.10 = (f32[2,6,64,128]{3,2,1,0:T(8,128)S(1)}, f32[2,6,64,128]{3,2,1,0:T(8,128)S(1)}, u32[]{:S(2)}, u32[]{:S(2)}) collective-permute-start(f32[2,6,64,128]{3,2,1,0:T(8,128)S(1)} %maximum_select_fusion.2), channel_id=1, source_target_pairs={{0,4},{4,8},{8,12},{12,16},{16,20},{20,24},{24,28},{28,0},{1,5},{5... | collective-permute-start | bytes 1179656 | tf_op jit(solution)/shard_map/ppermute | solution.py:21
  37.2 4.0 %collective-permute-start.6 = (f32[2,6,64,128]{3,2,1,0:T(8,128)S(1)}, f32[2,6,64,128]{3,2,1,0:T(8,128)S(1)}, u32[]{:S(2)}, u32[]{:S(2)}) collective-permute-start(f32[2,6,64,128]{3,2,1,0:T(8,128)S(1)} %maximum_select_fusion.2), channel_id=1, source_target_pairs={{0,28},{4,0},{8,4},{12,8},{16,12},{20,16},{24,20},{28,24},{1,29},{... | collective-permute-start | bytes 1179656 | tf_op jit(solution)/shard_map/ppermute | solution.py:21
  42.3 1.3 pad_maximum_fusion
  45.7 2.2 %collective-permute-done.10 = f32[2,6,64,128]{3,2,1,0:T(8,128)S(1)} collective-permute-done((f32[2,6,64,128]{3,2,1,0:T(8,128)S(1)}, f32[2,6,64,128]{3,2,1,0:T(8,128)S(1)}, u32[]{:S(2)}, u32[]{:S(2)}) %collective-permute-start.10) | collective-permute-done | bytes 393248 | tf_op jit(solution)/shard_map/ppermute | solution.py:21
  47.8 3.6 %collective-permute-start.7 = (f32[2,6,64,128]{3,2,1,0:T(8,128)S(1)}, f32[2,6,64,128]{3,2,1,0:T(8,128)S(1)}, u32[]{:S(2)}, u32[]{:S(2)}) collective-permute-start(f32[2,6,64,128]{3,2,1,0:T(8,128)S(1)} %collective-permute-done.6), channel_id=1, source_target_pairs={{0,28},{4,0},{8,4},{12,8},{16,12},{20,16},{24,20},{28,24},{1,29},{... | collective-permute-start | bytes 1179656 | tf_op jit(solution)/shard_map/ppermute | solution.py:21
  51.4 1.9 %constant_dynamic-update-slice_fusion.2 = f32[8,32,4096]{2,1,0:T(8,128)} fusion(f32[8,32,4096]{2,1,0:T(8,128)} %constant_dynamic-update-slice_fusion.3, f32[32,4096]{1,0:T(8,128)} %collective-permute-done), kind=kLoop, calls=%fused_computation.31 | loop fusion | bytes 1048576
  53.4 5.8 %collective-permute-done.11 = f32[2,6,64,128]{3,2,1,0:T(8,128)S(1)} collective-permute-done((f32[2,6,64,128]{3,2,1,0:T(8,128)S(1)}, f32[2,6,64,128]{3,2,1,0:T(8,128)S(1)}, u32[]{:S(2)}, u32[]{:S(2)}) %collective-permute-start.11) | collective-permute-done | bytes 393248 | tf_op jit(solution)/shard_map/ppermute | solution.py:21
  59.3 3.3 %collective-permute-start.8 = (f32[2,6,64,128]{3,2,1,0:T(8,128)S(1)}, f32[2,6,64,128]{3,2,1,0:T(8,128)S(1)}, u32[]{:S(2)}, u32[]{:S(2)}) collective-permute-start(f32[2,6,64,128]{3,2,1,0:T(8,128)S(1)} %collective-permute-done.7), channel_id=1, source_target_pairs={{0,28},{4,0},{8,4},{12,8},{16,12},{20,16},{24,20},{28,24},{1,29},{... | collective-permute-start | bytes 1179656 | tf_op jit(solution)/shard_map/ppermute | solution.py:21
  62.6 7.7 %collective-permute-done.12 = f32[2,6,64,128]{3,2,1,0:T(8,128)S(1)} collective-permute-done((f32[2,6,64,128]{3,2,1,0:T(8,128)S(1)}, f32[2,6,64,128]{3,2,1,0:T(8,128)S(1)}, u32[]{:S(2)}, u32[]{:S(2)}) %collective-permute-start.12) | collective-permute-done | bytes 393248 | tf_op jit(solution)/shard_map/ppermute | solution.py:21
  70.5 3.3 %collective-permute-start.9 = (f32[6,64,128]{2,1,0:T(8,128)S(1)}, f32[6,64,128]{2,1,0:T(8,128)S(1)}, u32[]{:S(2)}, u32[]{:S(2)}) collective-permute-start(f32[6,64,128]{2,1,0:T(8,128)S(1)} %slice_bitcast_fusion.3), channel_id=1, source_target_pairs={{0,28},{4,0},{8,4},{12,8},{16,12},{20,16},{24,20},{28,24},{1,29},{... | collective-permute-start | bytes 589832 | tf_op jit(solution)/shard_map/ppermute | solution.py:21
  74.8 2.4 %collective-permute-done.13 = f32[6,64,128]{2,1,0:T(8,128)S(1)} collective-permute-done((f32[6,64,128]{2,1,0:T(8,128)S(1)}, f32[6,64,128]{2,1,0:T(8,128)S(1)}, u32[]{:S(2)}, u32[]{:S(2)}) %collective-permute-start.13) | collective-permute-done | bytes 196640 | tf_op jit(solution)/shard_map/ppermute | solution.py:21
  77.6 2.4 %collective-permute-start.4 = (f32[32,4096]{1,0:T(8,128)S(1)}, f32[32,4096]{1,0:T(8,128)S(1)}, u32[]{:S(2)}, u32[]{:S(2)}) collective-permute-start(f32[32,4096]{1,0:T(8,128)S(1)} %slice_bitcast_fusion), channel_id=1, source_target_pairs={{0,32},{32,64},{64,96},{96,0},{1,33},{33,65},{65,97},{97,1},{2,34}... | collective-permute-start | bytes 1572872 | tf_op jit(solution)/shard_map/ppermute | solution.py:21
  82.1 1.1 collective-permute-done.3
  84.0 9.3 %collective-permute-done.4 = f32[32,4096]{1,0:T(8,128)S(1)} collective-permute-done((f32[32,4096]{1,0:T(8,128)S(1)}, f32[32,4096]{1,0:T(8,128)S(1)}, u32[]{:S(2)}, u32[]{:S(2)}) %collective-permute-start.4) | collective-permute-done | bytes 524320 | tf_op jit(solution)/shard_map/ppermute | solution.py:21
  94.2 7.9 %reshape.692 = f32[256,64,64]{2,1,0:T(8,128)} reshape(f32[8,32,4096]{2,1,0:T(8,128)} %bitcast_dynamic-update-slice_fusion) | data formatting | bytes 8388608 | tf_op jit(solution)/shard_map/reshape | solution.py:84
  102.1 6.1 %maximum_select_fusion = f32[2,8,2,6,64,128]{5,4,3,2,1,0:T(8,128)} fusion(f32[1,8,2,6,64,128]{5,4,3,2,1,0:T(8,128)} %bitcast.44, f32[1,8,2,6,64,128]{5,4,3,2,1,0:T(8,128)S(1)} %bitcast.74, pred[]{:T(512)S(6)} %eq.39), kind=kLoop, calls=%fused_computation.6 | loop fusion | flops 4718592 | bytes 12582913 | tf_op jit(solution)/shard_map/jit(_where)/select_n | solution.py:62
  108.2 7.1 %gather_fusion.1 = f32[256,64,128]{2,1,0:T(8,128)} fusion(f32[192,64,128]{2,1,0:T(8,128)} %bitcast.73, s32[1024]{0:T(1024)S(1)} %pad_clamp_fusion), kind=kCustom, calls=%fused_computation.1 | custom fusion | bytes 16778240 | tf_op jit(solution)/shard_map/jit(_take)/gather | solution.py:83
  115.3 12.7 %fusion.2 = f32[256,64,128]{2,1,0:T(8,128)S(1)} fusion(f32[256,64,64]{2,1,0:T(8,128)} %reshape.692, f32[256,64,128]{2,1,0:T(8,128)} %gather_fusion.1, pred[256]{0:T(512)(128)(4,1)S(1)} %compare_and_fusion), kind=kOutput, calls=%fused_computation.4 | convolution fusion | flops 1612709888 | bytes 20971776 | tf_op jit(solution)/shard_map/gij,gjc->gic/dot_general | solution.py:85
  127.9 7.7 %fusion = f32[32,64,128]{2,0,1:T(8,128)S(1)} fusion(f32[256,64,128]{2,1,0:T(8,128)S(1)} %fusion.2, s32[256]{0:T(256)S(1)} %eq.35), kind=kOutput, calls=%fused_computation.2 | convolution fusion | flops 805314560 | bytes 9438208 | tf_op jit(solution)/shard_map/gm,gic->mic/dot_general | solution.py:87
  135.7 1.6 %copy.7 = f32[32,64,128]{2,1,0:T(8,128)} copy(f32[32,64,128]{2,0,1:T(8,128)S(1)} %fusion) | data formatting | bytes 2097152 | tf_op jit(solution)/shard_map/gm,gic->mic/dot_general | solution.py:87
  (62 shorter events, 13.5 us)
Async XLA Ops:
  0.0 34.1 %collective-permute-start.5 = (f32[6,64,128]{2,1,0:T(8,128)}, f32[6,64,128]{2,1,0:T(8,128)S(1)}, u32[]{:S(2)}, u32[]{:S(2)}) collective-permute-start(f32[6,64,128]{2,1,0:T(8,128)} %param.7), channel_id=1, source_target_pairs={{0,2},{2,0},{1,3},{3,1},{4,6},{6,4},{5,7},{7,5},{8,10},{10,8},{9,1... | collective-permute-start | bytes 589832 | tf_op jit(solution)/shard_map/ppermute | solution.py:16
  2.1 40.1 %collective-permute-start = (f32[32,4096]{1,0:T(8,128)}, f32[32,4096]{1,0:T(8,128)}, u32[]{:S(2)}, u32[]{:S(2)}) collective-permute-start(f32[32,4096]{1,0:T(8,128)} %bitcast.75), channel_id=1, source_target_pairs={{0,128},{128,0},{1,129},{129,1},{2,130},{130,2},{3,131},{131,3},{4... | collective-permute-start | bytes 1572872 | tf_op jit(solution)/shard_map/ppermute | solution.py:16
  35.2 12.7 %collective-permute-start.10 = (f32[2,6,64,128]{3,2,1,0:T(8,128)S(1)}, f32[2,6,64,128]{3,2,1,0:T(8,128)S(1)}, u32[]{:S(2)}, u32[]{:S(2)}) collective-permute-start(f32[2,6,64,128]{3,2,1,0:T(8,128)S(1)} %maximum_select_fusion.2), channel_id=1, source_target_pairs={{0,4},{4,8},{8,12},{12,16},{16,20},{20,24},{24,28},{28,0},{1,5},{5... | collective-permute-start | bytes 1179656 | tf_op jit(solution)/shard_map/ppermute | solution.py:21
  37.2 10.7 %collective-permute-start.6 = (f32[2,6,64,128]{3,2,1,0:T(8,128)S(1)}, f32[2,6,64,128]{3,2,1,0:T(8,128)S(1)}, u32[]{:S(2)}, u32[]{:S(2)}) collective-permute-start(f32[2,6,64,128]{3,2,1,0:T(8,128)S(1)} %maximum_select_fusion.2), channel_id=1, source_target_pairs={{0,28},{4,0},{8,4},{12,8},{16,12},{20,16},{24,20},{28,24},{1,29},{... | collective-permute-start | bytes 1179656 | tf_op jit(solution)/shard_map/ppermute | solution.py:21
  43.6 30.2 %collective-permute-start.2 = (f32[2,32,4096]{2,1,0:T(8,128)S(1)}, f32[2,32,4096]{2,1,0:T(8,128)S(1)}, u32[]{:S(2)}, u32[]{:S(2)}) collective-permute-start(f32[2,32,4096]{2,1,0:T(8,128)S(1)} %pad_maximum_fusion), channel_id=1, source_target_pairs={{0,96},{32,0},{64,32},{96,64},{1,97},{33,1},{65,33},{97,65},{2,98}... | collective-permute-start | bytes 3145736 | tf_op jit(solution)/shard_map/ppermute | solution.py:21
  44.5 33.0 %collective-permute-start.1 = (f32[2,32,4096]{2,1,0:T(8,128)S(1)}, f32[2,32,4096]{2,1,0:T(8,128)S(1)}, u32[]{:S(2)}, u32[]{:S(2)}) collective-permute-start(f32[2,32,4096]{2,1,0:T(8,128)S(1)} %pad_maximum_fusion), channel_id=1, source_target_pairs={{0,32},{32,64},{64,96},{96,0},{1,33},{33,65},{65,97},{97,1},{2,34}... | collective-permute-start | bytes 3145736 | tf_op jit(solution)/shard_map/ppermute | solution.py:21
  47.8 11.4 %collective-permute-start.11 = (f32[2,6,64,128]{3,2,1,0:T(8,128)S(1)}, f32[2,6,64,128]{3,2,1,0:T(8,128)S(1)}, u32[]{:S(2)}, u32[]{:S(2)}) collective-permute-start(f32[2,6,64,128]{3,2,1,0:T(8,128)S(1)} %collective-permute-done.10), channel_id=1, source_target_pairs={{0,4},{4,8},{8,12},{12,16},{16,20},{20,24},{24,28},{28,0},{1,5},{5... | collective-permute-start | bytes 1179656 | tf_op jit(solution)/shard_map/ppermute | solution.py:21
  47.8 11.4 %collective-permute-start.7 = (f32[2,6,64,128]{3,2,1,0:T(8,128)S(1)}, f32[2,6,64,128]{3,2,1,0:T(8,128)S(1)}, u32[]{:S(2)}, u32[]{:S(2)}) collective-permute-start(f32[2,6,64,128]{3,2,1,0:T(8,128)S(1)} %collective-permute-done.6), channel_id=1, source_target_pairs={{0,28},{4,0},{8,4},{12,8},{16,12},{20,16},{24,20},{28,24},{1,29},{... | collective-permute-start | bytes 1179656 | tf_op jit(solution)/shard_map/ppermute | solution.py:21
  59.2 11.1 %collective-permute-start.12 = (f32[2,6,64,128]{3,2,1,0:T(8,128)S(1)}, f32[2,6,64,128]{3,2,1,0:T(8,128)S(1)}, u32[]{:S(2)}, u32[]{:S(2)}) collective-permute-start(f32[2,6,64,128]{3,2,1,0:T(8,128)S(1)} %collective-permute-done.11), channel_id=1, source_target_pairs={{0,4},{4,8},{8,12},{12,16},{16,20},{20,24},{24,28},{28,0},{1,5},{5... | collective-permute-start | bytes 1179656 | tf_op jit(solution)/shard_map/ppermute | solution.py:21
  59.3 11.2 %collective-permute-start.8 = (f32[2,6,64,128]{3,2,1,0:T(8,128)S(1)}, f32[2,6,64,128]{3,2,1,0:T(8,128)S(1)}, u32[]{:S(2)}, u32[]{:S(2)}) collective-permute-start(f32[2,6,64,128]{3,2,1,0:T(8,128)S(1)} %collective-permute-done.7), channel_id=1, source_target_pairs={{0,28},{4,0},{8,4},{12,8},{16,12},{20,16},{24,20},{28,24},{1,29},{... | collective-permute-start | bytes 1179656 | tf_op jit(solution)/shard_map/ppermute | solution.py:21
  70.3 7.0 %collective-permute-start.13 = (f32[6,64,128]{2,1,0:T(8,128)S(1)}, f32[6,64,128]{2,1,0:T(8,128)S(1)}, u32[]{:S(2)}, u32[]{:S(2)}) collective-permute-start(f32[6,64,128]{2,1,0:T(8,128)S(1)} %slice_bitcast_fusion.2), channel_id=1, source_target_pairs={{0,4},{4,8},{8,12},{12,16},{16,20},{20,24},{24,28},{28,0},{1,5},{5... | collective-permute-start | bytes 589832 | tf_op jit(solution)/shard_map/ppermute | solution.py:21
  70.5 6.8 %collective-permute-start.9 = (f32[6,64,128]{2,1,0:T(8,128)S(1)}, f32[6,64,128]{2,1,0:T(8,128)S(1)}, u32[]{:S(2)}, u32[]{:S(2)}) collective-permute-start(f32[6,64,128]{2,1,0:T(8,128)S(1)} %slice_bitcast_fusion.3), channel_id=1, source_target_pairs={{0,28},{4,0},{8,4},{12,8},{16,12},{20,16},{24,20},{28,24},{1,29},{... | collective-permute-start | bytes 589832 | tf_op jit(solution)/shard_map/ppermute | solution.py:21
  73.8 9.4 %collective-permute-start.3 = (f32[32,4096]{1,0:T(8,128)S(1)}, f32[32,4096]{1,0:T(8,128)S(1)}, u32[]{:S(2)}, u32[]{:S(2)}) collective-permute-start(f32[32,4096]{1,0:T(8,128)S(1)} %slice_bitcast_fusion.1), channel_id=1, source_target_pairs={{0,96},{32,0},{64,32},{96,64},{1,97},{33,1},{65,33},{97,65},{2,98}... | collective-permute-start | bytes 1572872 | tf_op jit(solution)/shard_map/ppermute | solution.py:21
  77.4 24.7 %collective-permute-start.14 = (f32[8,2,6,64,128]{4,3,2,1,0:T(8,128)S(1)}, f32[8,2,6,64,128]{4,3,2,1,0:T(8,128)}, u32[]{:S(2)}, u32[]{:S(2)}) collective-permute-start(f32[8,2,6,64,128]{4,3,2,1,0:T(8,128)S(1)} %bitcast_dynamic-update-slice_fusion.2), channel_id=1, source_target_pairs={{0,1},{1,0},{2,3},{3,2},{4,5},{5,4},{6,7},{7,6},{8,9},{9,8},{10,11... | collective-permute-start | bytes 9437192 | tf_op jit(solution)/shard_map/ppermute | solution.py:16
  77.6 15.8 %collective-permute-start.4 = (f32[32,4096]{1,0:T(8,128)S(1)}, f32[32,4096]{1,0:T(8,128)S(1)}, u32[]{:S(2)}, u32[]{:S(2)}) collective-permute-start(f32[32,4096]{1,0:T(8,128)S(1)} %slice_bitcast_fusion), channel_id=1, source_target_pairs={{0,32},{32,64},{64,96},{96,0},{1,33},{33,65},{65,97},{97,1},{2,34}... | collective-permute-start | bytes 1572872 | tf_op jit(solution)/shard_map/ppermute | solution.py:21
where the time goes:
time: 140 us; the launch traced here: 137 us
  waiting for transfers between devices  28.7 us (20%)
  local copies, waits for them, and re-layouts  26.8 us (19%)
  starting transfers between devices  25.4 us (18%)
  blocking collectives  24.6 us (18%)
  matrix products  20.4 us (15%)
  other arithmetic  11.1 us (8%)
    ppermute x12, waiting for transfers between devices, shift(): lax.ppermute(block, axis, [(i, (i + distance) % n) for i in range(n)])  28.7 us
    all_gather x1, blocking collectives, shards(): all_ints = lax.all_gather(ints, ROW, axis=0, tiled=False)  24.6 us
    ppermute x12, starting transfers between devices, shift(): lax.ppermute(block, axis, [(i, (i + distance) % n) for i in range(n)])  21.8 us
    dot_general x1, matrix products, shards(): terms = jnp.einsum('gij,gjc->gic', left, chosen, precision=highest)  12.7 us
    reshape x1, local copies, waits for them, and re-layouts, shards(): left = a_all.reshape(-1, BLK, BLK)  7.87 us
    dot_general x1, matrix products, shards(): out = jnp.einsum('gm,gic->mic', place, terms, precision=highest)  7.73 us
    gather x1, local copies, waits for them, and re-layouts, shards(): chosen = jnp.take(table, index.reshape(-1), axis=0)  7.09 us
    unnamed x10, local copies, waits for them, and re-layouts  6.95 us
  transfers between devices with their start and end apart: 15, of which 6 were waited for; matrix products, arithmetic and copies ran while one was open for 17% of the time, Pallas kernels for 0%

commit v1 on v0

--- a/solution.py
+++ b/solution.py
@@ -40,10 +40,7 @@
 
 def gather_b(b_own):
     n_z = lax.axis_size("z")
-    xh = lax.axis_index("xh")
-    core = lax.axis_index("core")
-    b_h = swap(b_own, "xh")
-    pair = jnp.where(xh == 0, jnp.stack([b_own, b_h]), jnp.stack([b_h, b_own]))
+    pair = jnp.stack([b_own, swap(b_own, "xh")])
     by_offset = [None] * n_z
     by_offset[0] = pair
     up = pair
@@ -58,8 +55,7 @@
     far_down = shift(down[1], "z", 1)
     by_offset[half] = jnp.stack([far_up, far_down])
     mine = jnp.stack(by_offset)
-    other = swap(mine, "core")
-    return jnp.where(core == 0, jnp.stack([mine, other]), jnp.stack([other, mine]))
+    return jnp.stack([mine, swap(mine, "core")])
 
 
 def shards(a_blocks, a_rows, a_slots, b_stripes):
@@ -69,20 +65,20 @@
     highest = lax.Precision.HIGHEST
 
     ints = jnp.stack([a_rows[0, 0], a_slots[0, 0]])
-    all_ints = lax.all_gather(ints, ROW, axis=0, tiled=False)
-
+    ints_k, _ = gather_a(ints)
     a_all, pid = gather_a(a_blocks[0, 0])
     table = gather_b(b_stripes)
     table = table.reshape(-1, BLK, columns)
 
-    ints_k = jnp.take(all_ints, pid, axis=0)
     rows = ints_k[:, 0]
     slots = ints_k[:, 1]
     d = (pid[:, None] - z) % n_z
-    index = (((slots // 6) % 2 * n_z + d) * 2 + slots // 12) * 6 + slots % 6
+    core_rel = (slots // 6) % 2 ^ lax.axis_index("core")
+    xh_rel = (slots // 12) ^ lax.axis_index("xh")
+    index = ((core_rel * n_z + d) * 2 + xh_rel) * 6 + slots % 6
     chosen = jnp.take(table, index.reshape(-1), axis=0)
     left = a_all.reshape(-1, BLK, BLK)
-    terms = jnp.einsum("gij,gjc->gic", left, chosen, precision=highest)
+    terms = jnp.einsum("gij,gjc->gic", left, chosen, precision=lax.Precision.HIGH)
     place = (rows.reshape(-1)[:, None] == jnp.arange(MB, dtype=jnp.int32)[None, :]).astype(jnp.float32)
     out = jnp.einsum("gm,gic->mic", place, terms, precision=highest)
     return out.reshape(MB * BLK, columns)

time: 140 us -> 133 us (0.950); the launches traced: 137 us -> 132 us
  blocking collectives: 24.6 us -> 0 us
  waiting for transfers between devices: 28.7 us -> 40 us
  starting transfers between devices: 25.4 us -> 31 us
  matrix products: 20.4 us -> 24 us
    all_gather x1 -> x0, blocking collectives: 24.6 us -> none  [shards(): all_ints = lax.all_gather(ints, ROW, axis=0, tiled=False)]
    ppermute x12 -> x16, waiting for transfers between devices: 28.7 us -> 40 us  [shift(): lax.ppermute(block, axis, [(i, (i + distance) % n) for i in range(n)])]
    select_n x4 -> x0, other arithmetic: 7.23 us -> none  [the longest x1 6.09 us: gather_b(): jnp.where(core == 0, jnp.stack([mine, other]), jnp.stack([other, mine]))]
    another operation x0 -> x3, other arithmetic: none -> 7.01 us  [the longest x1 5.38 us: gather_b(): return jnp.stack([mine, swap(mine, 'core')])]
    ppermute x12 -> x16, starting transfers between devices: 21.8 us -> 26.2 us  [shift(): lax.ppermute(block, axis, [(i, (i + distance) % n) for i in range(n)])]
    dot_general x1, matrix products: 7.73 us -> 10.6 us  [shards(): out = jnp.einsum('gm,gic->mic', place, terms, precision=highest)]
    ppermute x3 -> x4, starting transfers between devices: 3.65 us -> 4.85 us  [swap(): return lax.ppermute(block, axis, [(0, 1), (1, 0)])]
    unnamed x10 -> x14, local copies, waits for them, and re-layouts: 6.95 us -> 6.88 us
  transfers between devices with their start and end apart: 15 -> 20, of which waited for: 6 -> 12; matrix products, arithmetic and copies ran while one was open for 17% -> 17% of each run, Pallas kernels for 0% -> 0%
where the time goes in v1:
time: 133 us; the launch traced here: 132 us
  waiting for transfers between devices  40 us (30%)
  starting transfers between devices  31 us (23%)
  local copies, waits for them, and re-layouts  26.1 us (20%)
  matrix products  24 us (18%)
  other arithmetic  10.8 us (8%)
    ppermute x16, waiting for transfers between devices, shift(): lax.ppermute(block, axis, [(i, (i + distance) % n) for i in range(n)])  40 us
    ppermute x16, starting transfers between devices, shift(): lax.ppermute(block, axis, [(i, (i + distance) % n) for i in range(n)])  26.2 us
    dot_general x1, matrix products, shards(): jnp.einsum('gij,gjc->gic', left, chosen, precision=lax.Precision.HIGH)  13.3 us
    dot_general x1, matrix products, shards(): out = jnp.einsum('gm,gic->mic', place, terms, precision=highest)  10.6 us
    reshape x1, local copies, waits for them, and re-layouts, shards(): left = a_all.reshape(-1, BLK, BLK)  7.88 us
    gather x1, local copies, waits for them, and re-layouts, shards(): chosen = jnp.take(table, index.reshape(-1), axis=0)  7.09 us
    unnamed x14, local copies, waits for them, and re-layouts  6.88 us
    another operation x1, other arithmetic, gather_b(): return jnp.stack([mine, swap(mine, 'core')])  5.38 us
  transfers between devices with their start and end apart: 20, of which 12 were waited for; matrix products, arithmetic and copies ran while one was open for 17% of the time, Pallas kernels for 0%

profile of v1, /device:TPU:2, one launch (start us, length us, event | category | flops | bytes accessed | tf_op | source)
XLA Modules:
  0.0 132.1 jit_solution(9794807375036454107)
XLA Ops:
  0.7 2.2 %collective-permute-start = (s32[2,32]{1,0:T(2,128)S(1)}, s32[2,32]{1,0:T(2,128)S(1)}, u32[]{:S(2)}, u32[]{:S(2)}) collective-permute-start(s32[2,32]{1,0:T(2,128)S(1)} %get-tuple-element.19), channel_id=1, source_target_pairs={{0,128},{128,0},{1,129},{129,1},{2,130},{130,2},{3,131},{131,3},{4... | collective-permute-start | bytes 776 | tf_op jit(solution)/shard_map/ppermute | solution.py:16
  3.6 1.8 %collective-permute-start.5 = (f32[32,4096]{1,0:T(8,128)}, f32[32,4096]{1,0:T(8,128)}, u32[]{:S(2)}, u32[]{:S(2)}) collective-permute-start(f32[32,4096]{1,0:T(8,128)} %bitcast.76), channel_id=1, source_target_pairs={{0,128},{128,0},{1,129},{129,1},{2,130},{130,2},{3,131},{131,3},{4... | collective-permute-start | bytes 1572872 | tf_op jit(solution)/shard_map/ppermute | solution.py:16
  6.1 1.9 %constant_dynamic-update-slice_fusion.9 = f32[8,32,4096]{2,1,0:T(8,128)} fusion(f32[1,1,32,4096]{3,2,1,0:T(8,128)} %param.4), kind=kLoop, calls=%fused_computation.34 | loop fusion | bytes 1048576
  8.4 3.1 %collective-permute-start.2 = (s32[2,2,32]{2,1,0:T(2,128)S(1)}, s32[2,2,32]{2,1,0:T(2,128)S(1)}, u32[]{:S(2)}, u32[]{:S(2)}) collective-permute-start(s32[2,2,32]{2,1,0:T(2,128)S(1)} %pad_add_fusion), channel_id=1, source_target_pairs={{0,96},{32,0},{64,32},{96,64},{1,97},{33,1},{65,33},{97,65},{2,98}... | collective-permute-start | bytes 1544 | tf_op jit(solution)/shard_map/ppermute | solution.py:21
  12.8 3.5 %collective-permute-start.3 = (s32[2,32]{1,0:T(2,128)S(1)}, s32[2,32]{1,0:T(2,128)S(1)}, u32[]{:S(2)}, u32[]{:S(2)}) collective-permute-start(s32[2,32]{1,0:T(2,128)S(1)} %slice_bitcast_fusion.5), channel_id=1, source_target_pairs={{0,96},{32,0},{64,32},{96,64},{1,97},{33,1},{65,33},{97,65},{2,98}... | collective-permute-start | bytes 776 | tf_op jit(solution)/shard_map/ppermute | solution.py:21
  17.6 3.5 %collective-permute-done.4 = s32[2,32]{1,0:T(2,128)S(1)} collective-permute-done((s32[2,32]{1,0:T(2,128)S(1)}, s32[2,32]{1,0:T(2,128)S(1)}, u32[]{:S(2)}, u32[]{:S(2)}) %collective-permute-start.4) | collective-permute-done | bytes 288 | tf_op jit(solution)/shard_map/ppermute | solution.py:21
  24.3 5.9 %collective-permute-start.11 = (f32[2,6,64,128]{3,2,1,0:T(8,128)S(1)}, f32[2,6,64,128]{3,2,1,0:T(8,128)S(1)}, u32[]{:S(2)}, u32[]{:S(2)}) collective-permute-start(f32[2,6,64,128]{3,2,1,0:T(8,128)S(1)} %pad_maximum_fusion.2), channel_id=1, source_target_pairs={{0,28},{4,0},{8,4},{12,8},{16,12},{20,16},{24,20},{28,24},{1,29},{... | collective-permute-start | bytes 1179656 | tf_op jit(solution)/shard_map/ppermute | solution.py:21
  32.5 2.0 %collective-permute-start.6 = (f32[2,32,4096]{2,1,0:T(8,128)S(1)}, f32[2,32,4096]{2,1,0:T(8,128)S(1)}, u32[]{:S(2)}, u32[]{:S(2)}) collective-permute-start(f32[2,32,4096]{2,1,0:T(8,128)S(1)} %pad_maximum_fusion.1), channel_id=1, source_target_pairs={{0,32},{32,64},{64,96},{96,0},{1,33},{33,65},{65,97},{97,1},{2,34}... | collective-permute-start | bytes 3145736 | tf_op jit(solution)/shard_map/ppermute | solution.py:21
  34.6 1.9 %collective-permute-done.11 = f32[2,6,64,128]{3,2,1,0:T(8,128)S(1)} collective-permute-done((f32[2,6,64,128]{3,2,1,0:T(8,128)S(1)}, f32[2,6,64,128]{3,2,1,0:T(8,128)S(1)}, u32[]{:S(2)}, u32[]{:S(2)}) %collective-permute-start.11) | collective-permute-done | bytes 393248 | tf_op jit(solution)/shard_map/ppermute | solution.py:21
  36.4 3.7 %collective-permute-start.12 = (f32[2,6,64,128]{3,2,1,0:T(8,128)S(1)}, f32[2,6,64,128]{3,2,1,0:T(8,128)S(1)}, u32[]{:S(2)}, u32[]{:S(2)}) collective-permute-start(f32[2,6,64,128]{3,2,1,0:T(8,128)S(1)} %collective-permute-done.11), channel_id=1, source_target_pairs={{0,28},{4,0},{8,4},{12,8},{16,12},{20,16},{24,20},{28,24},{1,29},{... | collective-permute-start | bytes 1179656 | tf_op jit(solution)/shard_map/ppermute | solution.py:21
  40.4 1.9 %constant_dynamic-update-slice_fusion.8 = f32[8,32,4096]{2,1,0:T(8,128)} fusion(f32[8,32,4096]{2,1,0:T(8,128)} %constant_dynamic-update-slice_fusion.9, f32[32,4096]{1,0:T(8,128)} %collective-permute-done.5), kind=kLoop, calls=%fused_computation.33 | loop fusion | bytes 1048576
  42.3 4.9 %collective-permute-done.12 = f32[2,6,64,128]{3,2,1,0:T(8,128)S(1)} collective-permute-done((f32[2,6,64,128]{3,2,1,0:T(8,128)S(1)}, f32[2,6,64,128]{3,2,1,0:T(8,128)S(1)}, u32[]{:S(2)}, u32[]{:S(2)}) %collective-permute-start.12) | collective-permute-done | bytes 393248 | tf_op jit(solution)/shard_map/ppermute | solution.py:21
  47.2 3.7 %collective-permute-start.13 = (f32[2,6,64,128]{3,2,1,0:T(8,128)S(1)}, f32[2,6,64,128]{3,2,1,0:T(8,128)S(1)}, u32[]{:S(2)}, u32[]{:S(2)}) collective-permute-start(f32[2,6,64,128]{3,2,1,0:T(8,128)S(1)} %collective-permute-done.12), channel_id=1, source_target_pairs={{0,28},{4,0},{8,4},{12,8},{16,12},{20,16},{24,20},{28,24},{1,29},{... | collective-permute-start | bytes 1179656 | tf_op jit(solution)/shard_map/ppermute | solution.py:21
  51.5 6.8 %collective-permute-done.13 = f32[2,6,64,128]{3,2,1,0:T(8,128)S(1)} collective-permute-done((f32[2,6,64,128]{3,2,1,0:T(8,128)S(1)}, f32[2,6,64,128]{3,2,1,0:T(8,128)S(1)}, u32[]{:S(2)}, u32[]{:S(2)}) %collective-permute-start.13) | collective-permute-done | bytes 393248 | tf_op jit(solution)/shard_map/ppermute | solution.py:21
  58.3 3.9 %collective-permute-start.14 = (f32[6,64,128]{2,1,0:T(8,128)S(1)}, f32[6,64,128]{2,1,0:T(8,128)S(1)}, u32[]{:S(2)}, u32[]{:S(2)}) collective-permute-start(f32[6,64,128]{2,1,0:T(8,128)S(1)} %slice_bitcast_fusion.3), channel_id=1, source_target_pairs={{0,28},{4,0},{8,4},{12,8},{16,12},{20,16},{24,20},{28,24},{1,29},{... | collective-permute-start | bytes 589832 | tf_op jit(solution)/shard_map/ppermute | solution.py:21
  62.8 2.6 %collective-permute-done.14 = f32[6,64,128]{2,1,0:T(8,128)S(1)} collective-permute-done((f32[6,64,128]{2,1,0:T(8,128)S(1)}, f32[6,64,128]{2,1,0:T(8,128)S(1)}, u32[]{:S(2)}, u32[]{:S(2)}) %collective-permute-start.14) | collective-permute-done | bytes 196640 | tf_op jit(solution)/shard_map/ppermute | solution.py:21
  65.4 4.1 %collective-permute-done.18 = f32[6,64,128]{2,1,0:T(8,128)S(1)} collective-permute-done((f32[6,64,128]{2,1,0:T(8,128)S(1)}, f32[6,64,128]{2,1,0:T(8,128)S(1)}, u32[]{:S(2)}, u32[]{:S(2)}) %collective-permute-start.18) | collective-permute-done | bytes 196640 | tf_op jit(solution)/shard_map/ppermute | solution.py:21
  72.8 12.6 %collective-permute-done.9 = f32[32,4096]{1,0:T(8,128)S(1)} collective-permute-done((f32[32,4096]{1,0:T(8,128)S(1)}, f32[32,4096]{1,0:T(8,128)S(1)}, u32[]{:S(2)}, u32[]{:S(2)}) %collective-permute-start.9) | collective-permute-done | bytes 524320 | tf_op jit(solution)/shard_map/ppermute | solution.py:21
  86.2 7.9 %reshape.288 = f32[256,64,64]{2,1,0:T(8,128)} reshape(f32[8,32,4096]{2,1,0:T(8,128)} %bitcast_dynamic-update-slice_fusion) | data formatting | bytes 8388608 | tf_op jit(solution)/shard_map/reshape | solution.py:80
  94.1 5.4 %pad_maximum_fusion = f32[2,8,2,6,64,128]{5,4,3,2,1,0:T(8,128)} fusion(f32[1,8,2,6,64,128]{5,4,3,2,1,0:T(8,128)} %bitcast.39, f32[1,8,2,6,64,128]{5,4,3,2,1,0:T(8,128)S(1)} %bitcast.75), kind=kLoop, calls=%fused_computation.5 | loop fusion | flops 1572864 | bytes 12582912 | tf_op jit(solution)/shard_map/stack | solution.py:58
  99.5 7.1 %gather_fusion = f32[256,64,128]{2,1,0:T(8,128)} fusion(f32[192,64,128]{2,1,0:T(8,128)} %bitcast.74, s32[1024]{0:T(1024)S(1)} %pad_clamp_fusion), kind=kCustom, calls=%fused_computation | custom fusion | bytes 16778240 | tf_op jit(solution)/shard_map/jit(_take)/gather | solution.py:79
  106.6 13.3 %fusion.2 = f32[256,64,128]{2,1,0:T(8,128)} fusion(f32[256,64,64]{2,1,0:T(8,128)} %reshape.288, f32[256,64,128]{2,1,0:T(8,128)} %gather_fusion, pred[256]{0:T(512)(128)(4,1)S(1)} %compare_and_fusion), kind=kOutput, calls=%fused_computation.3 | convolution fusion | flops 807403520 | bytes 20971776 | tf_op jit(solution)/shard_map/gij,gjc->gic/dot_general | solution.py:81
  119.9 10.6 %fusion = f32[32,64,128]{2,0,1:T(8,128)S(1)} fusion(f32[256,64,128]{2,1,0:T(8,128)} %fusion.2, s32[256]{0:T(256)S(1)} %eq.29), kind=kOutput, calls=%fused_computation.1 | convolution fusion | flops 805314560 | bytes 9438208 | tf_op jit(solution)/shard_map/gm,gic->mic/dot_general | solution.py:83
  130.6 1.6 %copy.5 = f32[32,64,128]{2,1,0:T(8,128)} copy(f32[32,64,128]{2,0,1:T(8,128)S(1)} %fusion) | data formatting | bytes 2097152 | tf_op jit(solution)/shard_map/gm,gic->mic/dot_general | solution.py:83
  (74 shorter events, 16.0 us)
Async XLA Ops:
  0.7 7.7 %collective-permute-start = (s32[2,32]{1,0:T(2,128)S(1)}, s32[2,32]{1,0:T(2,128)S(1)}, u32[]{:S(2)}, u32[]{:S(2)}) collective-permute-start(s32[2,32]{1,0:T(2,128)S(1)} %get-tuple-element.19), channel_id=1, source_target_pairs={{0,128},{128,0},{1,129},{129,1},{2,130},{130,2},{3,131},{131,3},{4... | collective-permute-start | bytes 776 | tf_op jit(solution)/shard_map/ppermute | solution.py:16
  2.9 20.4 %collective-permute-start.10 = (f32[6,64,128]{2,1,0:T(8,128)}, f32[6,64,128]{2,1,0:T(8,128)S(1)}, u32[]{:S(2)}, u32[]{:S(2)}) collective-permute-start(f32[6,64,128]{2,1,0:T(8,128)} %param.7), channel_id=1, source_target_pairs={{0,2},{2,0},{1,3},{3,1},{4,6},{6,4},{5,7},{7,5},{8,10},{10,8},{9,1... | collective-permute-start | bytes 589832 | tf_op jit(solution)/shard_map/ppermute | solution.py:16
  3.6 27.5 %collective-permute-start.5 = (f32[32,4096]{1,0:T(8,128)}, f32[32,4096]{1,0:T(8,128)}, u32[]{:S(2)}, u32[]{:S(2)}) collective-permute-start(f32[32,4096]{1,0:T(8,128)} %bitcast.76), channel_id=1, source_target_pairs={{0,128},{128,0},{1,129},{129,1},{2,130},{130,2},{3,131},{131,3},{4... | collective-permute-start | bytes 1572872 | tf_op jit(solution)/shard_map/ppermute | solution.py:16
  8.4 4.4 %collective-permute-start.2 = (s32[2,2,32]{2,1,0:T(2,128)S(1)}, s32[2,2,32]{2,1,0:T(2,128)S(1)}, u32[]{:S(2)}, u32[]{:S(2)}) collective-permute-start(s32[2,2,32]{2,1,0:T(2,128)S(1)} %pad_add_fusion), channel_id=1, source_target_pairs={{0,96},{32,0},{64,32},{96,64},{1,97},{33,1},{65,33},{97,65},{2,98}... | collective-permute-start | bytes 1544 | tf_op jit(solution)/shard_map/ppermute | solution.py:21
  11.5 4.8 %collective-permute-start.1 = (s32[2,2,32]{2,1,0:T(2,128)S(1)}, s32[2,2,32]{2,1,0:T(2,128)S(1)}, u32[]{:S(2)}, u32[]{:S(2)}) collective-permute-start(s32[2,2,32]{2,1,0:T(2,128)S(1)} %pad_add_fusion), channel_id=1, source_target_pairs={{0,32},{32,64},{64,96},{96,0},{1,33},{33,65},{65,97},{97,1},{2,34}... | collective-permute-start | bytes 1544 | tf_op jit(solution)/shard_map/ppermute | solution.py:21
  12.8 4.8 %collective-permute-start.3 = (s32[2,32]{1,0:T(2,128)S(1)}, s32[2,32]{1,0:T(2,128)S(1)}, u32[]{:S(2)}, u32[]{:S(2)}) collective-permute-start(s32[2,32]{1,0:T(2,128)S(1)} %slice_bitcast_fusion.5), channel_id=1, source_target_pairs={{0,96},{32,0},{64,32},{96,64},{1,97},{33,1},{65,33},{97,65},{2,98}... | collective-permute-start | bytes 776 | tf_op jit(solution)/shard_map/ppermute | solution.py:21
  16.3 4.8 %collective-permute-start.4 = (s32[2,32]{1,0:T(2,128)S(1)}, s32[2,32]{1,0:T(2,128)S(1)}, u32[]{:S(2)}, u32[]{:S(2)}) collective-permute-start(s32[2,32]{1,0:T(2,128)S(1)} %slice_bitcast_fusion.4), channel_id=1, source_target_pairs={{0,32},{32,64},{64,96},{96,0},{1,33},{33,65},{65,97},{97,1},{2,34}... | collective-permute-start | bytes 776 | tf_op jit(solution)/shard_map/ppermute | solution.py:21
  24.3 12.2 %collective-permute-start.11 = (f32[2,6,64,128]{3,2,1,0:T(8,128)S(1)}, f32[2,6,64,128]{3,2,1,0:T(8,128)S(1)}, u32[]{:S(2)}, u32[]{:S(2)}) collective-permute-start(f32[2,6,64,128]{3,2,1,0:T(8,128)S(1)} %pad_maximum_fusion.2), channel_id=1, source_target_pairs={{0,28},{4,0},{8,4},{12,8},{16,12},{20,16},{24,20},{28,24},{1,29},{... | collective-permute-start | bytes 1179656 | tf_op jit(solution)/shard_map/ppermute | solution.py:21
  30.2 10.2 %collective-permute-start.15 = (f32[2,6,64,128]{3,2,1,0:T(8,128)S(1)}, f32[2,6,64,128]{3,2,1,0:T(8,128)S(1)}, u32[]{:S(2)}, u32[]{:S(2)}) collective-permute-start(f32[2,6,64,128]{3,2,1,0:T(8,128)S(1)} %pad_maximum_fusion.2), channel_id=1, source_target_pairs={{0,4},{4,8},{8,12},{12,16},{16,20},{20,24},{24,28},{28,0},{1,5},{5... | collective-permute-start | bytes 1179656 | tf_op jit(solution)/shard_map/ppermute | solution.py:21
  32.5 30.2 %collective-permute-start.7 = (f32[2,32,4096]{2,1,0:T(8,128)S(1)}, f32[2,32,4096]{2,1,0:T(8,128)S(1)}, u32[]{:S(2)}, u32[]{:S(2)}) collective-permute-start(f32[2,32,4096]{2,1,0:T(8,128)S(1)} %pad_maximum_fusion.1), channel_id=1, source_target_pairs={{0,96},{32,0},{64,32},{96,64},{1,97},{33,1},{65,33},{97,65},{2,98}... | collective-permute-start | bytes 3145736 | tf_op jit(solution)/shard_map/ppermute | solution.py:21
  32.5 37.2 %collective-permute-start.6 = (f32[2,32,4096]{2,1,0:T(8,128)S(1)}, f32[2,32,4096]{2,1,0:T(8,128)S(1)}, u32[]{:S(2)}, u32[]{:S(2)}) collective-permute-start(f32[2,32,4096]{2,1,0:T(8,128)S(1)} %pad_maximum_fusion.1), channel_id=1, source_target_pairs={{0,32},{32,64},{64,96},{96,0},{1,33},{33,65},{65,97},{97,1},{2,34}... | collective-permute-start | bytes 3145736 | tf_op jit(solution)/shard_map/ppermute | solution.py:21
  36.4 10.8 %collective-permute-start.12 = (f32[2,6,64,128]{3,2,1,0:T(8,128)S(1)}, f32[2,6,64,128]{3,2,1,0:T(8,128)S(1)}, u32[]{:S(2)}, u32[]{:S(2)}) collective-permute-start(f32[2,6,64,128]{3,2,1,0:T(8,128)S(1)} %collective-permute-done.11), channel_id=1, source_target_pairs={{0,28},{4,0},{8,4},{12,8},{16,12},{20,16},{24,20},{28,24},{1,29},{... | collective-permute-start | bytes 1179656 | tf_op jit(solution)/shard_map/ppermute | solution.py:21
  40.4 11.0 %collective-permute-start.16 = (f32[2,6,64,128]{3,2,1,0:T(8,128)S(1)}, f32[2,6,64,128]{3,2,1,0:T(8,128)S(1)}, u32[]{:S(2)}, u32[]{:S(2)}) collective-permute-start(f32[2,6,64,128]{3,2,1,0:T(8,128)S(1)} %collective-permute-done.15), channel_id=1, source_target_pairs={{0,4},{4,8},{8,12},{12,16},{16,20},{20,24},{24,28},{28,0},{1,5},{5... | collective-permute-start | bytes 1179656 | tf_op jit(solution)/shard_map/ppermute | solution.py:21
  47.2 11.1 %collective-permute-start.13 = (f32[2,6,64,128]{3,2,1,0:T(8,128)S(1)}, f32[2,6,64,128]{3,2,1,0:T(8,128)S(1)}, u32[]{:S(2)}, u32[]{:S(2)}) collective-permute-start(f32[2,6,64,128]{3,2,1,0:T(8,128)S(1)} %collective-permute-done.12), channel_id=1, source_target_pairs={{0,28},{4,0},{8,4},{12,8},{16,12},{20,16},{24,20},{28,24},{1,29},{... | collective-permute-start | bytes 1179656 | tf_op jit(solution)/shard_map/ppermute | solution.py:21
  51.4 11.1 %collective-permute-start.17 = (f32[2,6,64,128]{3,2,1,0:T(8,128)S(1)}, f32[2,6,64,128]{3,2,1,0:T(8,128)S(1)}, u32[]{:S(2)}, u32[]{:S(2)}) collective-permute-start(f32[2,6,64,128]{3,2,1,0:T(8,128)S(1)} %collective-permute-done.16), channel_id=1, source_target_pairs={{0,4},{4,8},{8,12},{12,16},{16,20},{20,24},{24,28},{28,0},{1,5},{5... | collective-permute-start | bytes 1179656 | tf_op jit(solution)/shard_map/ppermute | solution.py:21
  58.3 7.1 %collective-permute-start.14 = (f32[6,64,128]{2,1,0:T(8,128)S(1)}, f32[6,64,128]{2,1,0:T(8,128)S(1)}, u32[]{:S(2)}, u32[]{:S(2)}) collective-permute-start(f32[6,64,128]{2,1,0:T(8,128)S(1)} %slice_bitcast_fusion.3), channel_id=1, source_target_pairs={{0,28},{4,0},{8,4},{12,8},{16,12},{20,16},{24,20},{28,24},{1,29},{... | collective-permute-start | bytes 589832 | tf_op jit(solution)/shard_map/ppermute | solution.py:21
  62.5 7.0 %collective-permute-start.18 = (f32[6,64,128]{2,1,0:T(8,128)S(1)}, f32[6,64,128]{2,1,0:T(8,128)S(1)}, u32[]{:S(2)}, u32[]{:S(2)}) collective-permute-start(f32[6,64,128]{2,1,0:T(8,128)S(1)} %slice_bitcast_fusion.2), channel_id=1, source_target_pairs={{0,4},{4,8},{8,12},{12,16},{16,20},{20,24},{24,28},{28,0},{1,5},{5... | collective-permute-start | bytes 589832 | tf_op jit(solution)/shard_map/ppermute | solution.py:21
  62.7 9.3 %collective-permute-start.8 = (f32[32,4096]{1,0:T(8,128)S(1)}, f32[32,4096]{1,0:T(8,128)S(1)}, u32[]{:S(2)}, u32[]{:S(2)}) collective-permute-start(f32[32,4096]{1,0:T(8,128)S(1)} %slice_bitcast_fusion.1), channel_id=1, source_target_pairs={{0,96},{32,0},{64,32},{96,64},{1,97},{33,1},{65,33},{97,65},{2,98}... | collective-permute-start | bytes 1572872 | tf_op jit(solution)/shard_map/ppermute | solution.py:21
  69.6 24.5 %collective-permute-start.19 = (f32[8,2,6,64,128]{4,3,2,1,0:T(8,128)S(1)}, f32[8,2,6,64,128]{4,3,2,1,0:T(8,128)}, u32[]{:S(2)}, u32[]{:S(2)}) collective-permute-start(f32[8,2,6,64,128]{4,3,2,1,0:T(8,128)S(1)} %bitcast_dynamic-update-slice_fusion.2), channel_id=1, source_target_pairs={{0,1},{1,0},{2,3},{3,2},{4,5},{5,4},{6,7},{7,6},{8,9},{9,8},{10,11... | collective-permute-start | bytes 9437192 | tf_op jit(solution)/shard_map/ppermute | solution.py:16
  69.8 15.6 %collective-permute-start.9 = (f32[32,4096]{1,0:T(8,128)S(1)}, f32[32,4096]{1,0:T(8,128)S(1)}, u32[]{:S(2)}, u32[]{:S(2)}) collective-permute-start(f32[32,4096]{1,0:T(8,128)S(1)} %slice_bitcast_fusion), channel_id=1, source_target_pairs={{0,32},{32,64},{64,96},{96,0},{1,33},{33,65},{65,97},{97,1},{2,34}... | collective-permute-start | bytes 1572872 | tf_op jit(solution)/shard_map/ppermute | solution.py:21

commit v2 on v1

--- a/solution.py
+++ b/solution.py
@@ -39,22 +39,7 @@
 
 
 def gather_b(b_own):
-    n_z = lax.axis_size("z")
-    pair = jnp.stack([b_own, swap(b_own, "xh")])
-    by_offset = [None] * n_z
-    by_offset[0] = pair
-    up = pair
-    down = pair
-    half = n_z // 2
-    for d in range(1, half):
-        up = shift(up, "z", -1)
-        down = shift(down, "z", 1)
-        by_offset[d] = up
-        by_offset[n_z - d] = down
-    far_up = shift(up[0], "z", -1)
-    far_down = shift(down[1], "z", 1)
-    by_offset[half] = jnp.stack([far_up, far_down])
-    mine = jnp.stack(by_offset)
+    mine = lax.all_gather(b_own, ("z", "xh"), axis=0, tiled=True)
     return jnp.stack([mine, swap(mine, "core")])
 
 
@@ -64,18 +49,20 @@
     columns = b_stripes.shape[2]
     highest = lax.Precision.HIGHEST
 
-    ints = jnp.stack([a_rows[0, 0], a_slots[0, 0]])
-    ints_k, _ = gather_a(ints)
-    a_all, pid = gather_a(a_blocks[0, 0])
+    a_own = a_blocks[0, 0]
+    width = a_own.shape[1]
+    ints = jnp.stack([a_rows[0, 0], a_slots[0, 0]], axis=1).astype(jnp.float32)
+    ints = jnp.pad(ints, ((0, 0), (0, 128 - 2)))
+    payload, pid = gather_a(jnp.concatenate([a_own, ints], axis=1))
+    a_all = payload[:, :, :width]
+    ints_k = jnp.swapaxes(payload[:, :, width:width + 2], 1, 2).astype(jnp.int32)
     table = gather_b(b_stripes)
     table = table.reshape(-1, BLK, columns)
 
     rows = ints_k[:, 0]
     slots = ints_k[:, 1]
-    d = (pid[:, None] - z) % n_z
     core_rel = (slots // 6) % 2 ^ lax.axis_index("core")
-    xh_rel = (slots // 12) ^ lax.axis_index("xh")
-    index = ((core_rel * n_z + d) * 2 + xh_rel) * 6 + slots % 6
+    index = ((core_rel * n_z + pid[:, None]) * 2 + slots // 12) * 6 + slots % 6
     chosen = jnp.take(table, index.reshape(-1), axis=0)
     left = a_all.reshape(-1, BLK, BLK)
     terms = jnp.einsum("gij,gjc->gic", left, chosen, precision=lax.Precision.HIGH)

time: 133 us -> 169 us (1.27)
  waiting for transfers between devices: 40 us -> 81.3 us
  starting transfers between devices: 31 us -> 9.28 us
  between operations: 0.23 us -> 13.5 us
    all_gather x0 -> x1, waiting for transfers between devices: none -> 49.6 us  [gather_b(): mine = lax.all_gather(b_own, ('z', 'xh'), axis=0, tiled=True)]
    ppermute x16 -> x4, starting transfers between devices: 26.2 us -> 6.95 us  [shift(): lax.ppermute(block, axis, [(i, (i + distance) % n) for i in range(n)])]
    ppermute x16 -> x4, waiting for transfers between devices: 40 us -> 21.4 us  [shift(): lax.ppermute(block, axis, [(i, (i + distance) % n) for i in range(n)])]
    ppermute x4 -> x2, waiting for transfers between devices: 0.01 us -> 9.59 us  [swap(): return lax.ppermute(block, axis, [(0, 1), (1, 0)])]
    slice x0 -> x1, local copies, waits for them, and re-layouts: none -> 4.62 us  [shards(): a_all = payload[:, :, :width]]
    unnamed x14 -> x7, local copies, waits for them, and re-layouts: 6.88 us -> 3.93 us
    ppermute x4 -> x2, starting transfers between devices: 4.85 us -> 2.33 us  [swap(): return lax.ppermute(block, axis, [(0, 1), (1, 0)])]
  transfers between devices with their start and end apart: 20 -> 7, of which waited for: 12 -> 3; matrix products, arithmetic and copies ran while one was open for 17% -> 15% of each run, Pallas kernels for 0% -> 0%
where the time goes in v2:
time: 169 us; the launch traced here: 167 us
  waiting for transfers between devices  81.3 us (48%)
  local copies, waits for them, and re-layouts  27.3 us (16%)
  matrix products  24 us (14%)
  between operations  13.5 us (8%)
  other arithmetic  11.2 us (7%)
  starting transfers between devices  9.28 us (5%)
    all_gather x1, waiting for transfers between devices, gather_b(): mine = lax.all_gather(b_own, ('z', 'xh'), axis=0, tiled=True)  49.6 us
    ppermute x4, waiting for transfers between devices, shift(): lax.ppermute(block, axis, [(i, (i + distance) % n) for i in range(n)])  21.4 us
    dot_general x1, matrix products, shards(): jnp.einsum('gij,gjc->gic', left, chosen, precision=lax.Precision.HIGH)  13.3 us
    dot_general x1, matrix products, shards(): out = jnp.einsum('gm,gic->mic', place, terms, precision=highest)  10.6 us
    ppermute x2, waiting for transfers between devices, swap(): return lax.ppermute(block, axis, [(0, 1), (1, 0)])  9.59 us
    reshape x1, local copies, waits for them, and re-layouts, shards(): left = a_all.reshape(-1, BLK, BLK)  8.03 us
    gather x1, local copies, waits for them, and re-layouts, shards(): chosen = jnp.take(table, index.reshape(-1), axis=0)  7.09 us
    ppermute x4, starting transfers between devices, shift(): lax.ppermute(block, axis, [(i, (i + distance) % n) for i in range(n)])  6.95 us
  transfers between devices with their start and end apart: 7, of which 3 were waited for; matrix products, arithmetic and copies ran while one was open for 15% of the time, Pallas kernels for 0%

profile of v2, /device:TPU:2, one launch (start us, length us, event | category | flops | bytes accessed | tf_op | source)
XLA Modules:
  0.0 166.6 jit_solution(7138601471055393363)
XLA Ops:
  6.5 0.7 all-gather.2.cloned.1.call-update
  7.3 0.7 add_convert_fusion
  8.0 1.1 fusion.26
  9.1 2.3 %collective-permute-start = (f32[32,4224]{1,0:T(8,128)S(1)}, f32[32,4224]{1,0:T(8,128)S(1)}, u32[]{:S(2)}, u32[]{:S(2)}) collective-permute-start(f32[32,4224]{1,0:T(8,128)S(1)} %get-tuple-element.12), channel_id=1, source_target_pairs={{0,128},{128,0},{1,129},{129,1},{2,130},{130,2},{3,131},{131,3},{4... | collective-permute-start | bytes 1622024 | tf_op jit(solution)/shard_map/ppermute | solution.py:16
  11.8 1.9 %constant_dynamic-update-slice_fusion.3 = f32[8,32,4224]{2,1,0:T(8,128)} fusion(f32[32,2]{1,0:T(8,128)S(1)} %copy.11, f32[32,4096]{1,0:T(8,128)} %bitcast.39), kind=kLoop, calls=%fused_computation.31 | loop fusion | flops 405503 | bytes 1065216
  13.7 9.6 %collective-permute-done = f32[32,4224]{1,0:T(8,128)S(1)} collective-permute-done((f32[32,4224]{1,0:T(8,128)S(1)}, f32[32,4224]{1,0:T(8,128)S(1)}, u32[]{:S(2)}, u32[]{:S(2)}) %collective-permute-start) | collective-permute-done | bytes 540704 | tf_op jit(solution)/shard_map/ppermute | solution.py:16
  23.3 3.1 %collective-permute-start.2 = (f32[2,32,4224]{2,1,0:T(8,128)S(1)}, f32[2,32,4224]{2,1,0:T(8,128)S(1)}, u32[]{:S(2)}, u32[]{:S(2)}) collective-permute-start(f32[2,32,4224]{2,1,0:T(8,128)S(1)} %pad_maximum_fusion.1), channel_id=1, source_target_pairs={{0,96},{32,0},{64,32},{96,64},{1,97},{33,1},{65,33},{97,65},{2,98}... | collective-permute-start | bytes 3244040 | tf_op jit(solution)/shard_map/ppermute | solution.py:21
  26.4 0.8 constant_dynamic-update-slice_fusion.2
  27.3 21.4 %collective-permute-done.2 = f32[2,32,4224]{2,1,0:T(8,128)S(1)} collective-permute-done((f32[2,32,4224]{2,1,0:T(8,128)S(1)}, f32[2,32,4224]{2,1,0:T(8,128)S(1)}, u32[]{:S(2)}, u32[]{:S(2)}) %collective-permute-start.2) | collective-permute-done | bytes 1081376 | tf_op jit(solution)/shard_map/ppermute | solution.py:21
  48.7 3.8 %collective-permute-start.3 = (f32[32,4224]{1,0:T(8,128)S(1)}, f32[32,4224]{1,0:T(8,128)S(1)}, u32[]{:S(2)}, u32[]{:S(2)}) collective-permute-start(f32[32,4224]{1,0:T(8,128)S(1)} %slice_bitcast_fusion.1), channel_id=1, source_target_pairs={{0,96},{32,0},{64,32},{96,64},{1,97},{33,1},{65,33},{97,65},{2,98}... | collective-permute-start | bytes 1622024 | tf_op jit(solution)/shard_map/ppermute | solution.py:21
  52.6 1.1 constant_dynamic-update-slice_fusion.1
  53.7 1.1 constant_dynamic-update-slice_fusion
  54.8 49.6 %all-gather.2.cloned.1.call-done = f32[96,64,128]{2,1,0:T(8,128)} async-done(((f32[6,64,128]{2,1,0:T(8,128)}), f32[96,64,128]{2,1,0:T(8,128)}) %all-gather.2.cloned.1.call-update) | async-done | bytes 3145744 | tf_op jit(solution)/shard_map/all_gather | solution.py:42
  104.4 0.8 bitcast_dynamic-update-slice_fusion.1
  105.2 0.8 bitcast_dynamic-update-slice_fusion
  106.1 4.6 %slice.36 = f32[8,32,4096]{2,1,0:T(8,128)} slice(f32[8,32,4224]{2,1,0:T(8,128)} %bitcast_dynamic-update-slice_fusion), slice={[0:8], [0:32], [0:4096]} | slice | bytes 8388608 | tf_op jit(solution)/shard_map/slice | solution.py:57
  110.7 0.9 fusion.6
  112.4 0.7 slice_reduce_fusion
  113.6 8.0 %reshape.203 = f32[256,64,64]{2,1,0:T(8,128)} reshape(f32[8,32,4096]{2,1,0:T(8,128)} %slice.36) | data formatting | bytes 8388608 | tf_op jit(solution)/shard_map/reshape | solution.py:67
  121.7 5.4 %pad_maximum_fusion = f32[2,96,64,128]{3,2,1,0:T(8,128)} fusion(f32[1,96,64,128]{3,2,1,0:T(8,128)} %bitcast.20, f32[1,96,64,128]{3,2,1,0:T(8,128)S(1)} %bitcast.36), kind=kLoop, calls=%fused_computation.5 | loop fusion | flops 1572864 | bytes 12582912 | tf_op jit(solution)/shard_map/stack | solution.py:43
  127.1 7.1 %gather_fusion = f32[256,64,128]{2,1,0:T(8,128)} fusion(f32[192,64,128]{2,1,0:T(8,128)} %bitcast.35, s32[1024]{0:T(1024)S(1)} %pad_clamp_fusion), kind=kCustom, calls=%fused_computation | custom fusion | bytes 16778240 | tf_op jit(solution)/shard_map/jit(_take)/gather | solution.py:66
  134.2 13.3 %fusion.2 = f32[256,64,128]{2,1,0:T(8,128)} fusion(f32[256,64,64]{2,1,0:T(8,128)} %reshape.203, f32[256,64,128]{2,1,0:T(8,128)} %gather_fusion, pred[256]{0:T(512)(128)(4,1)S(1)} %compare_and_fusion), kind=kOutput, calls=%fused_computation.3 | convolution fusion | flops 807403520 | bytes 20971776 | tf_op jit(solution)/shard_map/gij,gjc->gic/dot_general | solution.py:68
  147.5 10.6 %fusion = f32[32,64,128]{2,0,1:T(8,128)S(1)} fusion(f32[256,64,128]{2,1,0:T(8,128)} %fusion.2, s32[256]{0:T(256)S(1)} %eq.27), kind=kOutput, calls=%fused_computation.1 | convolution fusion | flops 805314560 | bytes 9438208 | tf_op jit(solution)/shard_map/gm,gic->mic/dot_general | solution.py:70
  158.2 1.6 copy.10
  (33 shorter events, 2.0 us)
Async XLA Ops:
  6.5 97.9 %all-gather.2.cloned.1.call-start = ((), (), s32[]{:S(2)}) async-start(), calls=%async_computation | async-start | bytes 3342336 | tf_op jit(solution)/shard_map/all_gather | solution.py:42
  9.1 14.1 %collective-permute-start = (f32[32,4224]{1,0:T(8,128)S(1)}, f32[32,4224]{1,0:T(8,128)S(1)}, u32[]{:S(2)}, u32[]{:S(2)}) collective-permute-start(f32[32,4224]{1,0:T(8,128)S(1)} %get-tuple-element.12), channel_id=1, source_target_pairs={{0,128},{128,0},{1,129},{129,1},{2,130},{130,2},{3,131},{131,3},{4... | collective-permute-start | bytes 1622024 | tf_op jit(solution)/shard_map/ppermute | solution.py:16
  23.3 25.4 %collective-permute-start.2 = (f32[2,32,4224]{2,1,0:T(8,128)S(1)}, f32[2,32,4224]{2,1,0:T(8,128)S(1)}, u32[]{:S(2)}, u32[]{:S(2)}) collective-permute-start(f32[2,32,4224]{2,1,0:T(8,128)S(1)} %pad_maximum_fusion.1), channel_id=1, source_target_pairs={{0,96},{32,0},{64,32},{96,64},{1,97},{33,1},{65,33},{97,65},{2,98}... | collective-permute-start | bytes 3244040 | tf_op jit(solution)/shard_map/ppermute | solution.py:21
  26.4 26.1 %collective-permute-start.1 = (f32[2,32,4224]{2,1,0:T(8,128)S(1)}, f32[2,32,4224]{2,1,0:T(8,128)S(1)}, u32[]{:S(2)}, u32[]{:S(2)}) collective-permute-start(f32[2,32,4224]{2,1,0:T(8,128)S(1)} %pad_maximum_fusion.1), channel_id=1, source_target_pairs={{0,32},{32,64},{64,96},{96,0},{1,33},{33,65},{65,97},{97,1},{2,34}... | collective-permute-start | bytes 3244040 | tf_op jit(solution)/shard_map/ppermute | solution.py:21
  48.7 55.7 %collective-permute-start.3 = (f32[32,4224]{1,0:T(8,128)S(1)}, f32[32,4224]{1,0:T(8,128)S(1)}, u32[]{:S(2)}, u32[]{:S(2)}) collective-permute-start(f32[32,4224]{1,0:T(8,128)S(1)} %slice_bitcast_fusion.1), channel_id=1, source_target_pairs={{0,96},{32,0},{64,32},{96,64},{1,97},{33,1},{65,33},{97,65},{2,98}... | collective-permute-start | bytes 1622024 | tf_op jit(solution)/shard_map/ppermute | solution.py:21
  52.5 52.7 %collective-permute-start.4 = (f32[32,4224]{1,0:T(8,128)S(1)}, f32[32,4224]{1,0:T(8,128)S(1)}, u32[]{:S(2)}, u32[]{:S(2)}) collective-permute-start(f32[32,4224]{1,0:T(8,128)S(1)} %slice_bitcast_fusion), channel_id=1, source_target_pairs={{0,32},{32,64},{64,96},{96,0},{1,33},{33,65},{65,97},{97,1},{2,34}... | collective-permute-start | bytes 1622024 | tf_op jit(solution)/shard_map/ppermute | solution.py:21
  104.4 17.3 %collective-permute-start.5 = (f32[96,64,128]{2,1,0:T(8,128)}, f32[96,64,128]{2,1,0:T(8,128)}, u32[]{:S(2)}, u32[]{:S(2)}) collective-permute-start(f32[96,64,128]{2,1,0:T(8,128)} %all-gather.2.cloned.1.call-done), channel_id=1, source_target_pairs={{0,1},{1,0},{2,3},{3,2},{4,5},{5,4},{6,7},{7,6},{8,9},{9,8},{10,11... | collective-permute-start | bytes 9437192 | tf_op jit(solution)/shard_map/ppermute | solution.py:16
  113.6 8.1 %copy-start = (f32[96,64,128]{2,1,0:T(8,128)S(1)}, f32[96,64,128]{2,1,0:T(8,128)}, u32[]{:S(2)}) copy-start(f32[96,64,128]{2,1,0:T(8,128)} %all-gather.2.cloned.1.call-done) | copy-start | bytes 9437188
Sparse Core Ops, SparseCore 0:
  9.9 94.4 all-gather.1

commit v3 on v1

--- a/solution.py
+++ b/solution.py
@@ -54,19 +54,21 @@
     far_up = shift(up[0], "z", -1)
     far_down = shift(down[1], "z", 1)
     by_offset[half] = jnp.stack([far_up, far_down])
-    mine = jnp.stack(by_offset)
-    return jnp.stack([mine, swap(mine, "core")])
+    return jnp.stack(by_offset + [swap(piece, "core") for piece in by_offset])
 
 
 def shards(a_blocks, a_rows, a_slots, b_stripes):
     n_z = lax.axis_size("z")
     z = lax.axis_index("z")
     columns = b_stripes.shape[2]
-    highest = lax.Precision.HIGHEST
 
-    ints = jnp.stack([a_rows[0, 0], a_slots[0, 0]])
-    ints_k, _ = gather_a(ints)
-    a_all, pid = gather_a(a_blocks[0, 0])
+    a_own = a_blocks[0, 0]
+    width = a_own.shape[1]
+    ints = jnp.stack([a_rows[0, 0], a_slots[0, 0]], axis=1).astype(jnp.float32)
+    ints = jnp.pad(ints, ((0, 0), (0, 128 - 2)))
+    payload, pid = gather_a(jnp.concatenate([a_own, ints], axis=1))
+    a_all = payload[:, :, :width]
+    ints_k = jnp.swapaxes(payload[:, :, width:width + 2], 1, 2).astype(jnp.int32)
     table = gather_b(b_stripes)
     table = table.reshape(-1, BLK, columns)
 
@@ -80,7 +82,7 @@
     left = a_all.reshape(-1, BLK, BLK)
     terms = jnp.einsum("gij,gjc->gic", left, chosen, precision=lax.Precision.HIGH)
     place = (rows.reshape(-1)[:, None] == jnp.arange(MB, dtype=jnp.int32)[None, :]).astype(jnp.float32)
-    out = jnp.einsum("gm,gic->mic", place, terms, precision=highest)
+    out = jnp.einsum("gm,gic->mic", place, terms, precision=lax.Precision.HIGH)
     return out.reshape(MB * BLK, columns)
 
 

time: 133 us -> 144 us (1.083)
  local copies, waits for them, and re-layouts: 26.1 us -> 38.2 us
  waiting for transfers between devices: 40 us -> 44.1 us
  starting transfers between devices: 31 us -> 28.4 us
  matrix products: 24 us -> 22.4 us
  other arithmetic: 10.8 us -> 9.31 us
    ppermute x4 -> x10, waiting for transfers between devices: 0.01 us -> 14 us  [swap(): return lax.ppermute(block, axis, [(0, 1), (1, 0)])]
    ppermute x16 -> x12, waiting for transfers between devices: 40 us -> 30.1 us  [shift(): lax.ppermute(block, axis, [(i, (i + distance) % n) for i in range(n)])]
    unnamed x14 -> x18, local copies, waits for them, and re-layouts: 6.88 us -> 14.1 us
    another operation x1, other arithmetic: 5.38 us -> 0.03 us  [gather_b(): by_offset[half] = jnp.stack([far_up, far_down])]
    slice x0 -> x1, local copies, waits for them, and re-layouts: none -> 4.62 us  [shards(): a_all = payload[:, :, :width]]
    unnamed x3, other arithmetic: 1.66 us -> 4.36 us
    ppermute x16 -> x12, starting transfers between devices: 26.2 us -> 23.5 us  [shift(): lax.ppermute(block, axis, [(i, (i + distance) % n) for i in range(n)])]
    convert_element_type x0 -> x2, other arithmetic: none -> 1.6 us  [the longest x1 0.92 us: shards(): jnp.swapaxes(payload[:, :, width:width + 2], 1, 2).astype(jnp.int32)]
  transfers between devices with their start and end apart: 20 -> 22, of which waited for: 12 -> 9; matrix products, arithmetic and copies ran while one was open for 17% -> 14% of each run, Pallas kernels for 0% -> 0%
where the time goes in v3:
time: 144 us; the launch traced here: 143 us
  waiting for transfers between devices  44.1 us (31%)
  local copies, waits for them, and re-layouts  38.2 us (27%)
  starting transfers between devices  28.4 us (20%)
  matrix products  22.4 us (16%)
  other arithmetic  9.31 us (6%)
    ppermute x12, waiting for transfers between devices, shift(): lax.ppermute(block, axis, [(i, (i + distance) % n) for i in range(n)])  30.1 us
    ppermute x12, starting transfers between devices, shift(): lax.ppermute(block, axis, [(i, (i + distance) % n) for i in range(n)])  23.5 us
    unnamed x18, local copies, waits for them, and re-layouts  14.1 us
    ppermute x10, waiting for transfers between devices, swap(): return lax.ppermute(block, axis, [(0, 1), (1, 0)])  14 us
    dot_general x1, matrix products, shards(): jnp.einsum('gij,gjc->gic', left, chosen, precision=lax.Precision.HIGH)  13.3 us
    dot_general x1, matrix products, shards(): out = jnp.einsum('gm,gic->mic', place, terms, precision=lax.Precision.HIGH)  9.08 us
    reshape x1, local copies, waits for them, and re-layouts, shards(): left = a_all.reshape(-1, BLK, BLK)  7.9 us
    gather x1, local copies, waits for them, and re-layouts, shards(): chosen = jnp.take(table, index.reshape(-1), axis=0)  7.1 us
  transfers between devices with their start and end apart: 22, of which 9 were waited for; matrix products, arithmetic and copies ran while one was open for 14% of the time, Pallas kernels for 0%

profile of v3, /device:TPU:2, one launch (start us, length us, event | category | flops | bytes accessed | tf_op | source)
XLA Modules:
  0.0 142.6 jit_solution(1410596931710218507)
XLA Ops:
  1.9 2.3 %collective-permute-start = (f32[32,4224]{1,0:T(8,128)S(1)}, f32[32,4224]{1,0:T(8,128)S(1)}, u32[]{:S(2)}, u32[]{:S(2)}) collective-permute-start(f32[32,4224]{1,0:T(8,128)S(1)} %get-tuple-element.12), channel_id=1, source_target_pairs={{0,128},{128,0},{1,129},{129,1},{2,130},{130,2},{3,131},{131,3},{4... | collective-permute-start | bytes 1622024 | tf_op jit(solution)/shard_map/ppermute | solution.py:16
  4.9 1.9 %constant_dynamic-update-slice_fusion.3 = f32[8,32,4224]{2,1,0:T(8,128)} fusion(f32[32,2]{1,0:T(8,128)S(1)} %copy.9, f32[32,4096]{1,0:T(8,128)} %bitcast.75), kind=kLoop, calls=%fused_computation.47 | loop fusion | flops 405503 | bytes 1065216
  7.1 14.0 %collective-permute-done.5 = f32[6,64,128]{2,1,0:T(8,128)S(1)} collective-permute-done((f32[6,64,128]{2,1,0:T(8,128)}, f32[6,64,128]{2,1,0:T(8,128)S(1)}, u32[]{:S(2)}, u32[]{:S(2)}) %collective-permute-start.5) | collective-permute-done | bytes 196640 | tf_op jit(solution)/shard_map/ppermute | solution.py:16
  22.1 5.9 %collective-permute-start.6 = (f32[2,6,64,128]{3,2,1,0:T(8,128)S(1)}, f32[2,6,64,128]{3,2,1,0:T(8,128)S(1)}, u32[]{:S(2)}, u32[]{:S(2)}) collective-permute-start(f32[2,6,64,128]{3,2,1,0:T(8,128)S(1)} %pad_maximum_fusion.1), channel_id=1, source_target_pairs={{0,28},{4,0},{8,4},{12,8},{16,12},{20,16},{24,20},{28,24},{1,29},{... | collective-permute-start | bytes 1179656 | tf_op jit(solution)/shard_map/ppermute | solution.py:21
  28.0 1.7 %bitcast_dynamic-update-slice_fusion.17 = f32[16,2,6,64,128]{4,3,2,1,0:T(8,128)} fusion(f32[1,6,64,128]{3,2,1,0:T(8,128)S(1)} %bitcast.79, f32[1,6,64,128]{3,2,1,0:T(8,128)} %bitcast.77), kind=kLoop, calls=%fused_computation.31 | loop fusion | flops 98303 | bytes 786432
  29.8 1.7 %collective-permute-start.1 = (f32[2,32,4224]{2,1,0:T(8,128)S(1)}, f32[2,32,4224]{2,1,0:T(8,128)S(1)}, u32[]{:S(2)}, u32[]{:S(2)}) collective-permute-start(f32[2,32,4224]{2,1,0:T(8,128)S(1)} %pad_maximum_fusion), channel_id=1, source_target_pairs={{0,32},{32,64},{64,96},{96,0},{1,33},{33,65},{65,97},{97,1},{2,34}... | collective-permute-start | bytes 3244040 | tf_op jit(solution)/shard_map/ppermute | solution.py:21
  31.5 1.7 %collective-permute-start.2 = (f32[2,32,4224]{2,1,0:T(8,128)S(1)}, f32[2,32,4224]{2,1,0:T(8,128)S(1)}, u32[]{:S(2)}, u32[]{:S(2)}) collective-permute-start(f32[2,32,4224]{2,1,0:T(8,128)S(1)} %pad_maximum_fusion), channel_id=1, source_target_pairs={{0,96},{32,0},{64,32},{96,64},{1,97},{33,1},{65,33},{97,65},{2,98}... | collective-permute-start | bytes 3244040 | tf_op jit(solution)/shard_map/ppermute | solution.py:21
  33.1 2.4 %collective-permute-done.6 = f32[2,6,64,128]{3,2,1,0:T(8,128)S(1)} collective-permute-done((f32[2,6,64,128]{3,2,1,0:T(8,128)S(1)}, f32[2,6,64,128]{3,2,1,0:T(8,128)S(1)}, u32[]{:S(2)}, u32[]{:S(2)}) %collective-permute-start.6) | collective-permute-done | bytes 393248 | tf_op jit(solution)/shard_map/ppermute | solution.py:21
  35.5 3.7 %collective-permute-start.7 = (f32[2,6,64,128]{3,2,1,0:T(8,128)S(1)}, f32[2,6,64,128]{3,2,1,0:T(8,128)S(1)}, u32[]{:S(2)}, u32[]{:S(2)}) collective-permute-start(f32[2,6,64,128]{3,2,1,0:T(8,128)S(1)} %collective-permute-done.6), channel_id=1, source_target_pairs={{0,28},{4,0},{8,4},{12,8},{16,12},{20,16},{24,20},{28,24},{1,29},{... | collective-permute-start | bytes 1179656 | tf_op jit(solution)/shard_map/ppermute | solution.py:21
  40.1 5.8 %collective-permute-done.7 = f32[2,6,64,128]{3,2,1,0:T(8,128)S(1)} collective-permute-done((f32[2,6,64,128]{3,2,1,0:T(8,128)S(1)}, f32[2,6,64,128]{3,2,1,0:T(8,128)S(1)}, u32[]{:S(2)}, u32[]{:S(2)}) %collective-permute-start.7) | collective-permute-done | bytes 393248 | tf_op jit(solution)/shard_map/ppermute | solution.py:21
  45.9 3.7 %collective-permute-start.8 = (f32[2,6,64,128]{3,2,1,0:T(8,128)S(1)}, f32[2,6,64,128]{3,2,1,0:T(8,128)S(1)}, u32[]{:S(2)}, u32[]{:S(2)}) collective-permute-start(f32[2,6,64,128]{3,2,1,0:T(8,128)S(1)} %collective-permute-done.7), channel_id=1, source_target_pairs={{0,28},{4,0},{8,4},{12,8},{16,12},{20,16},{24,20},{28,24},{1,29},{... | collective-permute-start | bytes 1179656 | tf_op jit(solution)/shard_map/ppermute | solution.py:21
  51.2 4.2 %collective-permute-done.8 = f32[2,6,64,128]{3,2,1,0:T(8,128)S(1)} collective-permute-done((f32[2,6,64,128]{3,2,1,0:T(8,128)S(1)}, f32[2,6,64,128]{3,2,1,0:T(8,128)S(1)}, u32[]{:S(2)}, u32[]{:S(2)}) %collective-permute-start.8) | collective-permute-done | bytes 393248 | tf_op jit(solution)/shard_map/ppermute | solution.py:21
  55.4 3.8 %collective-permute-start.9 = (f32[6,64,128]{2,1,0:T(8,128)S(1)}, f32[6,64,128]{2,1,0:T(8,128)S(1)}, u32[]{:S(2)}, u32[]{:S(2)}) collective-permute-start(f32[6,64,128]{2,1,0:T(8,128)S(1)} %slice_bitcast_fusion.3), channel_id=1, source_target_pairs={{0,28},{4,0},{8,4},{12,8},{16,12},{20,16},{24,20},{28,24},{1,29},{... | collective-permute-start | bytes 589832 | tf_op jit(solution)/shard_map/ppermute | solution.py:21
  60.5 1.9 %collective-permute-done.9 = f32[6,64,128]{2,1,0:T(8,128)S(1)} collective-permute-done((f32[6,64,128]{2,1,0:T(8,128)S(1)}, f32[6,64,128]{2,1,0:T(8,128)S(1)}, u32[]{:S(2)}, u32[]{:S(2)}) %collective-permute-start.9) | collective-permute-done | bytes 196640 | tf_op jit(solution)/shard_map/ppermute | solution.py:21
  62.4 4.2 %collective-permute-done.13 = f32[6,64,128]{2,1,0:T(8,128)S(1)} collective-permute-done((f32[6,64,128]{2,1,0:T(8,128)S(1)}, f32[6,64,128]{2,1,0:T(8,128)S(1)}, u32[]{:S(2)}, u32[]{:S(2)}) %collective-permute-start.13) | collective-permute-done | bytes 196640 | tf_op jit(solution)/shard_map/ppermute | solution.py:21
  76.2 3.0 %collective-permute-start.3 = (f32[32,4224]{1,0:T(8,128)S(1)}, f32[32,4224]{1,0:T(8,128)S(1)}, u32[]{:S(2)}, u32[]{:S(2)}) collective-permute-start(f32[32,4224]{1,0:T(8,128)S(1)} %slice_bitcast_fusion.1), channel_id=1, source_target_pairs={{0,96},{32,0},{64,32},{96,64},{1,97},{33,1},{65,33},{97,65},{2,98}... | collective-permute-start | bytes 1622024 | tf_op jit(solution)/shard_map/ppermute | solution.py:21
  83.1 7.8 %collective-permute-done.3 = f32[32,4224]{1,0:T(8,128)S(1)} collective-permute-done((f32[32,4224]{1,0:T(8,128)S(1)}, f32[32,4224]{1,0:T(8,128)S(1)}, u32[]{:S(2)}, u32[]{:S(2)}) %collective-permute-start.3) | collective-permute-done | bytes 540704 | tf_op jit(solution)/shard_map/ppermute | solution.py:21
  91.8 3.3 %collective-permute-done.4 = f32[32,4224]{1,0:T(8,128)S(1)} collective-permute-done((f32[32,4224]{1,0:T(8,128)S(1)}, f32[32,4224]{1,0:T(8,128)S(1)}, u32[]{:S(2)}, u32[]{:S(2)}) %collective-permute-start.4) | collective-permute-done | bytes 540704 | tf_op jit(solution)/shard_map/ppermute | solution.py:21
  98.8 4.6 %slice.44 = f32[8,32,4096]{2,1,0:T(8,128)} slice(f32[8,32,4224]{2,1,0:T(8,128)} %bitcast_dynamic-update-slice_fusion), slice={[0:8], [0:32], [0:4096]} | slice | bytes 8388608 | tf_op jit(solution)/shard_map/slice | solution.py:70
  103.5 7.9 %reshape.288 = f32[256,64,64]{2,1,0:T(8,128)} reshape(f32[8,32,4096]{2,1,0:T(8,128)} %slice.44) | data formatting | bytes 8388608 | tf_op jit(solution)/shard_map/reshape | solution.py:82
  111.4 7.1 %gather_fusion = f32[256,64,128]{2,1,0:T(8,128)} fusion(f32[192,64,128]{2,1,0:T(8,128)} %bitcast.41, s32[1024]{0:T(1024)S(1)} %pad_clamp_fusion), kind=kCustom, calls=%fused_computation | custom fusion | bytes 16778240 | tf_op jit(solution)/shard_map/jit(_take)/gather | solution.py:81
  118.6 13.3 %fusion.2 = f32[256,64,128]{2,1,0:T(8,128)} fusion(f32[256,64,64]{2,1,0:T(8,128)} %reshape.288, f32[256,64,128]{2,1,0:T(8,128)} %gather_fusion, pred[256]{0:T(512)(128)(4,1)S(1)} %compare_and_fusion), kind=kOutput, calls=%fused_computation.3 | convolution fusion | flops 807403520 | bytes 20971776 | tf_op jit(solution)/shard_map/gij,gjc->gic/dot_general | solution.py:83
  131.9 9.1 %fusion = f32[32,64,128]{2,0,1:T(8,128)S(1)} fusion(f32[256,64,128]{2,1,0:T(8,128)} %fusion.2, s32[256]{0:T(256)S(1)} %eq.29), kind=kOutput, calls=%fused_computation.1 | convolution fusion | flops 402661376 | bytes 9438208 | tf_op jit(solution)/shard_map/gm,gic->mic/dot_general | solution.py:85
  141.0 1.6 %copy.7 = f32[32,64,128]{2,1,0:T(8,128)} copy(f32[32,64,128]{2,0,1:T(8,128)S(1)} %fusion) | data formatting | bytes 2097152 | tf_op jit(solution)/shard_map/gm,gic->mic/dot_general | solution.py:85
  (80 shorter events, 25.9 us)
Async XLA Ops:
  1.9 27.8 %collective-permute-start = (f32[32,4224]{1,0:T(8,128)S(1)}, f32[32,4224]{1,0:T(8,128)S(1)}, u32[]{:S(2)}, u32[]{:S(2)}) collective-permute-start(f32[32,4224]{1,0:T(8,128)S(1)} %get-tuple-element.12), channel_id=1, source_target_pairs={{0,128},{128,0},{1,129},{129,1},{2,130},{130,2},{3,131},{131,3},{4... | collective-permute-start | bytes 1622024 | tf_op jit(solution)/shard_map/ppermute | solution.py:16
  4.2 16.9 %collective-permute-start.5 = (f32[6,64,128]{2,1,0:T(8,128)}, f32[6,64,128]{2,1,0:T(8,128)S(1)}, u32[]{:S(2)}, u32[]{:S(2)}) collective-permute-start(f32[6,64,128]{2,1,0:T(8,128)} %param.7), channel_id=1, source_target_pairs={{0,2},{2,0},{1,3},{3,1},{4,6},{6,4},{5,7},{7,5},{8,10},{10,8},{9,1... | collective-permute-start | bytes 589832 | tf_op jit(solution)/shard_map/ppermute | solution.py:16
  22.1 13.5 %collective-permute-start.6 = (f32[2,6,64,128]{3,2,1,0:T(8,128)S(1)}, f32[2,6,64,128]{3,2,1,0:T(8,128)S(1)}, u32[]{:S(2)}, u32[]{:S(2)}) collective-permute-start(f32[2,6,64,128]{3,2,1,0:T(8,128)S(1)} %pad_maximum_fusion.1), channel_id=1, source_target_pairs={{0,28},{4,0},{8,4},{12,8},{16,12},{20,16},{24,20},{28,24},{1,29},{... | collective-permute-start | bytes 1179656 | tf_op jit(solution)/shard_map/ppermute | solution.py:21
  28.0 11.2 %collective-permute-start.10 = (f32[2,6,64,128]{3,2,1,0:T(8,128)S(1)}, f32[2,6,64,128]{3,2,1,0:T(8,128)S(1)}, u32[]{:S(2)}, u32[]{:S(2)}) collective-permute-start(f32[2,6,64,128]{3,2,1,0:T(8,128)S(1)} %pad_maximum_fusion.1), channel_id=1, source_target_pairs={{0,4},{4,8},{8,12},{12,16},{16,20},{20,24},{24,28},{28,0},{1,5},{5... | collective-permute-start | bytes 1179656 | tf_op jit(solution)/shard_map/ppermute | solution.py:21
  28.0 41.7 %collective-permute-start.14 = (f32[2,6,64,128]{3,2,1,0:T(8,128)S(1)}, f32[2,6,64,128]{3,2,1,0:T(8,128)S(1)}, u32[]{:S(2)}, u32[]{:S(2)}) collective-permute-start(f32[2,6,64,128]{3,2,1,0:T(8,128)S(1)} %pad_maximum_fusion.1), channel_id=1, source_target_pairs={{0,1},{1,0},{2,3},{3,2},{4,5},{5,4},{6,7},{7,6},{8,9},{9,8},{10,11... | collective-permute-start | bytes 1179656 | tf_op jit(solution)/shard_map/ppermute | solution.py:16
  29.8 43.5 %collective-permute-start.1 = (f32[2,32,4224]{2,1,0:T(8,128)S(1)}, f32[2,32,4224]{2,1,0:T(8,128)S(1)}, u32[]{:S(2)}, u32[]{:S(2)}) collective-permute-start(f32[2,32,4224]{2,1,0:T(8,128)S(1)} %pad_maximum_fusion), channel_id=1, source_target_pairs={{0,32},{32,64},{64,96},{96,0},{1,33},{33,65},{65,97},{97,1},{2,34}... | collective-permute-start | bytes 3244040 | tf_op jit(solution)/shard_map/ppermute | solution.py:21
  31.5 43.0 %collective-permute-start.2 = (f32[2,32,4224]{2,1,0:T(8,128)S(1)}, f32[2,32,4224]{2,1,0:T(8,128)S(1)}, u32[]{:S(2)}, u32[]{:S(2)}) collective-permute-start(f32[2,32,4224]{2,1,0:T(8,128)S(1)} %pad_maximum_fusion), channel_id=1, source_target_pairs={{0,96},{32,0},{64,32},{96,64},{1,97},{33,1},{65,33},{97,65},{2,98}... | collective-permute-start | bytes 3244040 | tf_op jit(solution)/shard_map/ppermute | solution.py:21
  35.5 10.4 %collective-permute-start.7 = (f32[2,6,64,128]{3,2,1,0:T(8,128)S(1)}, f32[2,6,64,128]{3,2,1,0:T(8,128)S(1)}, u32[]{:S(2)}, u32[]{:S(2)}) collective-permute-start(f32[2,6,64,128]{3,2,1,0:T(8,128)S(1)} %collective-permute-done.6), channel_id=1, source_target_pairs={{0,28},{4,0},{8,4},{12,8},{16,12},{20,16},{24,20},{28,24},{1,29},{... | collective-permute-start | bytes 1179656 | tf_op jit(solution)/shard_map/ppermute | solution.py:21
  39.2 11.1 %collective-permute-start.11 = (f32[2,6,64,128]{3,2,1,0:T(8,128)S(1)}, f32[2,6,64,128]{3,2,1,0:T(8,128)S(1)}, u32[]{:S(2)}, u32[]{:S(2)}) collective-permute-start(f32[2,6,64,128]{3,2,1,0:T(8,128)S(1)} %collective-permute-done.10), channel_id=1, source_target_pairs={{0,4},{4,8},{8,12},{12,16},{16,20},{20,24},{24,28},{28,0},{1,5},{5... | collective-permute-start | bytes 1179656 | tf_op jit(solution)/shard_map/ppermute | solution.py:21
  45.9 9.5 %collective-permute-start.8 = (f32[2,6,64,128]{3,2,1,0:T(8,128)S(1)}, f32[2,6,64,128]{3,2,1,0:T(8,128)S(1)}, u32[]{:S(2)}, u32[]{:S(2)}) collective-permute-start(f32[2,6,64,128]{3,2,1,0:T(8,128)S(1)} %collective-permute-done.7), channel_id=1, source_target_pairs={{0,28},{4,0},{8,4},{12,8},{16,12},{20,16},{24,20},{28,24},{1,29},{... | collective-permute-start | bytes 1179656 | tf_op jit(solution)/shard_map/ppermute | solution.py:21
  50.4 9.2 %collective-permute-start.12 = (f32[2,6,64,128]{3,2,1,0:T(8,128)S(1)}, f32[2,6,64,128]{3,2,1,0:T(8,128)S(1)}, u32[]{:S(2)}, u32[]{:S(2)}) collective-permute-start(f32[2,6,64,128]{3,2,1,0:T(8,128)S(1)} %collective-permute-done.11), channel_id=1, source_target_pairs={{0,4},{4,8},{8,12},{12,16},{16,20},{20,24},{24,28},{28,0},{1,5},{5... | collective-permute-start | bytes 1179656 | tf_op jit(solution)/shard_map/ppermute | solution.py:21
  55.4 7.0 %collective-permute-start.9 = (f32[6,64,128]{2,1,0:T(8,128)S(1)}, f32[6,64,128]{2,1,0:T(8,128)S(1)}, u32[]{:S(2)}, u32[]{:S(2)}) collective-permute-start(f32[6,64,128]{2,1,0:T(8,128)S(1)} %slice_bitcast_fusion.3), channel_id=1, source_target_pairs={{0,28},{4,0},{8,4},{12,8},{16,12},{20,16},{24,20},{28,24},{1,29},{... | collective-permute-start | bytes 589832 | tf_op jit(solution)/shard_map/ppermute | solution.py:21
  59.6 7.0 %collective-permute-start.13 = (f32[6,64,128]{2,1,0:T(8,128)S(1)}, f32[6,64,128]{2,1,0:T(8,128)S(1)}, u32[]{:S(2)}, u32[]{:S(2)}) collective-permute-start(f32[6,64,128]{2,1,0:T(8,128)S(1)} %slice_bitcast_fusion.2), channel_id=1, source_target_pairs={{0,4},{4,8},{8,12},{12,16},{16,20},{20,24},{24,28},{28,0},{1,5},{5... | collective-permute-start | bytes 589832 | tf_op jit(solution)/shard_map/ppermute | solution.py:21
  62.4 8.7 %collective-permute-start.15 = (f32[2,6,64,128]{3,2,1,0:T(8,128)S(1)}, f32[2,6,64,128]{3,2,1,0:T(8,128)S(1)}, u32[]{:S(2)}, u32[]{:S(2)}) collective-permute-start(f32[2,6,64,128]{3,2,1,0:T(8,128)S(1)} %collective-permute-done.6), channel_id=1, source_target_pairs={{0,1},{1,0},{2,3},{3,2},{4,5},{5,4},{6,7},{7,6},{8,9},{9,8},{10,11... | collective-permute-start | bytes 1179656 | tf_op jit(solution)/shard_map/ppermute | solution.py:16
  66.6 15.8 %collective-permute-start.21 = (f32[2,6,64,128]{3,2,1,0:T(8,128)S(1)}, f32[2,6,64,128]{3,2,1,0:T(8,128)S(1)}, u32[]{:S(2)}, u32[]{:S(2)}) collective-permute-start(f32[2,6,64,128]{3,2,1,0:T(8,128)S(1)} %collective-permute-done.10), channel_id=1, source_target_pairs={{0,1},{1,0},{2,3},{3,2},{4,5},{5,4},{6,7},{7,6},{8,9},{9,8},{10,11... | collective-permute-start | bytes 1179656 | tf_op jit(solution)/shard_map/ppermute | solution.py:16
  69.7 2.4 %collective-permute-start.16 = (f32[2,6,64,128]{3,2,1,0:T(8,128)S(1)}, f32[2,6,64,128]{3,2,1,0:T(8,128)S(1)}, u32[]{:S(2)}, u32[]{:S(2)}) collective-permute-start(f32[2,6,64,128]{3,2,1,0:T(8,128)S(1)} %collective-permute-done.7), channel_id=1, source_target_pairs={{0,1},{1,0},{2,3},{3,2},{4,5},{5,4},{6,7},{7,6},{8,9},{9,8},{10,11... | collective-permute-start | bytes 1179656 | tf_op jit(solution)/shard_map/ppermute | solution.py:16
  71.0 10.6 %collective-permute-start.20 = (f32[2,6,64,128]{3,2,1,0:T(8,128)S(1)}, f32[2,6,64,128]{3,2,1,0:T(8,128)S(1)}, u32[]{:S(2)}, u32[]{:S(2)}) collective-permute-start(f32[2,6,64,128]{3,2,1,0:T(8,128)S(1)} %collective-permute-done.11), channel_id=1, source_target_pairs={{0,1},{1,0},{2,3},{3,2},{4,5},{5,4},{6,7},{7,6},{8,9},{9,8},{10,11... | collective-permute-start | bytes 1179656 | tf_op jit(solution)/shard_map/ppermute | solution.py:16
  72.1 4.1 %collective-permute-start.17 = (f32[2,6,64,128]{3,2,1,0:T(8,128)S(1)}, f32[2,6,64,128]{3,2,1,0:T(8,128)S(1)}, u32[]{:S(2)}, u32[]{:S(2)}) collective-permute-start(f32[2,6,64,128]{3,2,1,0:T(8,128)S(1)} %collective-permute-done.8), channel_id=1, source_target_pairs={{0,1},{1,0},{2,3},{3,2},{4,5},{5,4},{6,7},{7,6},{8,9},{9,8},{10,11... | collective-permute-start | bytes 1179656 | tf_op jit(solution)/shard_map/ppermute | solution.py:16
  73.3 7.5 %collective-permute-start.19 = (f32[2,6,64,128]{3,2,1,0:T(8,128)S(1)}, f32[2,6,64,128]{3,2,1,0:T(8,128)S(1)}, u32[]{:S(2)}, u32[]{:S(2)}) collective-permute-start(f32[2,6,64,128]{3,2,1,0:T(8,128)S(1)} %collective-permute-done.12), channel_id=1, source_target_pairs={{0,1},{1,0},{2,3},{3,2},{4,5},{5,4},{6,7},{7,6},{8,9},{9,8},{10,11... | collective-permute-start | bytes 1179656 | tf_op jit(solution)/shard_map/ppermute | solution.py:16
  74.5 5.5 %collective-permute-start.18 = (f32[2,6,64,128]{3,2,1,0:T(8,128)S(1)}, f32[2,6,64,128]{3,2,1,0:T(8,128)S(1)}, u32[]{:S(2)}, u32[]{:S(2)}) collective-permute-start(f32[2,6,64,128]{3,2,1,0:T(8,128)S(1)} %pad_maximum_fusion.2), channel_id=1, source_target_pairs={{0,1},{1,0},{2,3},{3,2},{4,5},{5,4},{6,7},{7,6},{8,9},{9,8},{10,11... | collective-permute-start | bytes 1179656 | tf_op jit(solution)/shard_map/ppermute | solution.py:16
  76.2 14.7 %collective-permute-start.3 = (f32[32,4224]{1,0:T(8,128)S(1)}, f32[32,4224]{1,0:T(8,128)S(1)}, u32[]{:S(2)}, u32[]{:S(2)}) collective-permute-start(f32[32,4224]{1,0:T(8,128)S(1)} %slice_bitcast_fusion.1), channel_id=1, source_target_pairs={{0,96},{32,0},{64,32},{96,64},{1,97},{33,1},{65,33},{97,65},{2,98}... | collective-permute-start | bytes 1622024 | tf_op jit(solution)/shard_map/ppermute | solution.py:21
  80.0 15.1 %collective-permute-start.4 = (f32[32,4224]{1,0:T(8,128)S(1)}, f32[32,4224]{1,0:T(8,128)S(1)}, u32[]{:S(2)}, u32[]{:S(2)}) collective-permute-start(f32[32,4224]{1,0:T(8,128)S(1)} %slice_bitcast_fusion), channel_id=1, source_target_pairs={{0,32},{32,64},{64,96},{96,0},{1,33},{33,65},{65,97},{97,1},{2,34}... | collective-permute-start | bytes 1622024 | tf_op jit(solution)/shard_map/ppermute | solution.py:21

commit v4 on v1

--- a/solution.py
+++ b/solution.py
@@ -1,6 +1,8 @@
 import jax
 import jax.numpy as jnp
 from jax import lax
+from jax.experimental import pallas as pl
+from jax.experimental.pallas import tpu as pltpu
 from jax.sharding import Mesh
 from jax.sharding import PartitionSpec as P
 
@@ -58,11 +60,51 @@
     return jnp.stack([mine, swap(mine, "core")])
 
 
+def product_kernel(index_ref, rows_ref, a_ref, table_ref, out_ref):
+    out_ref[...] = jnp.zeros_like(out_ref)
+    blocks = out_ref.shape[0]
+
+    def one_slot(g, carry):
+        row = rows_ref[g]
+
+        @pl.when(row < blocks)
+        def _():
+            term = jnp.dot(
+                a_ref[g],
+                table_ref[index_ref[g]],
+                precision=lax.Precision.HIGHEST,
+                preferred_element_type=jnp.float32,
+            )
+            out_ref[row] += term
+
+        return carry
+
+    lax.fori_loop(0, a_ref.shape[0], one_slot, 0)
+
+
+def product(index, rows, left, table):
+    slots, blk, _ = left.shape
+    columns = table.shape[2]
+    vmem = pl.BlockSpec(memory_space=pltpu.VMEM)
+    smem = pl.BlockSpec(memory_space=pltpu.SMEM)
+    return pl.pallas_call(
+        product_kernel,
+        out_shape=jax.ShapeDtypeStruct((MB, blk, columns), jnp.float32),
+        in_specs=[smem, smem, vmem, vmem],
+        out_specs=vmem,
+        compiler_params=pltpu.CompilerParams(vmem_limit_bytes=48 * 1024 * 1024),
+        cost_estimate=pl.CostEstimate(
+            flops=2 * slots * blk * blk * columns,
+            bytes_accessed=4 * (left.size + table.size + MB * blk * columns),
+            transcendentals=0,
+        ),
+    )(index, rows, left, table)
+
+
 def shards(a_blocks, a_rows, a_slots, b_stripes):
     n_z = lax.axis_size("z")
     z = lax.axis_index("z")
     columns = b_stripes.shape[2]
-    highest = lax.Precision.HIGHEST
 
     ints = jnp.stack([a_rows[0, 0], a_slots[0, 0]])
     ints_k, _ = gather_a(ints)
@@ -76,11 +118,8 @@
     core_rel = (slots // 6) % 2 ^ lax.axis_index("core")
     xh_rel = (slots // 12) ^ lax.axis_index("xh")
     index = ((core_rel * n_z + d) * 2 + xh_rel) * 6 + slots % 6
-    chosen = jnp.take(table, index.reshape(-1), axis=0)
     left = a_all.reshape(-1, BLK, BLK)
-    terms = jnp.einsum("gij,gjc->gic", left, chosen, precision=lax.Precision.HIGH)
-    place = (rows.reshape(-1)[:, None] == jnp.arange(MB, dtype=jnp.int32)[None, :]).astype(jnp.float32)
-    out = jnp.einsum("gm,gic->mic", place, terms, precision=highest)
+    out = product(index.reshape(-1), rows.reshape(-1), left, table)
     return out.reshape(MB * BLK, columns)
 
 

time: 133 us -> 138 us (1.038)
  the two profiles are of different devices: /device:TPU:2 before, /device:TPU:100 now
where the time goes in v4:
time: 138 us
  Pallas kernels  48.5 us (35%)
  waiting for transfers between devices  37 us (27%)
  starting transfers between devices  25.8 us (19%)
  local copies, waits for them, and re-layouts  16.4 us (12%)
  other arithmetic  10.2 us (7%)
    pallas_call x1, Pallas kernels, product(): pl.pallas_call(product_kernel, out_shape=jax.ShapeDtypeStruct((MB, blk, c...  48.5 us
    ppermute x16, waiting for transfers between devices, shift(): lax.ppermute(block, axis, [(i, (i + distance) % n) for i in range(n)])  37 us
    ppermute x16, starting transfers between devices, shift(): lax.ppermute(block, axis, [(i, (i + distance) % n) for i in range(n)])  22.6 us
    reshape x1, local copies, waits for them, and re-layouts, shards(): left = a_all.reshape(-1, BLK, BLK)  7.88 us
    unnamed x14, local copies, waits for them, and re-layouts  6.88 us
    another operation x1, other arithmetic, gather_b(): return jnp.stack([mine, swap(mine, 'core')])  5.43 us
    ppermute x4, starting transfers between devices, swap(): return lax.ppermute(block, axis, [(0, 1), (1, 0)])  3.23 us
  transfers between devices with their start and end apart: 20, of which 9 were waited for; matrix products, arithmetic and copies ran while one was open for 15% of the time, Pallas kernels for 0%

profile of v4, /device:TPU:100, one launch (start us, length us, event | category | flops | bytes accessed | tf_op | source)
XLA Modules:
  0.0 138.1 jit_solution(8657485192651100929)
XLA Ops:
  0.7 1.2 collective-permute-start
  2.7 1.1 collective-permute-start.5
  4.5 1.9 %constant_dynamic-update-slice_fusion.9 = f32[8,32,4096]{2,1,0:T(8,128)} fusion(f32[1,1,32,4096]{3,2,1,0:T(8,128)} %param.4), kind=kLoop, calls=%fused_computation.27 | loop fusion | bytes 1048576
  6.7 3.1 %collective-permute-start.2 = (s32[2,2,32]{2,1,0:T(2,128)S(1)}, s32[2,2,32]{2,1,0:T(2,128)S(1)}, u32[]{:S(2)}, u32[]{:S(2)}) collective-permute-start(s32[2,2,32]{2,1,0:T(2,128)S(1)} %pad_add_fusion), channel_id=1, source_target_pairs={{0,96},{32,0},{64,32},{96,64},{1,97},{33,1},{65,33},{97,65},{2,98}... | collective-permute-start | bytes 1544 | tf_op jit(solution)/shard_map/ppermute | solution.py:23
  9.8 1.3 collective-permute-done.2
  11.1 3.5 %collective-permute-start.3 = (s32[2,32]{1,0:T(2,128)S(1)}, s32[2,32]{1,0:T(2,128)S(1)}, u32[]{:S(2)}, u32[]{:S(2)}) collective-permute-start(s32[2,32]{1,0:T(2,128)S(1)} %slice_bitcast_fusion.5), channel_id=1, source_target_pairs={{0,96},{32,0},{64,32},{96,64},{1,97},{33,1},{65,33},{97,65},{2,98}... | collective-permute-start | bytes 776 | tf_op jit(solution)/shard_map/ppermute | solution.py:23
  14.6 1.3 collective-permute-done.3
  15.9 3.5 %collective-permute-done.4 = s32[2,32]{1,0:T(2,128)S(1)} collective-permute-done((s32[2,32]{1,0:T(2,128)S(1)}, s32[2,32]{1,0:T(2,128)S(1)}, u32[]{:S(2)}, u32[]{:S(2)}) %collective-permute-start.4) | collective-permute-done | bytes 288 | tf_op jit(solution)/shard_map/ppermute | solution.py:23
  21.1 3.1 %collective-permute-start.15 = (f32[2,6,64,128]{3,2,1,0:T(8,128)S(1)}, f32[2,6,64,128]{3,2,1,0:T(8,128)S(1)}, u32[]{:S(2)}, u32[]{:S(2)}) collective-permute-start(f32[2,6,64,128]{3,2,1,0:T(8,128)S(1)} %pad_maximum_fusion.2), channel_id=1, source_target_pairs={{0,4},{4,8},{8,12},{12,16},{16,20},{20,24},{24,28},{28,0},{1,5},{5... | collective-permute-start | bytes 1179656 | tf_op jit(solution)/shard_map/ppermute | solution.py:23
  25.2 1.3 pad_maximum_fusion.1
  26.6 2.0 %collective-permute-start.6 = (f32[2,32,4096]{2,1,0:T(8,128)S(1)}, f32[2,32,4096]{2,1,0:T(8,128)S(1)}, u32[]{:S(2)}, u32[]{:S(2)}) collective-permute-start(f32[2,32,4096]{2,1,0:T(8,128)S(1)} %pad_maximum_fusion.1), channel_id=1, source_target_pairs={{0,32},{32,64},{64,96},{96,0},{1,33},{33,65},{65,97},{97,1},{2,34}... | collective-permute-start | bytes 3145736 | tf_op jit(solution)/shard_map/ppermute | solution.py:23
  28.6 2.0 %collective-permute-done.11 = f32[2,6,64,128]{3,2,1,0:T(8,128)S(1)} collective-permute-done((f32[2,6,64,128]{3,2,1,0:T(8,128)S(1)}, f32[2,6,64,128]{3,2,1,0:T(8,128)S(1)}, u32[]{:S(2)}, u32[]{:S(2)}) %collective-permute-start.11) | collective-permute-done | bytes 393248 | tf_op jit(solution)/shard_map/ppermute | solution.py:23
  30.6 3.4 %collective-permute-start.16 = (f32[2,6,64,128]{3,2,1,0:T(8,128)S(1)}, f32[2,6,64,128]{3,2,1,0:T(8,128)S(1)}, u32[]{:S(2)}, u32[]{:S(2)}) collective-permute-start(f32[2,6,64,128]{3,2,1,0:T(8,128)S(1)} %collective-permute-done.15), channel_id=1, source_target_pairs={{0,4},{4,8},{8,12},{12,16},{16,20},{20,24},{24,28},{28,0},{1,5},{5... | collective-permute-start | bytes 1179656 | tf_op jit(solution)/shard_map/ppermute | solution.py:23
  34.1 1.9 %constant_dynamic-update-slice_fusion.8 = f32[8,32,4096]{2,1,0:T(8,128)} fusion(f32[8,32,4096]{2,1,0:T(8,128)} %constant_dynamic-update-slice_fusion.9, f32[32,4096]{1,0:T(8,128)} %collective-permute-done.5), kind=kLoop, calls=%fused_computation.26 | loop fusion | bytes 1048576
  36.0 5.3 %collective-permute-done.12 = f32[2,6,64,128]{3,2,1,0:T(8,128)S(1)} collective-permute-done((f32[2,6,64,128]{3,2,1,0:T(8,128)S(1)}, f32[2,6,64,128]{3,2,1,0:T(8,128)S(1)}, u32[]{:S(2)}, u32[]{:S(2)}) %collective-permute-start.12) | collective-permute-done | bytes 393248 | tf_op jit(solution)/shard_map/ppermute | solution.py:23
  41.3 3.4 %collective-permute-start.17 = (f32[2,6,64,128]{3,2,1,0:T(8,128)S(1)}, f32[2,6,64,128]{3,2,1,0:T(8,128)S(1)}, u32[]{:S(2)}, u32[]{:S(2)}) collective-permute-start(f32[2,6,64,128]{3,2,1,0:T(8,128)S(1)} %collective-permute-done.16), channel_id=1, source_target_pairs={{0,4},{4,8},{8,12},{12,16},{16,20},{20,24},{24,28},{28,0},{1,5},{5... | collective-permute-start | bytes 1179656 | tf_op jit(solution)/shard_map/ppermute | solution.py:23
  44.7 7.7 %collective-permute-done.13 = f32[2,6,64,128]{3,2,1,0:T(8,128)S(1)} collective-permute-done((f32[2,6,64,128]{3,2,1,0:T(8,128)S(1)}, f32[2,6,64,128]{3,2,1,0:T(8,128)S(1)}, u32[]{:S(2)}, u32[]{:S(2)}) %collective-permute-start.13) | collective-permute-done | bytes 393248 | tf_op jit(solution)/shard_map/ppermute | solution.py:23
  52.7 3.3 %collective-permute-start.18 = (f32[6,64,128]{2,1,0:T(8,128)S(1)}, f32[6,64,128]{2,1,0:T(8,128)S(1)}, u32[]{:S(2)}, u32[]{:S(2)}) collective-permute-start(f32[6,64,128]{2,1,0:T(8,128)S(1)} %slice_bitcast_fusion.2), channel_id=1, source_target_pairs={{0,4},{4,8},{8,12},{12,16},{16,20},{20,24},{24,28},{28,0},{1,5},{5... | collective-permute-start | bytes 589832 | tf_op jit(solution)/shard_map/ppermute | solution.py:23
  56.2 3.4 %collective-permute-done.14 = f32[6,64,128]{2,1,0:T(8,128)S(1)} collective-permute-done((f32[6,64,128]{2,1,0:T(8,128)S(1)}, f32[6,64,128]{2,1,0:T(8,128)S(1)}, u32[]{:S(2)}, u32[]{:S(2)}) %collective-permute-start.14) | collective-permute-done | bytes 196640 | tf_op jit(solution)/shard_map/ppermute | solution.py:23
  62.1 3.3 %collective-permute-done.8 = f32[32,4096]{1,0:T(8,128)S(1)} collective-permute-done((f32[32,4096]{1,0:T(8,128)S(1)}, f32[32,4096]{1,0:T(8,128)S(1)}, u32[]{:S(2)}, u32[]{:S(2)}) %collective-permute-start.8) | collective-permute-done | bytes 524320 | tf_op jit(solution)/shard_map/ppermute | solution.py:23
  66.2 9.3 %collective-permute-done.9 = f32[32,4096]{1,0:T(8,128)S(1)} collective-permute-done((f32[32,4096]{1,0:T(8,128)S(1)}, f32[32,4096]{1,0:T(8,128)S(1)}, u32[]{:S(2)}, u32[]{:S(2)}) %collective-permute-start.9) | collective-permute-done | bytes 524320 | tf_op jit(solution)/shard_map/ppermute | solution.py:23
  76.3 7.9 %reshape.108.a_ref = f32[256,64,64]{2,1,0:T(8,128)} reshape(f32[8,32,4096]{2,1,0:T(8,128)} %bitcast_dynamic-update-slice_fusion) | data formatting | bytes 8388608 | tf_op jit(solution)/shard_map/reshape | solution.py:121
  84.2 5.4 %pad_maximum_fusion = f32[2,8,2,6,64,128]{5,4,3,2,1,0:T(8,128)} fusion(f32[1,8,2,6,64,128]{5,4,3,2,1,0:T(8,128)} %bitcast.38, f32[1,8,2,6,64,128]{5,4,3,2,1,0:T(8,128)S(1)} %bitcast.67), kind=kLoop, calls=%fused_computation | loop fusion | flops 1572864 | bytes 12582912 | tf_op jit(solution)/shard_map/stack | solution.py:60
  89.6 48.5 %shard_map.46 = f32[32,64,128]{2,1,0:T(8,128)} custom-call(s32[256]{0:T(256)S(1)} %fusion.6.index_ref, s32[256]{0:T(256)S(1)} %reshape_squeeze.3.rows_ref, f32[256,64,64]{2,1,0:T(8,128)} %reshape.108.a_ref, f32[192,64,128]{2,1,0:T(8,128)} %bitcast.66), custom_call_target="tpu_custom_call" | custom-call | flops 268435456 | bytes 11534336 | tf_op jit(solution)/shard_map/pallas_call | solution.py:90
  (62 shorter events, 9.8 us)
Async XLA Ops:
  0.7 6.0 %collective-permute-start = (s32[2,32]{1,0:T(2,128)S(1)}, s32[2,32]{1,0:T(2,128)S(1)}, u32[]{:S(2)}, u32[]{:S(2)}) collective-permute-start(s32[2,32]{1,0:T(2,128)S(1)} %get-tuple-element.12), channel_id=1, source_target_pairs={{0,128},{128,0},{1,129},{129,1},{2,130},{130,2},{3,131},{131,3},{4... | collective-permute-start | bytes 776 | tf_op jit(solution)/shard_map/ppermute | solution.py:18
  1.9 18.1 %collective-permute-start.10 = (f32[6,64,128]{2,1,0:T(8,128)}, f32[6,64,128]{2,1,0:T(8,128)S(1)}, u32[]{:S(2)}, u32[]{:S(2)}) collective-permute-start(f32[6,64,128]{2,1,0:T(8,128)} %param.7), channel_id=1, source_target_pairs={{0,2},{2,0},{1,3},{3,1},{4,6},{6,4},{5,7},{7,5},{8,10},{10,8},{9,1... | collective-permute-start | bytes 589832 | tf_op jit(solution)/shard_map/ppermute | solution.py:18
  2.7 22.6 %collective-permute-start.5 = (f32[32,4096]{1,0:T(8,128)}, f32[32,4096]{1,0:T(8,128)}, u32[]{:S(2)}, u32[]{:S(2)}) collective-permute-start(f32[32,4096]{1,0:T(8,128)} %bitcast.68), channel_id=1, source_target_pairs={{0,128},{128,0},{1,129},{129,1},{2,130},{130,2},{3,131},{131,3},{4... | collective-permute-start | bytes 1572872 | tf_op jit(solution)/shard_map/ppermute | solution.py:18
  6.7 4.4 %collective-permute-start.2 = (s32[2,2,32]{2,1,0:T(2,128)S(1)}, s32[2,2,32]{2,1,0:T(2,128)S(1)}, u32[]{:S(2)}, u32[]{:S(2)}) collective-permute-start(s32[2,2,32]{2,1,0:T(2,128)S(1)} %pad_add_fusion), channel_id=1, source_target_pairs={{0,96},{32,0},{64,32},{96,64},{1,97},{33,1},{65,33},{97,65},{2,98}... | collective-permute-start | bytes 1544 | tf_op jit(solution)/shard_map/ppermute | solution.py:23
  9.8 4.8 %collective-permute-start.1 = (s32[2,2,32]{2,1,0:T(2,128)S(1)}, s32[2,2,32]{2,1,0:T(2,128)S(1)}, u32[]{:S(2)}, u32[]{:S(2)}) collective-permute-start(s32[2,2,32]{2,1,0:T(2,128)S(1)} %pad_add_fusion), channel_id=1, source_target_pairs={{0,32},{32,64},{64,96},{96,0},{1,33},{33,65},{65,97},{97,1},{2,34}... | collective-permute-start | bytes 1544 | tf_op jit(solution)/shard_map/ppermute | solution.py:23
  11.1 4.8 %collective-permute-start.3 = (s32[2,32]{1,0:T(2,128)S(1)}, s32[2,32]{1,0:T(2,128)S(1)}, u32[]{:S(2)}, u32[]{:S(2)}) collective-permute-start(s32[2,32]{1,0:T(2,128)S(1)} %slice_bitcast_fusion.5), channel_id=1, source_target_pairs={{0,96},{32,0},{64,32},{96,64},{1,97},{33,1},{65,33},{97,65},{2,98}... | collective-permute-start | bytes 776 | tf_op jit(solution)/shard_map/ppermute | solution.py:23
  14.6 4.8 %collective-permute-start.4 = (s32[2,32]{1,0:T(2,128)S(1)}, s32[2,32]{1,0:T(2,128)S(1)}, u32[]{:S(2)}, u32[]{:S(2)}) collective-permute-start(s32[2,32]{1,0:T(2,128)S(1)} %slice_bitcast_fusion.4), channel_id=1, source_target_pairs={{0,32},{32,64},{64,96},{96,0},{1,33},{33,65},{65,97},{97,1},{2,34}... | collective-permute-start | bytes 776 | tf_op jit(solution)/shard_map/ppermute | solution.py:23
  21.0 9.7 %collective-permute-start.11 = (f32[2,6,64,128]{3,2,1,0:T(8,128)S(1)}, f32[2,6,64,128]{3,2,1,0:T(8,128)S(1)}, u32[]{:S(2)}, u32[]{:S(2)}) collective-permute-start(f32[2,6,64,128]{3,2,1,0:T(8,128)S(1)} %pad_maximum_fusion.2), channel_id=1, source_target_pairs={{0,28},{4,0},{8,4},{12,8},{16,12},{20,16},{24,20},{28,24},{1,29},{... | collective-permute-start | bytes 1179656 | tf_op jit(solution)/shard_map/ppermute | solution.py:23
  21.1 9.5 %collective-permute-start.15 = (f32[2,6,64,128]{3,2,1,0:T(8,128)S(1)}, f32[2,6,64,128]{3,2,1,0:T(8,128)S(1)}, u32[]{:S(2)}, u32[]{:S(2)}) collective-permute-start(f32[2,6,64,128]{3,2,1,0:T(8,128)S(1)} %pad_maximum_fusion.2), channel_id=1, source_target_pairs={{0,4},{4,8},{8,12},{12,16},{16,20},{20,24},{24,28},{28,0},{1,5},{5... | collective-permute-start | bytes 1179656 | tf_op jit(solution)/shard_map/ppermute | solution.py:23
  26.5 29.6 %collective-permute-start.7 = (f32[2,32,4096]{2,1,0:T(8,128)S(1)}, f32[2,32,4096]{2,1,0:T(8,128)S(1)}, u32[]{:S(2)}, u32[]{:S(2)}) collective-permute-start(f32[2,32,4096]{2,1,0:T(8,128)S(1)} %pad_maximum_fusion.1), channel_id=1, source_target_pairs={{0,96},{32,0},{64,32},{96,64},{1,97},{33,1},{65,33},{97,65},{2,98}... | collective-permute-start | bytes 3145736 | tf_op jit(solution)/shard_map/ppermute | solution.py:23
  26.6 33.2 %collective-permute-start.6 = (f32[2,32,4096]{2,1,0:T(8,128)S(1)}, f32[2,32,4096]{2,1,0:T(8,128)S(1)}, u32[]{:S(2)}, u32[]{:S(2)}) collective-permute-start(f32[2,32,4096]{2,1,0:T(8,128)S(1)} %pad_maximum_fusion.1), channel_id=1, source_target_pairs={{0,32},{32,64},{64,96},{96,0},{1,33},{33,65},{65,97},{97,1},{2,34}... | collective-permute-start | bytes 3145736 | tf_op jit(solution)/shard_map/ppermute | solution.py:23
  30.6 10.6 %collective-permute-start.12 = (f32[2,6,64,128]{3,2,1,0:T(8,128)S(1)}, f32[2,6,64,128]{3,2,1,0:T(8,128)S(1)}, u32[]{:S(2)}, u32[]{:S(2)}) collective-permute-start(f32[2,6,64,128]{3,2,1,0:T(8,128)S(1)} %collective-permute-done.11), channel_id=1, source_target_pairs={{0,28},{4,0},{8,4},{12,8},{16,12},{20,16},{24,20},{28,24},{1,29},{... | collective-permute-start | bytes 1179656 | tf_op jit(solution)/shard_map/ppermute | solution.py:23
  30.6 10.6 %collective-permute-start.16 = (f32[2,6,64,128]{3,2,1,0:T(8,128)S(1)}, f32[2,6,64,128]{3,2,1,0:T(8,128)S(1)}, u32[]{:S(2)}, u32[]{:S(2)}) collective-permute-start(f32[2,6,64,128]{3,2,1,0:T(8,128)S(1)} %collective-permute-done.15), channel_id=1, source_target_pairs={{0,4},{4,8},{8,12},{12,16},{16,20},{20,24},{24,28},{28,0},{1,5},{5... | collective-permute-start | bytes 1179656 | tf_op jit(solution)/shard_map/ppermute | solution.py:23
  41.2 11.2 %collective-permute-start.13 = (f32[2,6,64,128]{3,2,1,0:T(8,128)S(1)}, f32[2,6,64,128]{3,2,1,0:T(8,128)S(1)}, u32[]{:S(2)}, u32[]{:S(2)}) collective-permute-start(f32[2,6,64,128]{3,2,1,0:T(8,128)S(1)} %collective-permute-done.12), channel_id=1, source_target_pairs={{0,28},{4,0},{8,4},{12,8},{16,12},{20,16},{24,20},{28,24},{1,29},{... | collective-permute-start | bytes 1179656 | tf_op jit(solution)/shard_map/ppermute | solution.py:23
  41.3 11.4 %collective-permute-start.17 = (f32[2,6,64,128]{3,2,1,0:T(8,128)S(1)}, f32[2,6,64,128]{3,2,1,0:T(8,128)S(1)}, u32[]{:S(2)}, u32[]{:S(2)}) collective-permute-start(f32[2,6,64,128]{3,2,1,0:T(8,128)S(1)} %collective-permute-done.16), channel_id=1, source_target_pairs={{0,4},{4,8},{8,12},{12,16},{16,20},{20,24},{24,28},{28,0},{1,5},{5... | collective-permute-start | bytes 1179656 | tf_op jit(solution)/shard_map/ppermute | solution.py:23
  52.4 7.1 %collective-permute-start.14 = (f32[6,64,128]{2,1,0:T(8,128)S(1)}, f32[6,64,128]{2,1,0:T(8,128)S(1)}, u32[]{:S(2)}, u32[]{:S(2)}) collective-permute-start(f32[6,64,128]{2,1,0:T(8,128)S(1)} %slice_bitcast_fusion.3), channel_id=1, source_target_pairs={{0,28},{4,0},{8,4},{12,8},{16,12},{20,16},{24,20},{28,24},{1,29},{... | collective-permute-start | bytes 589832 | tf_op jit(solution)/shard_map/ppermute | solution.py:23
  52.7 6.8 %collective-permute-start.18 = (f32[6,64,128]{2,1,0:T(8,128)S(1)}, f32[6,64,128]{2,1,0:T(8,128)S(1)}, u32[]{:S(2)}, u32[]{:S(2)}) collective-permute-start(f32[6,64,128]{2,1,0:T(8,128)S(1)} %slice_bitcast_fusion.2), channel_id=1, source_target_pairs={{0,4},{4,8},{8,12},{12,16},{16,20},{20,24},{24,28},{28,0},{1,5},{5... | collective-permute-start | bytes 589832 | tf_op jit(solution)/shard_map/ppermute | solution.py:23
  56.1 9.3 %collective-permute-start.8 = (f32[32,4096]{1,0:T(8,128)S(1)}, f32[32,4096]{1,0:T(8,128)S(1)}, u32[]{:S(2)}, u32[]{:S(2)}) collective-permute-start(f32[32,4096]{1,0:T(8,128)S(1)} %slice_bitcast_fusion.1), channel_id=1, source_target_pairs={{0,96},{32,0},{64,32},{96,64},{1,97},{33,1},{65,33},{97,65},{2,98}... | collective-permute-start | bytes 1572872 | tf_op jit(solution)/shard_map/ppermute | solution.py:23
  59.7 24.5 %collective-permute-start.19 = (f32[8,2,6,64,128]{4,3,2,1,0:T(8,128)S(1)}, f32[8,2,6,64,128]{4,3,2,1,0:T(8,128)}, u32[]{:S(2)}, u32[]{:S(2)}) collective-permute-start(f32[8,2,6,64,128]{4,3,2,1,0:T(8,128)S(1)} %bitcast_dynamic-update-slice_fusion.2), channel_id=1, source_target_pairs={{0,1},{1,0},{2,3},{3,2},{4,5},{5,4},{6,7},{7,6},{8,9},{9,8},{10,11... | collective-permute-start | bytes 9437192 | tf_op jit(solution)/shard_map/ppermute | solution.py:18
  59.9 15.6 %collective-permute-start.9 = (f32[32,4096]{1,0:T(8,128)S(1)}, f32[32,4096]{1,0:T(8,128)S(1)}, u32[]{:S(2)}, u32[]{:S(2)}) collective-permute-start(f32[32,4096]{1,0:T(8,128)S(1)} %slice_bitcast_fusion), channel_id=1, source_target_pairs={{0,32},{32,64},{64,96},{96,0},{1,33},{33,65},{65,97},{97,1},{2,34}... | collective-permute-start | bytes 1572872 | tf_op jit(solution)/shard_map/ppermute | solution.py:23

commit v5 on v4

--- a/solution.py
+++ b/solution.py
@@ -60,26 +60,26 @@
     return jnp.stack([mine, swap(mine, "core")])
 
 
-def product_kernel(index_ref, rows_ref, a_ref, table_ref, out_ref):
-    out_ref[...] = jnp.zeros_like(out_ref)
+def product_kernel(index_ref, rows_ref, a_ref, table_ref, out_ref, acc_ref):
+    acc_ref[...] = jnp.zeros_like(acc_ref)
     blocks = out_ref.shape[0]
 
     def one_slot(g, carry):
-        row = rows_ref[g]
-
-        @pl.when(row < blocks)
-        def _():
-            term = jnp.dot(
-                a_ref[g],
-                table_ref[index_ref[g]],
-                precision=lax.Precision.HIGHEST,
-                preferred_element_type=jnp.float32,
-            )
-            out_ref[row] += term
-
+        row = jnp.minimum(rows_ref[g], blocks)
+        left = a_ref[g]
+        right = table_ref[index_ref[g]]
+        left_hi = left.astype(jnp.bfloat16)
+        left_lo = (left - left_hi.astype(jnp.float32)).astype(jnp.bfloat16)
+        right_hi = right.astype(jnp.bfloat16)
+        right_lo = (right - right_hi.astype(jnp.float32)).astype(jnp.bfloat16)
+        term = jnp.dot(left_hi, right_hi, preferred_element_type=jnp.float32)
+        term += jnp.dot(left_hi, right_lo, preferred_element_type=jnp.float32)
+        term += jnp.dot(left_lo, right_hi, preferred_element_type=jnp.float32)
+        acc_ref[row] += term
         return carry
 
-    lax.fori_loop(0, a_ref.shape[0], one_slot, 0)
+    lax.fori_loop(0, a_ref.shape[0], one_slot, 0, unroll=8)
+    out_ref[...] = acc_ref[:blocks]
 
 
 def product(index, rows, left, table):
@@ -92,6 +92,7 @@
         out_shape=jax.ShapeDtypeStruct((MB, blk, columns), jnp.float32),
         in_specs=[smem, smem, vmem, vmem],
         out_specs=vmem,
+        scratch_shapes=[pltpu.VMEM((MB + 1, blk, columns), jnp.float32)],
         compiler_params=pltpu.CompilerParams(vmem_limit_bytes=48 * 1024 * 1024),
         cost_estimate=pl.CostEstimate(
             flops=2 * slots * blk * blk * columns,

time: 138 us -> 113 us (0.82)
  the two profiles are of different devices: /device:TPU:100 before, /device:TPU:2 now
where the time goes in v5:
time: 113 us
  waiting for transfers between devices  40 us (35%)
  starting transfers between devices  31 us (27%)
  local copies, waits for them, and re-layouts  16.4 us (15%)
  Pallas kernels  14.8 us (13%)
  other arithmetic  10.2 us (9%)
    ppermute x16, waiting for transfers between devices, shift(): lax.ppermute(block, axis, [(i, (i + distance) % n) for i in range(n)])  40 us
    ppermute x16, starting transfers between devices, shift(): lax.ppermute(block, axis, [(i, (i + distance) % n) for i in range(n)])  26.2 us
    pallas_call x1, Pallas kernels, product(): pl.pallas_call(product_kernel, out_shape=jax.ShapeDtypeStruct((MB, blk, c...  14.8 us
    reshape x1, local copies, waits for them, and re-layouts, shards(): left = a_all.reshape(-1, BLK, BLK)  7.88 us
    unnamed x14, local copies, waits for them, and re-layouts  6.88 us
    another operation x1, other arithmetic, gather_b(): return jnp.stack([mine, swap(mine, 'core')])  5.43 us
    ppermute x4, starting transfers between devices, swap(): return lax.ppermute(block, axis, [(0, 1), (1, 0)])  4.85 us
  transfers between devices with their start and end apart: 20, of which 12 were waited for; matrix products, arithmetic and copies ran while one was open for 18% of the time, Pallas kernels for 0%

profile of v5, /device:TPU:2, one launch (start us, length us, event | category | flops | bytes accessed | tf_op | source)
XLA Modules:
  0.0 112.6 jit_solution(11558992544806060579)
XLA Ops:
  0.7 2.2 %collective-permute-start = (s32[2,32]{1,0:T(2,128)S(1)}, s32[2,32]{1,0:T(2,128)S(1)}, u32[]{:S(2)}, u32[]{:S(2)}) collective-permute-start(s32[2,32]{1,0:T(2,128)S(1)} %get-tuple-element.12), channel_id=1, source_target_pairs={{0,128},{128,0},{1,129},{129,1},{2,130},{130,2},{3,131},{131,3},{4... | collective-permute-start | bytes 776 | tf_op jit(solution)/shard_map/ppermute | solution.py:18
  3.6 1.8 %collective-permute-start.5 = (f32[32,4096]{1,0:T(8,128)}, f32[32,4096]{1,0:T(8,128)}, u32[]{:S(2)}, u32[]{:S(2)}) collective-permute-start(f32[32,4096]{1,0:T(8,128)} %bitcast.68), channel_id=1, source_target_pairs={{0,128},{128,0},{1,129},{129,1},{2,130},{130,2},{3,131},{131,3},{4... | collective-permute-start | bytes 1572872 | tf_op jit(solution)/shard_map/ppermute | solution.py:18
  6.1 1.9 %constant_dynamic-update-slice_fusion.9 = f32[8,32,4096]{2,1,0:T(8,128)} fusion(f32[1,1,32,4096]{3,2,1,0:T(8,128)} %param.4), kind=kLoop, calls=%fused_computation.27 | loop fusion | bytes 1048576
  8.3 3.1 %collective-permute-start.2 = (s32[2,2,32]{2,1,0:T(2,128)S(1)}, s32[2,2,32]{2,1,0:T(2,128)S(1)}, u32[]{:S(2)}, u32[]{:S(2)}) collective-permute-start(s32[2,2,32]{2,1,0:T(2,128)S(1)} %pad_add_fusion), channel_id=1, source_target_pairs={{0,96},{32,0},{64,32},{96,64},{1,97},{33,1},{65,33},{97,65},{2,98}... | collective-permute-start | bytes 1544 | tf_op jit(solution)/shard_map/ppermute | solution.py:23
  11.4 1.3 %collective-permute-done.2 = s32[2,2,32]{2,1,0:T(2,128)S(1)} collective-permute-done((s32[2,2,32]{2,1,0:T(2,128)S(1)}, s32[2,2,32]{2,1,0:T(2,128)S(1)}, u32[]{:S(2)}, u32[]{:S(2)}) %collective-permute-start.2) | collective-permute-done | bytes 544 | tf_op jit(solution)/shard_map/ppermute | solution.py:23
  12.7 3.5 %collective-permute-start.3 = (s32[2,32]{1,0:T(2,128)S(1)}, s32[2,32]{1,0:T(2,128)S(1)}, u32[]{:S(2)}, u32[]{:S(2)}) collective-permute-start(s32[2,32]{1,0:T(2,128)S(1)} %slice_bitcast_fusion.5), channel_id=1, source_target_pairs={{0,96},{32,0},{64,32},{96,64},{1,97},{33,1},{65,33},{97,65},{2,98}... | collective-permute-start | bytes 776 | tf_op jit(solution)/shard_map/ppermute | solution.py:23
  16.2 1.3 %collective-permute-done.3 = s32[2,32]{1,0:T(2,128)S(1)} collective-permute-done((s32[2,32]{1,0:T(2,128)S(1)}, s32[2,32]{1,0:T(2,128)S(1)}, u32[]{:S(2)}, u32[]{:S(2)}) %collective-permute-start.3) | collective-permute-done | bytes 288 | tf_op jit(solution)/shard_map/ppermute | solution.py:23
  17.5 3.5 %collective-permute-done.4 = s32[2,32]{1,0:T(2,128)S(1)} collective-permute-done((s32[2,32]{1,0:T(2,128)S(1)}, s32[2,32]{1,0:T(2,128)S(1)}, u32[]{:S(2)}, u32[]{:S(2)}) %collective-permute-start.4) | collective-permute-done | bytes 288 | tf_op jit(solution)/shard_map/ppermute | solution.py:23
  22.6 5.9 %collective-permute-start.11 = (f32[2,6,64,128]{3,2,1,0:T(8,128)S(1)}, f32[2,6,64,128]{3,2,1,0:T(8,128)S(1)}, u32[]{:S(2)}, u32[]{:S(2)}) collective-permute-start(f32[2,6,64,128]{3,2,1,0:T(8,128)S(1)} %pad_maximum_fusion.2), channel_id=1, source_target_pairs={{0,28},{4,0},{8,4},{12,8},{16,12},{20,16},{24,20},{28,24},{1,29},{... | collective-permute-start | bytes 1179656 | tf_op jit(solution)/shard_map/ppermute | solution.py:23
  29.5 1.3 %pad_maximum_fusion.1 = f32[2,32,4096]{2,1,0:T(8,128)S(1)} fusion(f32[1,32,4096]{2,1,0:T(8,128)} %bitcast.18, f32[1,32,4096]{2,1,0:T(8,128)} %bitcast.69), kind=kLoop, calls=%fused_computation.1 | loop fusion | flops 262144 | bytes 2097152 | tf_op jit(solution)/shard_map/stack | solution.py:31
  30.9 2.0 %collective-permute-start.6 = (f32[2,32,4096]{2,1,0:T(8,128)S(1)}, f32[2,32,4096]{2,1,0:T(8,128)S(1)}, u32[]{:S(2)}, u32[]{:S(2)}) collective-permute-start(f32[2,32,4096]{2,1,0:T(8,128)S(1)} %pad_maximum_fusion.1), channel_id=1, source_target_pairs={{0,32},{32,64},{64,96},{96,0},{1,33},{33,65},{65,97},{97,1},{2,34}... | collective-permute-start | bytes 3145736 | tf_op jit(solution)/shard_map/ppermute | solution.py:23
  32.9 1.9 %collective-permute-done.11 = f32[2,6,64,128]{3,2,1,0:T(8,128)S(1)} collective-permute-done((f32[2,6,64,128]{3,2,1,0:T(8,128)S(1)}, f32[2,6,64,128]{3,2,1,0:T(8,128)S(1)}, u32[]{:S(2)}, u32[]{:S(2)}) %collective-permute-start.11) | collective-permute-done | bytes 393248 | tf_op jit(solution)/shard_map/ppermute | solution.py:23
  34.7 3.7 %collective-permute-start.12 = (f32[2,6,64,128]{3,2,1,0:T(8,128)S(1)}, f32[2,6,64,128]{3,2,1,0:T(8,128)S(1)}, u32[]{:S(2)}, u32[]{:S(2)}) collective-permute-start(f32[2,6,64,128]{3,2,1,0:T(8,128)S(1)} %collective-permute-done.11), channel_id=1, source_target_pairs={{0,28},{4,0},{8,4},{12,8},{16,12},{20,16},{24,20},{28,24},{1,29},{... | collective-permute-start | bytes 1179656 | tf_op jit(solution)/shard_map/ppermute | solution.py:23
  38.7 1.9 %constant_dynamic-update-slice_fusion.8 = f32[8,32,4096]{2,1,0:T(8,128)} fusion(f32[8,32,4096]{2,1,0:T(8,128)} %constant_dynamic-update-slice_fusion.9, f32[32,4096]{1,0:T(8,128)} %collective-permute-done.5), kind=kLoop, calls=%fused_computation.26 | loop fusion | bytes 1048576
  40.6 4.9 %collective-permute-done.12 = f32[2,6,64,128]{3,2,1,0:T(8,128)S(1)} collective-permute-done((f32[2,6,64,128]{3,2,1,0:T(8,128)S(1)}, f32[2,6,64,128]{3,2,1,0:T(8,128)S(1)}, u32[]{:S(2)}, u32[]{:S(2)}) %collective-permute-start.12) | collective-permute-done | bytes 393248 | tf_op jit(solution)/shard_map/ppermute | solution.py:23
  45.5 3.7 %collective-permute-start.13 = (f32[2,6,64,128]{3,2,1,0:T(8,128)S(1)}, f32[2,6,64,128]{3,2,1,0:T(8,128)S(1)}, u32[]{:S(2)}, u32[]{:S(2)}) collective-permute-start(f32[2,6,64,128]{3,2,1,0:T(8,128)S(1)} %collective-permute-done.12), channel_id=1, source_target_pairs={{0,28},{4,0},{8,4},{12,8},{16,12},{20,16},{24,20},{28,24},{1,29},{... | collective-permute-start | bytes 1179656 | tf_op jit(solution)/shard_map/ppermute | solution.py:23
  49.8 6.8 %collective-permute-done.13 = f32[2,6,64,128]{3,2,1,0:T(8,128)S(1)} collective-permute-done((f32[2,6,64,128]{3,2,1,0:T(8,128)S(1)}, f32[2,6,64,128]{3,2,1,0:T(8,128)S(1)}, u32[]{:S(2)}, u32[]{:S(2)}) %collective-permute-start.13) | collective-permute-done | bytes 393248 | tf_op jit(solution)/shard_map/ppermute | solution.py:23
  56.6 3.9 %collective-permute-start.14 = (f32[6,64,128]{2,1,0:T(8,128)S(1)}, f32[6,64,128]{2,1,0:T(8,128)S(1)}, u32[]{:S(2)}, u32[]{:S(2)}) collective-permute-start(f32[6,64,128]{2,1,0:T(8,128)S(1)} %slice_bitcast_fusion.3), channel_id=1, source_target_pairs={{0,28},{4,0},{8,4},{12,8},{16,12},{20,16},{24,20},{28,24},{1,29},{... | collective-permute-start | bytes 589832 | tf_op jit(solution)/shard_map/ppermute | solution.py:23
  61.1 2.6 %collective-permute-done.14 = f32[6,64,128]{2,1,0:T(8,128)S(1)} collective-permute-done((f32[6,64,128]{2,1,0:T(8,128)S(1)}, f32[6,64,128]{2,1,0:T(8,128)S(1)}, u32[]{:S(2)}, u32[]{:S(2)}) %collective-permute-start.14) | collective-permute-done | bytes 196640 | tf_op jit(solution)/shard_map/ppermute | solution.py:23
  63.7 4.1 %collective-permute-done.18 = f32[6,64,128]{2,1,0:T(8,128)S(1)} collective-permute-done((f32[6,64,128]{2,1,0:T(8,128)S(1)}, f32[6,64,128]{2,1,0:T(8,128)S(1)}, u32[]{:S(2)}, u32[]{:S(2)}) %collective-permute-start.18) | collective-permute-done | bytes 196640 | tf_op jit(solution)/shard_map/ppermute | solution.py:23
  71.1 12.6 %collective-permute-done.9 = f32[32,4096]{1,0:T(8,128)S(1)} collective-permute-done((f32[32,4096]{1,0:T(8,128)S(1)}, f32[32,4096]{1,0:T(8,128)S(1)}, u32[]{:S(2)}, u32[]{:S(2)}) %collective-permute-start.9) | collective-permute-done | bytes 524320 | tf_op jit(solution)/shard_map/ppermute | solution.py:23
  84.5 7.9 %reshape.108.a_ref = f32[256,64,64]{2,1,0:T(8,128)} reshape(f32[8,32,4096]{2,1,0:T(8,128)} %bitcast_dynamic-update-slice_fusion) | data formatting | bytes 8388608 | tf_op jit(solution)/shard_map/reshape | solution.py:122
  92.4 5.4 %pad_maximum_fusion = f32[2,8,2,6,64,128]{5,4,3,2,1,0:T(8,128)} fusion(f32[1,8,2,6,64,128]{5,4,3,2,1,0:T(8,128)} %bitcast.38, f32[1,8,2,6,64,128]{5,4,3,2,1,0:T(8,128)S(1)} %bitcast.67), kind=kLoop, calls=%fused_computation | loop fusion | flops 1572864 | bytes 12582912 | tf_op jit(solution)/shard_map/stack | solution.py:60
  97.9 14.8 %shard_map.46 = f32[32,64,128]{2,1,0:T(8,128)} custom-call(s32[256]{0:T(256)S(1)} %fusion.6.index_ref, s32[256]{0:T(256)S(1)} %reshape_squeeze.3.rows_ref, f32[256,64,64]{2,1,0:T(8,128)} %reshape.108.a_ref, f32[192,64,128]{2,1,0:T(8,128)} %bitcast.66), custom_call_target="tpu_custom_call" | custom-call | flops 268435456 | bytes 11534336 | tf_op jit(solution)/shard_map/pallas_call | solution.py:90
  (62 shorter events, 10.4 us)
Async XLA Ops:
  0.7 7.6 %collective-permute-start = (s32[2,32]{1,0:T(2,128)S(1)}, s32[2,32]{1,0:T(2,128)S(1)}, u32[]{:S(2)}, u32[]{:S(2)}) collective-permute-start(s32[2,32]{1,0:T(2,128)S(1)} %get-tuple-element.12), channel_id=1, source_target_pairs={{0,128},{128,0},{1,129},{129,1},{2,130},{130,2},{3,131},{131,3},{4... | collective-permute-start | bytes 776 | tf_op jit(solution)/shard_map/ppermute | solution.py:18
  2.9 18.7 %collective-permute-start.10 = (f32[6,64,128]{2,1,0:T(8,128)}, f32[6,64,128]{2,1,0:T(8,128)S(1)}, u32[]{:S(2)}, u32[]{:S(2)}) collective-permute-start(f32[6,64,128]{2,1,0:T(8,128)} %param.7), channel_id=1, source_target_pairs={{0,2},{2,0},{1,3},{3,1},{4,6},{6,4},{5,7},{7,5},{8,10},{10,8},{9,1... | collective-permute-start | bytes 589832 | tf_op jit(solution)/shard_map/ppermute | solution.py:18
  3.6 25.8 %collective-permute-start.5 = (f32[32,4096]{1,0:T(8,128)}, f32[32,4096]{1,0:T(8,128)}, u32[]{:S(2)}, u32[]{:S(2)}) collective-permute-start(f32[32,4096]{1,0:T(8,128)} %bitcast.68), channel_id=1, source_target_pairs={{0,128},{128,0},{1,129},{129,1},{2,130},{130,2},{3,131},{131,3},{4... | collective-permute-start | bytes 1572872 | tf_op jit(solution)/shard_map/ppermute | solution.py:18
  8.3 4.4 %collective-permute-start.2 = (s32[2,2,32]{2,1,0:T(2,128)S(1)}, s32[2,2,32]{2,1,0:T(2,128)S(1)}, u32[]{:S(2)}, u32[]{:S(2)}) collective-permute-start(s32[2,2,32]{2,1,0:T(2,128)S(1)} %pad_add_fusion), channel_id=1, source_target_pairs={{0,96},{32,0},{64,32},{96,64},{1,97},{33,1},{65,33},{97,65},{2,98}... | collective-permute-start | bytes 1544 | tf_op jit(solution)/shard_map/ppermute | solution.py:23
  11.4 4.8 %collective-permute-start.1 = (s32[2,2,32]{2,1,0:T(2,128)S(1)}, s32[2,2,32]{2,1,0:T(2,128)S(1)}, u32[]{:S(2)}, u32[]{:S(2)}) collective-permute-start(s32[2,2,32]{2,1,0:T(2,128)S(1)} %pad_add_fusion), channel_id=1, source_target_pairs={{0,32},{32,64},{64,96},{96,0},{1,33},{33,65},{65,97},{97,1},{2,34}... | collective-permute-start | bytes 1544 | tf_op jit(solution)/shard_map/ppermute | solution.py:23
  12.7 4.8 %collective-permute-start.3 = (s32[2,32]{1,0:T(2,128)S(1)}, s32[2,32]{1,0:T(2,128)S(1)}, u32[]{:S(2)}, u32[]{:S(2)}) collective-permute-start(s32[2,32]{1,0:T(2,128)S(1)} %slice_bitcast_fusion.5), channel_id=1, source_target_pairs={{0,96},{32,0},{64,32},{96,64},{1,97},{33,1},{65,33},{97,65},{2,98}... | collective-permute-start | bytes 776 | tf_op jit(solution)/shard_map/ppermute | solution.py:23
  16.2 4.8 %collective-permute-start.4 = (s32[2,32]{1,0:T(2,128)S(1)}, s32[2,32]{1,0:T(2,128)S(1)}, u32[]{:S(2)}, u32[]{:S(2)}) collective-permute-start(s32[2,32]{1,0:T(2,128)S(1)} %slice_bitcast_fusion.4), channel_id=1, source_target_pairs={{0,32},{32,64},{64,96},{96,0},{1,33},{33,65},{65,97},{97,1},{2,34}... | collective-permute-start | bytes 776 | tf_op jit(solution)/shard_map/ppermute | solution.py:23
  22.6 12.2 %collective-permute-start.11 = (f32[2,6,64,128]{3,2,1,0:T(8,128)S(1)}, f32[2,6,64,128]{3,2,1,0:T(8,128)S(1)}, u32[]{:S(2)}, u32[]{:S(2)}) collective-permute-start(f32[2,6,64,128]{3,2,1,0:T(8,128)S(1)} %pad_maximum_fusion.2), channel_id=1, source_target_pairs={{0,28},{4,0},{8,4},{12,8},{16,12},{20,16},{24,20},{28,24},{1,29},{... | collective-permute-start | bytes 1179656 | tf_op jit(solution)/shard_map/ppermute | solution.py:23
  28.5 10.2 %collective-permute-start.15 = (f32[2,6,64,128]{3,2,1,0:T(8,128)S(1)}, f32[2,6,64,128]{3,2,1,0:T(8,128)S(1)}, u32[]{:S(2)}, u32[]{:S(2)}) collective-permute-start(f32[2,6,64,128]{3,2,1,0:T(8,128)S(1)} %pad_maximum_fusion.2), channel_id=1, source_target_pairs={{0,4},{4,8},{8,12},{12,16},{16,20},{20,24},{24,28},{28,0},{1,5},{5... | collective-permute-start | bytes 1179656 | tf_op jit(solution)/shard_map/ppermute | solution.py:23
  30.8 30.2 %collective-permute-start.7 = (f32[2,32,4096]{2,1,0:T(8,128)S(1)}, f32[2,32,4096]{2,1,0:T(8,128)S(1)}, u32[]{:S(2)}, u32[]{:S(2)}) collective-permute-start(f32[2,32,4096]{2,1,0:T(8,128)S(1)} %pad_maximum_fusion.1), channel_id=1, source_target_pairs={{0,96},{32,0},{64,32},{96,64},{1,97},{33,1},{65,33},{97,65},{2,98}... | collective-permute-start | bytes 3145736 | tf_op jit(solution)/shard_map/ppermute | solution.py:23
  30.9 37.2 %collective-permute-start.6 = (f32[2,32,4096]{2,1,0:T(8,128)S(1)}, f32[2,32,4096]{2,1,0:T(8,128)S(1)}, u32[]{:S(2)}, u32[]{:S(2)}) collective-permute-start(f32[2,32,4096]{2,1,0:T(8,128)S(1)} %pad_maximum_fusion.1), channel_id=1, source_target_pairs={{0,32},{32,64},{64,96},{96,0},{1,33},{33,65},{65,97},{97,1},{2,34}... | collective-permute-start | bytes 3145736 | tf_op jit(solution)/shard_map/ppermute | solution.py:23
  34.7 10.8 %collective-permute-start.12 = (f32[2,6,64,128]{3,2,1,0:T(8,128)S(1)}, f32[2,6,64,128]{3,2,1,0:T(8,128)S(1)}, u32[]{:S(2)}, u32[]{:S(2)}) collective-permute-start(f32[2,6,64,128]{3,2,1,0:T(8,128)S(1)} %collective-permute-done.11), channel_id=1, source_target_pairs={{0,28},{4,0},{8,4},{12,8},{16,12},{20,16},{24,20},{28,24},{1,29},{... | collective-permute-start | bytes 1179656 | tf_op jit(solution)/shard_map/ppermute | solution.py:23
  38.7 11.0 %collective-permute-start.16 = (f32[2,6,64,128]{3,2,1,0:T(8,128)S(1)}, f32[2,6,64,128]{3,2,1,0:T(8,128)S(1)}, u32[]{:S(2)}, u32[]{:S(2)}) collective-permute-start(f32[2,6,64,128]{3,2,1,0:T(8,128)S(1)} %collective-permute-done.15), channel_id=1, source_target_pairs={{0,4},{4,8},{8,12},{12,16},{16,20},{20,24},{24,28},{28,0},{1,5},{5... | collective-permute-start | bytes 1179656 | tf_op jit(solution)/shard_map/ppermute | solution.py:23
  45.5 11.1 %collective-permute-start.13 = (f32[2,6,64,128]{3,2,1,0:T(8,128)S(1)}, f32[2,6,64,128]{3,2,1,0:T(8,128)S(1)}, u32[]{:S(2)}, u32[]{:S(2)}) collective-permute-start(f32[2,6,64,128]{3,2,1,0:T(8,128)S(1)} %collective-permute-done.12), channel_id=1, source_target_pairs={{0,28},{4,0},{8,4},{12,8},{16,12},{20,16},{24,20},{28,24},{1,29},{... | collective-permute-start | bytes 1179656 | tf_op jit(solution)/shard_map/ppermute | solution.py:23
  49.7 11.1 %collective-permute-start.17 = (f32[2,6,64,128]{3,2,1,0:T(8,128)S(1)}, f32[2,6,64,128]{3,2,1,0:T(8,128)S(1)}, u32[]{:S(2)}, u32[]{:S(2)}) collective-permute-start(f32[2,6,64,128]{3,2,1,0:T(8,128)S(1)} %collective-permute-done.16), channel_id=1, source_target_pairs={{0,4},{4,8},{8,12},{12,16},{16,20},{20,24},{24,28},{28,0},{1,5},{5... | collective-permute-start | bytes 1179656 | tf_op jit(solution)/shard_map/ppermute | solution.py:23
  56.6 7.1 %collective-permute-start.14 = (f32[6,64,128]{2,1,0:T(8,128)S(1)}, f32[6,64,128]{2,1,0:T(8,128)S(1)}, u32[]{:S(2)}, u32[]{:S(2)}) collective-permute-start(f32[6,64,128]{2,1,0:T(8,128)S(1)} %slice_bitcast_fusion.3), channel_id=1, source_target_pairs={{0,28},{4,0},{8,4},{12,8},{16,12},{20,16},{24,20},{28,24},{1,29},{... | collective-permute-start | bytes 589832 | tf_op jit(solution)/shard_map/ppermute | solution.py:23
  60.9 7.0 %collective-permute-start.18 = (f32[6,64,128]{2,1,0:T(8,128)S(1)}, f32[6,64,128]{2,1,0:T(8,128)S(1)}, u32[]{:S(2)}, u32[]{:S(2)}) collective-permute-start(f32[6,64,128]{2,1,0:T(8,128)S(1)} %slice_bitcast_fusion.2), channel_id=1, source_target_pairs={{0,4},{4,8},{8,12},{12,16},{16,20},{20,24},{24,28},{28,0},{1,5},{5... | collective-permute-start | bytes 589832 | tf_op jit(solution)/shard_map/ppermute | solution.py:23
  61.0 9.3 %collective-permute-start.8 = (f32[32,4096]{1,0:T(8,128)S(1)}, f32[32,4096]{1,0:T(8,128)S(1)}, u32[]{:S(2)}, u32[]{:S(2)}) collective-permute-start(f32[32,4096]{1,0:T(8,128)S(1)} %slice_bitcast_fusion.1), channel_id=1, source_target_pairs={{0,96},{32,0},{64,32},{96,64},{1,97},{33,1},{65,33},{97,65},{2,98}... | collective-permute-start | bytes 1572872 | tf_op jit(solution)/shard_map/ppermute | solution.py:23
  68.0 24.5 %collective-permute-start.19 = (f32[8,2,6,64,128]{4,3,2,1,0:T(8,128)S(1)}, f32[8,2,6,64,128]{4,3,2,1,0:T(8,128)}, u32[]{:S(2)}, u32[]{:S(2)}) collective-permute-start(f32[8,2,6,64,128]{4,3,2,1,0:T(8,128)S(1)} %bitcast_dynamic-update-slice_fusion.2), channel_id=1, source_target_pairs={{0,1},{1,0},{2,3},{3,2},{4,5},{5,4},{6,7},{7,6},{8,9},{9,8},{10,11... | collective-permute-start | bytes 9437192 | tf_op jit(solution)/shard_map/ppermute | solution.py:18
  68.1 15.6 %collective-permute-start.9 = (f32[32,4096]{1,0:T(8,128)S(1)}, f32[32,4096]{1,0:T(8,128)S(1)}, u32[]{:S(2)}, u32[]{:S(2)}) collective-permute-start(f32[32,4096]{1,0:T(8,128)S(1)} %slice_bitcast_fusion), channel_id=1, source_target_pairs={{0,32},{32,64},{64,96},{96,0},{1,33},{33,65},{65,97},{97,1},{2,34}... | collective-permute-start | bytes 1572872 | tf_op jit(solution)/shard_map/ppermute | solution.py:23

commit v6 on v5

--- a/solution.py
+++ b/solution.py
@@ -23,21 +23,27 @@
     return lax.ppermute(block, axis, [(i, (i + distance) % n) for i in range(n)])
 
 
-def gather_a(a_own):
+def gather_a(a_own, halves=True):
     n_y = lax.axis_size("y")
     xl = lax.axis_index("xl")
     y = lax.axis_index("y")
+    half = a_own.shape[0] // 2
     a_x = swap(a_own, "xl")
-    bundle = jnp.stack([a_own, a_x])
-    from_minus = shift(bundle, "y", 1)
-    from_plus = shift(bundle, "y", -1)
-    far_a = shift(from_plus[0], "y", -1)
-    far_b = shift(from_minus[1], "y", 1)
-    panels = [a_own, a_x, from_minus[0], from_minus[1], from_plus[0], from_plus[1], far_a, far_b]
-    ys = [y, y, y - 1, y - 1, y + 1, y + 1, y + 2, y + 2]
-    xls = [xl, 1 - xl] * 4
+    own_minus = shift(a_own, "y", 1)
+    own_plus = shift(a_own, "y", -1)
+    x_minus = shift(a_x, "y", 1)
+    x_plus = shift(a_x, "y", -1)
+    if halves:
+        far_own = jnp.concatenate([shift(own_plus[:half], "y", -1), shift(own_minus[half:], "y", 1)])
+        far_x = jnp.concatenate([shift(x_plus[:half], "y", -1), shift(x_minus[half:], "y", 1)])
+    else:
+        far_own = shift(own_plus, "y", -1)
+        far_x = shift(x_plus, "y", -1)
+    panels = [a_own, a_x, own_minus, own_plus, x_minus, x_plus, far_own, far_x]
+    ys = [y, y, y - 1, y + 1, y - 1, y + 1, y + 2, y + 2]
+    xls = [xl, 1 - xl, xl, xl, 1 - xl, 1 - xl, xl, 1 - xl]
     pid = jnp.stack([xls[k] * n_y + (ys[k] % n_y) for k in range(8)]).astype(jnp.int32)
-    return jnp.stack(panels), pid
+    return panels, pid
 
 
 def gather_b(b_own):
@@ -57,17 +63,20 @@
     far_down = shift(down[1], "z", 1)
     by_offset[half] = jnp.stack([far_up, far_down])
     mine = jnp.stack(by_offset)
-    return jnp.stack([mine, swap(mine, "core")])
+    return mine, swap(mine, "core")
 
 
-def product_kernel(index_ref, rows_ref, a_ref, table_ref, out_ref, acc_ref):
+def product_kernel(index_ref, rows_ref, a_ref, mine_ref, other_ref, out_ref, acc_ref):
     acc_ref[...] = jnp.zeros_like(acc_ref)
     blocks = out_ref.shape[0]
 
     def one_slot(g, carry):
         row = jnp.minimum(rows_ref[g], blocks)
         left = a_ref[g]
-        right = table_ref[index_ref[g]]
+        stripes = mine_ref.shape[0]
+        index = index_ref[g]
+        local = index % stripes
+        right = jnp.where(index < stripes, mine_ref[local], other_ref[local])
         left_hi = left.astype(jnp.bfloat16)
         left_lo = (left - left_hi.astype(jnp.float32)).astype(jnp.bfloat16)
         right_hi = right.astype(jnp.bfloat16)
@@ -82,24 +91,24 @@
     out_ref[...] = acc_ref[:blocks]
 
 
-def product(index, rows, left, table):
+def product(index, rows, left, mine, other):
     slots, blk, _ = left.shape
-    columns = table.shape[2]
+    columns = mine.shape[2]
     vmem = pl.BlockSpec(memory_space=pltpu.VMEM)
     smem = pl.BlockSpec(memory_space=pltpu.SMEM)
     return pl.pallas_call(
         product_kernel,
         out_shape=jax.ShapeDtypeStruct((MB, blk, columns), jnp.float32),
-        in_specs=[smem, smem, vmem, vmem],
+        in_specs=[smem, smem, vmem, vmem, vmem],
         out_specs=vmem,
         scratch_shapes=[pltpu.VMEM((MB + 1, blk, columns), jnp.float32)],
         compiler_params=pltpu.CompilerParams(vmem_limit_bytes=48 * 1024 * 1024),
         cost_estimate=pl.CostEstimate(
             flops=2 * slots * blk * blk * columns,
-            bytes_accessed=4 * (left.size + table.size + MB * blk * columns),
+            bytes_accessed=4 * (left.size + 2 * mine.size + MB * blk * columns),
             transcendentals=0,
         ),
-    )(index, rows, left, table)
+    )(index, rows, left, mine, other)
 
 
 def shards(a_blocks, a_rows, a_slots, b_stripes):
@@ -108,10 +117,13 @@
     columns = b_stripes.shape[2]
 
     ints = jnp.stack([a_rows[0, 0], a_slots[0, 0]])
-    ints_k, _ = gather_a(ints)
-    a_all, pid = gather_a(a_blocks[0, 0])
-    table = gather_b(b_stripes)
-    table = table.reshape(-1, BLK, columns)
+    ints_k, _ = gather_a(ints, halves=False)
+    ints_k = jnp.stack(ints_k)
+    panels, pid = gather_a(a_blocks[0, 0])
+    a_all = jnp.stack([p.reshape(-1, BLK, BLK) for p in panels])
+    mine, other = gather_b(b_stripes)
+    mine = mine.reshape(-1, BLK, columns)
+    other = other.reshape(-1, BLK, columns)
 
     rows = ints_k[:, 0]
     slots = ints_k[:, 1]
@@ -120,7 +132,7 @@
     xh_rel = (slots // 12) ^ lax.axis_index("xh")
     index = ((core_rel * n_z + d) * 2 + xh_rel) * 6 + slots % 6
     left = a_all.reshape(-1, BLK, BLK)
-    out = product(index.reshape(-1), rows.reshape(-1), left, table)
+    out = product(index.reshape(-1), rows.reshape(-1), left, mine, other)
     return out.reshape(MB * BLK, columns)
 
 

time: 113 us -> 147 us (1.30); the launches traced: 113 us -> 144 us
  local copies, waits for them, and re-layouts: 16.4 us -> 41 us
  starting transfers between devices: 31 us -> 45.3 us
  other arithmetic: 10.2 us -> 6.28 us
  waiting for transfers between devices: 40 us -> 37.5 us
    another operation x3 -> x11, local copies, waits for them, and re-layouts: 0.92 us -> 21.1 us  [the longest x9 21.1 us: shards(): a_all = jnp.stack([p.reshape(-1, BLK, BLK) for p in panels])]
    ppermute x16 -> x22, waiting for transfers between devices: 40 us -> 22.3 us  [shift(): lax.ppermute(block, axis, [(i, (i + distance) % n) for i in range(n)])]
    ppermute x4, waiting for transfers between devices: 0.01 us -> 15.2 us  [swap(): return lax.ppermute(block, axis, [(0, 1), (1, 0)])]
    ppermute x16 -> x22, starting transfers between devices: 26.2 us -> 41 us  [shift(): lax.ppermute(block, axis, [(i, (i + distance) % n) for i in range(n)])]
    reshape x1 -> x0, local copies, waits for them, and re-layouts: 7.88 us -> none  [shards(): left = a_all.reshape(-1, BLK, BLK)]
    another operation x4 -> x1, other arithmetic: 7.39 us -> 0.72 us  [shards(): ints = jnp.stack([a_rows[0, 0], a_slots[0, 0]])]
    unnamed x14 -> x28, local copies, waits for them, and re-layouts: 6.88 us -> 12.9 us
    slice x0 -> x4, local copies, waits for them, and re-layouts: none -> 5.28 us  [the longest x1 1.68 us: gather_a(): own_plus[:half]]
  transfers between devices with their start and end apart: 20 -> 26, of which waited for: 12 -> 12; matrix products, arithmetic and copies ran while one was open for 18% -> 32% of each run, Pallas kernels for 0% -> 0%
where the time goes in v6:
time: 147 us; the launch traced here: 144 us
  starting transfers between devices  45.3 us (31%)
  local copies, waits for them, and re-layouts  41 us (28%)
  waiting for transfers between devices  37.5 us (26%)
  Pallas kernels  14 us (10%)
  other arithmetic  6.28 us (4%)
    ppermute x22, starting transfers between devices, shift(): lax.ppermute(block, axis, [(i, (i + distance) % n) for i in range(n)])  41 us
    ppermute x22, waiting for transfers between devices, shift(): lax.ppermute(block, axis, [(i, (i + distance) % n) for i in range(n)])  22.3 us
    another operation x9, local copies, waits for them, and re-layouts, shards(): a_all = jnp.stack([p.reshape(-1, BLK, BLK) for p in panels])  21.1 us
    ppermute x4, waiting for transfers between devices, swap(): return lax.ppermute(block, axis, [(0, 1), (1, 0)])  15.2 us
    pallas_call x1, Pallas kernels, product(): pl.pallas_call(product_kernel, out_shape=jax.ShapeDtypeStruct((MB, blk, c...  14 us
    unnamed x28, local copies, waits for them, and re-layouts  12.9 us
    ppermute x4, starting transfers between devices, swap(): return lax.ppermute(block, axis, [(0, 1), (1, 0)])  4.24 us
  transfers between devices with their start and end apart: 26, of which 12 were waited for; matrix products, arithmetic and copies ran while one was open for 32% of the time, Pallas kernels for 0%

profile of v6, /device:TPU:2, one launch (start us, length us, event | category | flops | bytes accessed | tf_op | source)
XLA Modules:
  0.0 144.3 jit_solution(3138908287829041352)
XLA Ops:
  3.0 3.2 %collective-permute-start.2 = (s32[2,32]{1,0:T(2,128)S(1)}, s32[2,32]{1,0:T(2,128)S(1)}, u32[]{:S(2)}, u32[]{:S(2)}) collective-permute-start(s32[2,32]{1,0:T(2,128)S(1)} %pad_add_fusion), channel_id=1, source_target_pairs={{0,96},{32,0},{64,32},{96,64},{1,97},{33,1},{65,33},{97,65},{2,98}... | collective-permute-start | bytes 776 | tf_op jit(solution)/shard_map/ppermute | solution.py:23
  8.2 15.2 %collective-permute-done.16 = f32[6,64,128]{2,1,0:T(8,128)S(1)} collective-permute-done((f32[6,64,128]{2,1,0:T(8,128)}, f32[6,64,128]{2,1,0:T(8,128)S(1)}, u32[]{:S(2)}, u32[]{:S(2)}) %collective-permute-start.16) | collective-permute-done | bytes 196640 | tf_op jit(solution)/shard_map/ppermute | solution.py:18
  29.7 4.0 %collective-permute-start.17 = (f32[2,6,64,128]{3,2,1,0:T(8,128)S(1)}, f32[2,6,64,128]{3,2,1,0:T(8,128)S(1)}, u32[]{:S(2)}, u32[]{:S(2)}) collective-permute-start(f32[2,6,64,128]{3,2,1,0:T(8,128)S(1)} %pad_maximum_fusion.2), channel_id=1, source_target_pairs={{0,28},{4,0},{8,4},{12,8},{16,12},{20,16},{24,20},{28,24},{1,29},{... | collective-permute-start | bytes 1179656 | tf_op jit(solution)/shard_map/ppermute | solution.py:23
  34.0 3.8 %collective-permute-done.21 = f32[2,6,64,128]{3,2,1,0:T(8,128)} collective-permute-done((f32[2,6,64,128]{3,2,1,0:T(8,128)S(1)}, f32[2,6,64,128]{3,2,1,0:T(8,128)}, u32[]{:S(2)}, u32[]{:S(2)}) %collective-permute-start.21) | collective-permute-done | bytes 393248 | tf_op jit(solution)/shard_map/ppermute | solution.py:23
  40.4 3.7 %collective-permute-start.18 = (f32[2,6,64,128]{3,2,1,0:T(8,128)S(1)}, f32[2,6,64,128]{3,2,1,0:T(8,128)S(1)}, u32[]{:S(2)}, u32[]{:S(2)}) collective-permute-start(f32[2,6,64,128]{3,2,1,0:T(8,128)S(1)} %collective-permute-done.17), channel_id=1, source_target_pairs={{0,28},{4,0},{8,4},{12,8},{16,12},{20,16},{24,20},{28,24},{1,29},{... | collective-permute-start | bytes 1179656 | tf_op jit(solution)/shard_map/ppermute | solution.py:23
  44.2 3.7 %collective-permute-done.22 = f32[2,6,64,128]{3,2,1,0:T(8,128)S(1)} collective-permute-done((f32[2,6,64,128]{3,2,1,0:T(8,128)}, f32[2,6,64,128]{3,2,1,0:T(8,128)S(1)}, u32[]{:S(2)}, u32[]{:S(2)}) %collective-permute-start.22) | collective-permute-done | bytes 393248 | tf_op jit(solution)/shard_map/ppermute | solution.py:23
  50.1 3.7 %collective-permute-start.19 = (f32[2,6,64,128]{3,2,1,0:T(8,128)S(1)}, f32[2,6,64,128]{3,2,1,0:T(8,128)S(1)}, u32[]{:S(2)}, u32[]{:S(2)}) collective-permute-start(f32[2,6,64,128]{3,2,1,0:T(8,128)S(1)} %collective-permute-done.18), channel_id=1, source_target_pairs={{0,28},{4,0},{8,4},{12,8},{16,12},{20,16},{24,20},{28,24},{1,29},{... | collective-permute-start | bytes 1179656 | tf_op jit(solution)/shard_map/ppermute | solution.py:23
  53.8 3.3 %collective-permute-done.23 = f32[2,6,64,128]{3,2,1,0:T(8,128)S(1)} collective-permute-done((f32[2,6,64,128]{3,2,1,0:T(8,128)S(1)}, f32[2,6,64,128]{3,2,1,0:T(8,128)S(1)}, u32[]{:S(2)}, u32[]{:S(2)}) %collective-permute-start.23) | collective-permute-done | bytes 393248 | tf_op jit(solution)/shard_map/ppermute | solution.py:23
  57.2 2.5 %collective-permute-done.19 = f32[2,6,64,128]{3,2,1,0:T(8,128)S(1)} collective-permute-done((f32[2,6,64,128]{3,2,1,0:T(8,128)S(1)}, f32[2,6,64,128]{3,2,1,0:T(8,128)S(1)}, u32[]{:S(2)}, u32[]{:S(2)}) %collective-permute-start.19) | collective-permute-done | bytes 393248 | tf_op jit(solution)/shard_map/ppermute | solution.py:23
  59.8 3.8 %collective-permute-start.20 = (f32[6,64,128]{2,1,0:T(8,128)S(1)}, f32[6,64,128]{2,1,0:T(8,128)S(1)}, u32[]{:S(2)}, u32[]{:S(2)}) collective-permute-start(f32[6,64,128]{2,1,0:T(8,128)S(1)} %slice_bitcast_fusion.1), channel_id=1, source_target_pairs={{0,28},{4,0},{8,4},{12,8},{16,12},{20,16},{24,20},{28,24},{1,29},{... | collective-permute-start | bytes 589832 | tf_op jit(solution)/shard_map/ppermute | solution.py:23
  70.3 2.8 %collective-permute-start.5 = (s32[2,32]{1,0:T(2,128)S(1)}, s32[2,32]{1,0:T(2,128)S(1)}, u32[]{:S(2)}, u32[]{:S(2)}) collective-permute-start(s32[2,32]{1,0:T(2,128)S(1)} %collective-permute-done.2), channel_id=1, source_target_pairs={{0,96},{32,0},{64,32},{96,64},{1,97},{33,1},{65,33},{97,65},{2,98}... | collective-permute-start | bytes 776 | tf_op jit(solution)/shard_map/ppermute | solution.py:23
  74.4 3.5 %collective-permute-start.6 = (s32[2,32]{1,0:T(2,128)S(1)}, s32[2,32]{1,0:T(2,128)S(1)}, u32[]{:S(2)}, u32[]{:S(2)}) collective-permute-start(s32[2,32]{1,0:T(2,128)S(1)} %collective-permute-done.4), channel_id=1, source_target_pairs={{0,96},{32,0},{64,32},{96,64},{1,97},{33,1},{65,33},{97,65},{2,98}... | collective-permute-start | bytes 776 | tf_op jit(solution)/shard_map/ppermute | solution.py:23
  82.6 3.5 %collective-permute-start.12 = (f32[16,4096]{1,0:T(8,128)}, f32[16,4096]{1,0:T(8,128)}, u32[]{:S(2)}, u32[]{:S(2)}) collective-permute-start(f32[16,4096]{1,0:T(8,128)} %slice.34), channel_id=1, source_target_pairs={{0,96},{32,0},{64,32},{96,64},{1,97},{33,1},{65,33},{97,65},{2,98}... | collective-permute-start | bytes 786440 | tf_op jit(solution)/shard_map/ppermute | solution.py:23
  86.1 2.5 %stack_reshape.22 = f32[1,32,64,64]{3,2,1,0:T(8,128)} reshape(f32[32,4096]{1,0:T(8,128)} %collective-permute-done.8) | data formatting | bytes 1048576 | tf_op jit(solution)/shard_map/stack;reshape | solution.py:123
  88.5 2.5 %stack_reshape.23 = f32[1,32,64,64]{3,2,1,0:T(8,128)} reshape(f32[32,4096]{1,0:T(8,128)} %collective-permute-done.9) | data formatting | bytes 1048576 | tf_op jit(solution)/shard_map/stack;reshape | solution.py:123
  91.1 2.4 %stack_reshape.21 = f32[1,32,64,64]{3,2,1,0:T(8,128)} reshape(f32[32,4096]{1,0:T(8,128)} %collective-permute-done.7) | data formatting | bytes 1048576 | tf_op jit(solution)/shard_map/stack;reshape | solution.py:123
  93.5 3.2 %collective-permute-start.11 = (f32[32,4096]{1,0:T(8,128)}, f32[32,4096]{1,0:T(8,128)}, u32[]{:S(2)}, u32[]{:S(2)}) collective-permute-start(f32[32,4096]{1,0:T(8,128)} %collective-permute-done.7), channel_id=1, source_target_pairs={{0,96},{32,0},{64,32},{96,64},{1,97},{33,1},{65,33},{97,65},{2,98}... | collective-permute-start | bytes 1572872 | tf_op jit(solution)/shard_map/ppermute | solution.py:23
  104.3 2.5 %stack_reshape.26 = f32[1,32,64,64]{3,2,1,0:T(8,128)} reshape(f32[32,4096]{1,0:T(8,128)} %pad_maximum_fusion) | data formatting | bytes 1048576 | tf_op jit(solution)/shard_map/stack;reshape | solution.py:123
  109.5 3.2 %collective-permute-start.14 = (f32[16,4096]{1,0:T(8,128)}, f32[16,4096]{1,0:T(8,128)}, u32[]{:S(2)}, u32[]{:S(2)}) collective-permute-start(f32[16,4096]{1,0:T(8,128)} %slice.36), channel_id=1, source_target_pairs={{0,96},{32,0},{64,32},{96,64},{1,97},{33,1},{65,33},{97,65},{2,98}... | collective-permute-start | bytes 786440 | tf_op jit(solution)/shard_map/ppermute | solution.py:23
  112.8 2.4 %stack_reshape.24 = f32[1,32,64,64]{3,2,1,0:T(8,128)} reshape(f32[32,4096]{1,0:T(8,128)} %collective-permute-done.10) | data formatting | bytes 1048576 | tf_op jit(solution)/shard_map/stack;reshape | solution.py:123
  115.2 2.5 %stack_reshape.25 = f32[1,32,64,64]{3,2,1,0:T(8,128)} reshape(f32[32,4096]{1,0:T(8,128)} %collective-permute-done.11) | data formatting | bytes 1048576 | tf_op jit(solution)/shard_map/stack;reshape | solution.py:123
  117.7 2.4 %constant_dynamic-update-slice_fusion.11 = f32[8,32,64,64]{3,2,1,0:T(8,128)} fusion(f32[8,32,64,64]{3,2,1,0:T(8,128)} %constant_dynamic-update-slice_fusion.12, f32[1,32,64,64]{3,2,1,0:T(8,128)} %stack_reshape.24), kind=kLoop, calls=%fused_computation.25 | loop fusion | bytes 2097152
  125.4 2.4 %stack_reshape.27 = f32[1,32,64,64]{3,2,1,0:T(8,128)} reshape(f32[32,4096]{1,0:T(8,128)} %pad_maximum_fusion.1) | data formatting | bytes 1048576 | tf_op jit(solution)/shard_map/stack;reshape | solution.py:123
  130.2 14.0 %shard_map.46 = f32[32,64,128]{2,1,0:T(8,128)} custom-call(s32[256]{0:T(256)S(1)} %fusion.6.index_ref, s32[256]{0:T(256)S(1)} %reshape_squeeze.3.rows_ref, f32[256,64,64]{2,1,0:T(8,128)} %bitcast.60, f32[96,64,128]{2,1,0:T(8,128)S(1)} %bitcast.59, f32[96,64,128]{2,1,0:T(8,128)} %bitcast.35.other_ref), custom_call_target="tpu_custom_call" | custom-call | flops 268435456 | bytes 11534336 | tf_op jit(solution)/shard_map/pallas_call | solution.py:99
  (94 shorter events, 47.2 us)
Async XLA Ops:
  0.7 29.0 %collective-permute-start = (s32[2,32]{1,0:T(2,128)S(1)}, s32[2,32]{1,0:T(2,128)S(1)}, u32[]{:S(2)}, u32[]{:S(2)}) collective-permute-start(s32[2,32]{1,0:T(2,128)S(1)} %pad_add_fusion), channel_id=1, source_target_pairs={{0,128},{128,0},{1,129},{129,1},{2,130},{130,2},{3,131},{131,3},{4... | collective-permute-start | bytes 776 | tf_op jit(solution)/shard_map/ppermute | solution.py:18
  3.0 30.8 %collective-permute-start.1 = (s32[2,32]{1,0:T(2,128)S(1)}, s32[2,32]{1,0:T(2,128)S(1)}, u32[]{:S(2)}, u32[]{:S(2)}) collective-permute-start(s32[2,32]{1,0:T(2,128)S(1)} %pad_add_fusion), channel_id=1, source_target_pairs={{0,32},{32,64},{64,96},{96,0},{1,33},{33,65},{65,97},{97,1},{2,34}... | collective-permute-start | bytes 776 | tf_op jit(solution)/shard_map/ppermute | solution.py:23
  3.0 34.9 %collective-permute-start.2 = (s32[2,32]{1,0:T(2,128)S(1)}, s32[2,32]{1,0:T(2,128)S(1)}, u32[]{:S(2)}, u32[]{:S(2)}) collective-permute-start(s32[2,32]{1,0:T(2,128)S(1)} %pad_add_fusion), channel_id=1, source_target_pairs={{0,96},{32,0},{64,32},{96,64},{1,97},{33,1},{65,33},{97,65},{2,98}... | collective-permute-start | bytes 776 | tf_op jit(solution)/shard_map/ppermute | solution.py:23
  6.2 84.8 %collective-permute-start.7 = (f32[32,4096]{1,0:T(8,128)}, f32[32,4096]{1,0:T(8,128)}, u32[]{:S(2)}, u32[]{:S(2)}) collective-permute-start(f32[32,4096]{1,0:T(8,128)} %bitcast.18), channel_id=1, source_target_pairs={{0,128},{128,0},{1,129},{129,1},{2,130},{130,2},{3,131},{131,3},{4... | collective-permute-start | bytes 1572872 | tf_op jit(solution)/shard_map/ppermute | solution.py:18
  6.3 17.1 %collective-permute-start.16 = (f32[6,64,128]{2,1,0:T(8,128)}, f32[6,64,128]{2,1,0:T(8,128)S(1)}, u32[]{:S(2)}, u32[]{:S(2)}) collective-permute-start(f32[6,64,128]{2,1,0:T(8,128)} %param.7), channel_id=1, source_target_pairs={{0,2},{2,0},{1,3},{3,1},{4,6},{6,4},{5,7},{7,5},{8,10},{10,8},{9,1... | collective-permute-start | bytes 589832 | tf_op jit(solution)/shard_map/ppermute | solution.py:18
  24.3 13.5 %collective-permute-start.21 = (f32[2,6,64,128]{3,2,1,0:T(8,128)S(1)}, f32[2,6,64,128]{3,2,1,0:T(8,128)}, u32[]{:S(2)}, u32[]{:S(2)}) collective-permute-start(f32[2,6,64,128]{3,2,1,0:T(8,128)S(1)} %pad_maximum_fusion.2), channel_id=1, source_target_pairs={{0,4},{4,8},{8,12},{12,16},{16,20},{20,24},{24,28},{28,0},{1,5},{5... | collective-permute-start | bytes 1179656 | tf_op jit(solution)/shard_map/ppermute | solution.py:23
  29.7 10.7 %collective-permute-start.17 = (f32[2,6,64,128]{3,2,1,0:T(8,128)S(1)}, f32[2,6,64,128]{3,2,1,0:T(8,128)S(1)}, u32[]{:S(2)}, u32[]{:S(2)}) collective-permute-start(f32[2,6,64,128]{3,2,1,0:T(8,128)S(1)} %pad_maximum_fusion.2), channel_id=1, source_target_pairs={{0,28},{4,0},{8,4},{12,8},{16,12},{20,16},{24,20},{28,24},{1,29},{... | collective-permute-start | bytes 1179656 | tf_op jit(solution)/shard_map/ppermute | solution.py:23
  33.7 46.1 %collective-permute-start.8 = (f32[32,4096]{1,0:T(8,128)}, f32[32,4096]{1,0:T(8,128)}, u32[]{:S(2)}, u32[]{:S(2)}) collective-permute-start(f32[32,4096]{1,0:T(8,128)} %bitcast.18), channel_id=1, source_target_pairs={{0,32},{32,64},{64,96},{96,0},{1,33},{33,65},{65,97},{97,1},{2,34}... | collective-permute-start | bytes 1572872 | tf_op jit(solution)/shard_map/ppermute | solution.py:23
  37.9 10.1 %collective-permute-start.22 = (f32[2,6,64,128]{3,2,1,0:T(8,128)}, f32[2,6,64,128]{3,2,1,0:T(8,128)S(1)}, u32[]{:S(2)}, u32[]{:S(2)}) collective-permute-start(f32[2,6,64,128]{3,2,1,0:T(8,128)} %collective-permute-done.21), channel_id=1, source_target_pairs={{0,4},{4,8},{8,12},{12,16},{16,20},{20,24},{24,28},{28,0},{1,5},{5... | collective-permute-start | bytes 1179656 | tf_op jit(solution)/shard_map/ppermute | solution.py:23
  37.9 43.0 %collective-permute-start.9 = (f32[32,4096]{1,0:T(8,128)}, f32[32,4096]{1,0:T(8,128)}, u32[]{:S(2)}, u32[]{:S(2)}) collective-permute-start(f32[32,4096]{1,0:T(8,128)} %bitcast.18), channel_id=1, source_target_pairs={{0,96},{32,0},{64,32},{96,64},{1,97},{33,1},{65,33},{97,65},{2,98}... | collective-permute-start | bytes 1572872 | tf_op jit(solution)/shard_map/ppermute | solution.py:23
  40.4 9.7 %collective-permute-start.18 = (f32[2,6,64,128]{3,2,1,0:T(8,128)S(1)}, f32[2,6,64,128]{3,2,1,0:T(8,128)S(1)}, u32[]{:S(2)}, u32[]{:S(2)}) collective-permute-start(f32[2,6,64,128]{3,2,1,0:T(8,128)S(1)} %collective-permute-done.17), channel_id=1, source_target_pairs={{0,28},{4,0},{8,4},{12,8},{16,12},{20,16},{24,20},{28,24},{1,29},{... | collective-permute-start | bytes 1179656 | tf_op jit(solution)/shard_map/ppermute | solution.py:23
  47.9 9.2 %collective-permute-start.23 = (f32[2,6,64,128]{3,2,1,0:T(8,128)S(1)}, f32[2,6,64,128]{3,2,1,0:T(8,128)S(1)}, u32[]{:S(2)}, u32[]{:S(2)}) collective-permute-start(f32[2,6,64,128]{3,2,1,0:T(8,128)S(1)} %collective-permute-done.22), channel_id=1, source_target_pairs={{0,4},{4,8},{8,12},{12,16},{16,20},{20,24},{24,28},{28,0},{1,5},{5... | collective-permute-start | bytes 1179656 | tf_op jit(solution)/shard_map/ppermute | solution.py:23
  50.1 9.6 %collective-permute-start.19 = (f32[2,6,64,128]{3,2,1,0:T(8,128)S(1)}, f32[2,6,64,128]{3,2,1,0:T(8,128)S(1)}, u32[]{:S(2)}, u32[]{:S(2)}) collective-permute-start(f32[2,6,64,128]{3,2,1,0:T(8,128)S(1)} %collective-permute-done.18), channel_id=1, source_target_pairs={{0,28},{4,0},{8,4},{12,8},{16,12},{20,16},{24,20},{28,24},{1,29},{... | collective-permute-start | bytes 1179656 | tf_op jit(solution)/shard_map/ppermute | solution.py:23
  57.1 7.0 %collective-permute-start.24 = (f32[6,64,128]{2,1,0:T(8,128)S(1)}, f32[6,64,128]{2,1,0:T(8,128)S(1)}, u32[]{:S(2)}, u32[]{:S(2)}) collective-permute-start(f32[6,64,128]{2,1,0:T(8,128)S(1)} %slice_bitcast_fusion), channel_id=1, source_target_pairs={{0,4},{4,8},{8,12},{12,16},{16,20},{20,24},{24,28},{28,0},{1,5},{5... | collective-permute-start | bytes 589832 | tf_op jit(solution)/shard_map/ppermute | solution.py:23
  59.8 7.0 %collective-permute-start.20 = (f32[6,64,128]{2,1,0:T(8,128)S(1)}, f32[6,64,128]{2,1,0:T(8,128)S(1)}, u32[]{:S(2)}, u32[]{:S(2)}) collective-permute-start(f32[6,64,128]{2,1,0:T(8,128)S(1)} %slice_bitcast_fusion.1), channel_id=1, source_target_pairs={{0,28},{4,0},{8,4},{12,8},{16,12},{20,16},{24,20},{28,24},{1,29},{... | collective-permute-start | bytes 589832 | tf_op jit(solution)/shard_map/ppermute | solution.py:23
  64.1 5.4 %collective-permute-start.3 = (s32[2,32]{1,0:T(2,128)S(1)}, s32[2,32]{1,0:T(2,128)S(1)}, u32[]{:S(2)}, u32[]{:S(2)}) collective-permute-start(s32[2,32]{1,0:T(2,128)S(1)} %copy-done.4), channel_id=1, source_target_pairs={{0,32},{32,64},{64,96},{96,0},{1,33},{33,65},{65,97},{97,1},{2,34}... | collective-permute-start | bytes 776 | tf_op jit(solution)/shard_map/ppermute | solution.py:23
  69.5 60.8 %collective-permute-start.25 = (f32[8,2,6,64,128]{4,3,2,1,0:T(8,128)S(1)}, f32[8,2,6,64,128]{4,3,2,1,0:T(8,128)}, u32[]{:S(2)}, u32[]{:S(2)}) collective-permute-start(f32[8,2,6,64,128]{4,3,2,1,0:T(8,128)S(1)} %bitcast_dynamic-update-slice_fusion), channel_id=1, source_target_pairs={{0,1},{1,0},{2,3},{3,2},{4,5},{5,4},{6,7},{7,6},{8,9},{9,8},{10,11... | collective-permute-start | bytes 9437192 | tf_op jit(solution)/shard_map/ppermute | solution.py:18
  74.4 4.8 %collective-permute-start.6 = (s32[2,32]{1,0:T(2,128)S(1)}, s32[2,32]{1,0:T(2,128)S(1)}, u32[]{:S(2)}, u32[]{:S(2)}) collective-permute-start(s32[2,32]{1,0:T(2,128)S(1)} %collective-permute-done.4), channel_id=1, source_target_pairs={{0,96},{32,0},{64,32},{96,64},{1,97},{33,1},{65,33},{97,65},{2,98}... | collective-permute-start | bytes 776 | tf_op jit(solution)/shard_map/ppermute | solution.py:23
  80.8 21.7 %collective-permute-start.13 = (f32[16,4096]{1,0:T(8,128)S(1)}, f32[16,4096]{1,0:T(8,128)}, u32[]{:S(2)}, u32[]{:S(2)}) collective-permute-start(f32[16,4096]{1,0:T(8,128)S(1)} %slice.35), channel_id=1, source_target_pairs={{0,32},{32,64},{64,96},{96,0},{1,33},{33,65},{65,97},{97,1},{2,34}... | collective-permute-start | bytes 786440 | tf_op jit(solution)/shard_map/ppermute | solution.py:23
  82.6 19.9 %collective-permute-start.12 = (f32[16,4096]{1,0:T(8,128)}, f32[16,4096]{1,0:T(8,128)}, u32[]{:S(2)}, u32[]{:S(2)}) collective-permute-start(f32[16,4096]{1,0:T(8,128)} %slice.34), channel_id=1, source_target_pairs={{0,96},{32,0},{64,32},{96,64},{1,97},{33,1},{65,33},{97,65},{2,98}... | collective-permute-start | bytes 786440 | tf_op jit(solution)/shard_map/ppermute | solution.py:23
  93.5 13.3 %collective-permute-start.10 = (f32[32,4096]{1,0:T(8,128)}, f32[32,4096]{1,0:T(8,128)}, u32[]{:S(2)}, u32[]{:S(2)}) collective-permute-start(f32[32,4096]{1,0:T(8,128)} %collective-permute-done.7), channel_id=1, source_target_pairs={{0,32},{32,64},{64,96},{96,0},{1,33},{33,65},{65,97},{97,1},{2,34}... | collective-permute-start | bytes 1572872 | tf_op jit(solution)/shard_map/ppermute | solution.py:23
  93.5 14.4 %collective-permute-start.11 = (f32[32,4096]{1,0:T(8,128)}, f32[32,4096]{1,0:T(8,128)}, u32[]{:S(2)}, u32[]{:S(2)}) collective-permute-start(f32[32,4096]{1,0:T(8,128)} %collective-permute-done.7), channel_id=1, source_target_pairs={{0,96},{32,0},{64,32},{96,64},{1,97},{33,1},{65,33},{97,65},{2,98}... | collective-permute-start | bytes 1572872 | tf_op jit(solution)/shard_map/ppermute | solution.py:23
  107.8 15.8 %collective-permute-start.15 = (f32[16,4096]{1,0:T(8,128)S(1)}, f32[16,4096]{1,0:T(8,128)}, u32[]{:S(2)}, u32[]{:S(2)}) collective-permute-start(f32[16,4096]{1,0:T(8,128)S(1)} %slice.37), channel_id=1, source_target_pairs={{0,32},{32,64},{64,96},{96,0},{1,33},{33,65},{65,97},{97,1},{2,34}... | collective-permute-start | bytes 786440 | tf_op jit(solution)/shard_map/ppermute | solution.py:23
  109.5 14.0 %collective-permute-start.14 = (f32[16,4096]{1,0:T(8,128)}, f32[16,4096]{1,0:T(8,128)}, u32[]{:S(2)}, u32[]{:S(2)}) collective-permute-start(f32[16,4096]{1,0:T(8,128)} %slice.36), channel_id=1, source_target_pairs={{0,96},{32,0},{64,32},{96,64},{1,97},{33,1},{65,33},{97,65},{2,98}... | collective-permute-start | bytes 786440 | tf_op jit(solution)/shard_map/ppermute | solution.py:23
  (7 other events, 98.8 us)

commit v7 on v5

--- a/solution.py
+++ b/solution.py
@@ -57,49 +57,66 @@
     far_down = shift(down[1], "z", 1)
     by_offset[half] = jnp.stack([far_up, far_down])
     mine = jnp.stack(by_offset)
-    return jnp.stack([mine, swap(mine, "core")])
+    return mine, swap(mine, "core")
 
 
-def product_kernel(index_ref, rows_ref, a_ref, table_ref, out_ref, acc_ref):
+def product_kernel(index_ref, rows_ref, a_ref, mine_ref, other_ref, out_ref, acc_ref):
     acc_ref[...] = jnp.zeros_like(acc_ref)
     blocks = out_ref.shape[0]
+    stripes = mine_ref.shape[0]
+    blk = a_ref.shape[1]
 
-    def one_slot(g, carry):
-        row = jnp.minimum(rows_ref[g], blocks)
-        left = a_ref[g]
-        right = table_ref[index_ref[g]]
-        left_hi = left.astype(jnp.bfloat16)
-        left_lo = (left - left_hi.astype(jnp.float32)).astype(jnp.bfloat16)
-        right_hi = right.astype(jnp.bfloat16)
-        right_lo = (right - right_hi.astype(jnp.float32)).astype(jnp.bfloat16)
-        term = jnp.dot(left_hi, right_hi, preferred_element_type=jnp.float32)
-        term += jnp.dot(left_hi, right_lo, preferred_element_type=jnp.float32)
-        term += jnp.dot(left_lo, right_hi, preferred_element_type=jnp.float32)
-        acc_ref[row] += term
+    def one_pair(t, carry):
+        pair = a_ref[t]
+        pair_hi = pair.astype(jnp.bfloat16)
+        pair_lo = (pair - pair_hi.astype(jnp.float32)).astype(jnp.bfloat16)
+        for u in range(2):
+            g = 2 * t + u
+            row = jnp.minimum(rows_ref[g], blocks)
+            index = index_ref[g]
+            local = index % stripes
+            right = jnp.where(index < stripes, mine_ref[local], other_ref[local])
+            right_hi = right.astype(jnp.bfloat16)
+            right_lo = (right - right_hi.astype(jnp.float32)).astype(jnp.bfloat16)
+            zeros = jnp.zeros_like(right_hi)
+            pieces_hi = [right_hi, zeros] if u == 0 else [zeros, right_hi]
+            pieces_lo = [right_lo, zeros] if u == 0 else [zeros, right_lo]
+            right_hi = jnp.concatenate(pieces_hi, axis=0)
+            right_lo = jnp.concatenate(pieces_lo, axis=0)
+            term = jnp.dot(pair_hi, right_hi, preferred_element_type=jnp.float32)
+            term += jnp.dot(pair_hi, right_lo, preferred_element_type=jnp.float32)
+            term += jnp.dot(pair_lo, right_hi, preferred_element_type=jnp.float32)
+            acc_ref[row] += term
         return carry
 
-    lax.fori_loop(0, a_ref.shape[0], one_slot, 0, unroll=8)
+    lax.fori_loop(0, a_ref.shape[0], one_pair, 0, unroll=4)
     out_ref[...] = acc_ref[:blocks]
 
 
-def product(index, rows, left, table):
-    slots, blk, _ = left.shape
-    columns = table.shape[2]
+def product(index, rows, pairs, mine, other):
+    n_pairs, blk, _ = pairs.shape
+    columns = mine.shape[2]
     vmem = pl.BlockSpec(memory_space=pltpu.VMEM)
     smem = pl.BlockSpec(memory_space=pltpu.SMEM)
     return pl.pallas_call(
         product_kernel,
         out_shape=jax.ShapeDtypeStruct((MB, blk, columns), jnp.float32),
-        in_specs=[smem, smem, vmem, vmem],
+        in_specs=[smem, smem, vmem, vmem, vmem],
         out_specs=vmem,
         scratch_shapes=[pltpu.VMEM((MB + 1, blk, columns), jnp.float32)],
         compiler_params=pltpu.CompilerParams(vmem_limit_bytes=48 * 1024 * 1024),
         cost_estimate=pl.CostEstimate(
-            flops=2 * slots * blk * blk * columns,
-            bytes_accessed=4 * (left.size + table.size + MB * blk * columns),
+            flops=2 * 2 * n_pairs * blk * blk * columns,
+            bytes_accessed=4 * (pairs.size + 2 * mine.size + MB * blk * columns),
             transcendentals=0,
         ),
-    )(index, rows, left, table)
+    )(index, rows, pairs, mine, other)
+
+
+def as_pairs(panel):
+    slots = panel.shape[0]
+    blocks = panel.reshape(slots // 2, 2, BLK, BLK)
+    return jnp.swapaxes(blocks, 1, 2).reshape(slots // 2, BLK, 2 * BLK)
 
 
 def shards(a_blocks, a_rows, a_slots, b_stripes):
@@ -109,9 +126,10 @@
 
     ints = jnp.stack([a_rows[0, 0], a_slots[0, 0]])
     ints_k, _ = gather_a(ints)
-    a_all, pid = gather_a(a_blocks[0, 0])
-    table = gather_b(b_stripes)
-    table = table.reshape(-1, BLK, columns)
+    a_all, pid = gather_a(as_pairs(a_blocks[0, 0]))
+    mine, other = gather_b(b_stripes)
+    mine = mine.reshape(-1, BLK, columns)
+    other = other.reshape(-1, BLK, columns)
 
     rows = ints_k[:, 0]
     slots = ints_k[:, 1]
@@ -119,8 +137,8 @@
     core_rel = (slots // 6) % 2 ^ lax.axis_index("core")
     xh_rel = (slots // 12) ^ lax.axis_index("xh")
     index = ((core_rel * n_z + d) * 2 + xh_rel) * 6 + slots % 6
-    left = a_all.reshape(-1, BLK, BLK)
-    out = product(index.reshape(-1), rows.reshape(-1), left, table)
+    pairs = a_all.reshape(-1, BLK, 2 * BLK)
+    out = product(index.reshape(-1), rows.reshape(-1), pairs, mine, other)
     return out.reshape(MB * BLK, columns)
 
 

time: 113 us -> 121 us (1.071)
  waiting for transfers between devices: 40 us -> 52 us
  other arithmetic: 10.2 us -> 3.05 us
  local copies, waits for them, and re-layouts: 16.4 us -> 18.4 us
  starting transfers between devices: 31 us -> 32.6 us
    ppermute x16, waiting for transfers between devices: 40 us -> 52 us  [shift(): lax.ppermute(block, axis, [(i, (i + distance) % n) for i in range(n)])]
    reshape x1, local copies, waits for them, and re-layouts: 7.88 us -> 1.39 us  [as_pairs(): return jnp.swapaxes(blocks, 1, 2).reshape(slots // 2, BLK, 2 * BLK)]
    another operation x1 -> x0, other arithmetic: 5.43 us -> none  [gather_b(): return jnp.stack([mine, swap(mine, 'core')])]
    unnamed x14 -> x24, local copies, waits for them, and re-layouts: 6.88 us -> 9.42 us
    ppermute x16, starting transfers between devices: 26.2 us -> 28.4 us  [shift(): lax.ppermute(block, axis, [(i, (i + distance) % n) for i in range(n)])]
    unnamed x3, other arithmetic: 1.66 us -> 0.06 us
    another operation x1 -> x2, local copies, waits for them, and re-layouts: 0.08 us -> 1.53 us  [the longest x1 1.45 us: as_pairs(): blocks = panel.reshape(slots // 2, 2, BLK, BLK)]
  transfers between devices with their start and end apart: 20 -> 20, of which waited for: 12 -> 10; matrix products, arithmetic and copies ran while one was open for 18% -> 18% of each run, Pallas kernels for 0% -> 0%
where the time goes in v7:
time: 121 us
  waiting for transfers between devices  52 us (43%)
  starting transfers between devices  32.6 us (27%)
  local copies, waits for them, and re-layouts  18.4 us (15%)
  Pallas kernels  14.6 us (12%)
  other arithmetic  3.05 us (3%)
    ppermute x16, waiting for transfers between devices, shift(): lax.ppermute(block, axis, [(i, (i + distance) % n) for i in range(n)])  52 us
    ppermute x16, starting transfers between devices, shift(): lax.ppermute(block, axis, [(i, (i + distance) % n) for i in range(n)])  28.4 us
    pallas_call x1, Pallas kernels, product(): pl.pallas_call(product_kernel, out_shape=jax.ShapeDtypeStruct((MB, blk, c...  14.6 us
    unnamed x24, local copies, waits for them, and re-layouts  9.42 us
    ppermute x4, starting transfers between devices, swap(): return lax.ppermute(block, axis, [(0, 1), (1, 0)])  4.24 us
  transfers between devices with their start and end apart: 20, of which 10 were waited for; matrix products, arithmetic and copies ran while one was open for 18% of the time, Pallas kernels for 0%

profile of v7, /device:TPU:2, one launch (start us, length us, event | category | flops | bytes accessed | tf_op | source)
XLA Modules:
  0.0 121.0 jit_solution(14879338636552956247)
XLA Ops:
  0.0 2.1 %collective-permute-start.10 = (f32[6,64,128]{2,1,0:T(8,128)}, f32[6,64,128]{2,1,0:T(8,128)S(1)}, u32[]{:S(2)}, u32[]{:S(2)}) collective-permute-start(f32[6,64,128]{2,1,0:T(8,128)} %param.7), channel_id=1, source_target_pairs={{0,2},{2,0},{1,3},{3,1},{4,6},{6,4},{5,7},{7,5},{8,10},{10,8},{9,1... | collective-permute-start | bytes 589832 | tf_op jit(solution)/shard_map/ppermute | solution.py:18
  2.8 1.4 %collective-permute-start = (s32[2,32]{1,0:T(2,128)S(1)}, s32[2,32]{1,0:T(2,128)S(1)}, u32[]{:S(2)}, u32[]{:S(2)}) collective-permute-start(s32[2,32]{1,0:T(2,128)S(1)} %get-tuple-element.12), channel_id=1, source_target_pairs={{0,128},{128,0},{1,129},{129,1},{2,130},{130,2},{3,131},{131,3},{4... | collective-permute-start | bytes 776 | tf_op jit(solution)/shard_map/ppermute | solution.py:18
  4.2 1.5 %reshape_squeeze.7 = f32[16,2,64,64]{3,2,1,0:T(8,128)S(1)} reshape(f32[1,1,32,4096]{3,2,1,0:T(8,128)} %param.4) | data formatting | bytes 1048576 | tf_op jit(solution)/shard_map/reshape;squeeze | solution.py:118
  8.7 5.9 %collective-permute-start.11 = (f32[2,6,64,128]{3,2,1,0:T(8,128)S(1)}, f32[2,6,64,128]{3,2,1,0:T(8,128)}, u32[]{:S(2)}, u32[]{:S(2)}) collective-permute-start(f32[2,6,64,128]{3,2,1,0:T(8,128)S(1)} %pad_maximum_fusion.1), channel_id=1, source_target_pairs={{0,28},{4,0},{8,4},{12,8},{16,12},{20,16},{24,20},{28,24},{1,29},{... | collective-permute-start | bytes 1179656 | tf_op jit(solution)/shard_map/ppermute | solution.py:23
  16.2 9.4 %collective-permute-done.15 = f32[2,6,64,128]{3,2,1,0:T(8,128)} collective-permute-done((f32[2,6,64,128]{3,2,1,0:T(8,128)S(1)}, f32[2,6,64,128]{3,2,1,0:T(8,128)}, u32[]{:S(2)}, u32[]{:S(2)}) %collective-permute-start.15) | collective-permute-done | bytes 393248 | tf_op jit(solution)/shard_map/ppermute | solution.py:23
  25.7 1.7 %collective-permute-start.1 = (s32[2,2,32]{2,1,0:T(2,128)S(1)}, s32[2,2,32]{2,1,0:T(2,128)S(1)}, u32[]{:S(2)}, u32[]{:S(2)}) collective-permute-start(s32[2,2,32]{2,1,0:T(2,128)S(1)} %pad_add_fusion), channel_id=1, source_target_pairs={{0,32},{32,64},{64,96},{96,0},{1,33},{33,65},{65,97},{97,1},{2,34}... | collective-permute-start | bytes 1544 | tf_op jit(solution)/shard_map/ppermute | solution.py:23
  27.3 1.7 %collective-permute-start.2 = (s32[2,2,32]{2,1,0:T(2,128)S(1)}, s32[2,2,32]{2,1,0:T(2,128)S(1)}, u32[]{:S(2)}, u32[]{:S(2)}) collective-permute-start(s32[2,2,32]{2,1,0:T(2,128)S(1)} %pad_add_fusion), channel_id=1, source_target_pairs={{0,96},{32,0},{64,32},{96,64},{1,97},{33,1},{65,33},{97,65},{2,98}... | collective-permute-start | bytes 1544 | tf_op jit(solution)/shard_map/ppermute | solution.py:23
  29.0 3.2 %collective-permute-start.12 = (f32[2,6,64,128]{3,2,1,0:T(8,128)}, f32[2,6,64,128]{3,2,1,0:T(8,128)S(1)}, u32[]{:S(2)}, u32[]{:S(2)}) collective-permute-start(f32[2,6,64,128]{3,2,1,0:T(8,128)} %collective-permute-done.11), channel_id=1, source_target_pairs={{0,28},{4,0},{8,4},{12,8},{16,12},{20,16},{24,20},{28,24},{1,29},{... | collective-permute-start | bytes 1179656 | tf_op jit(solution)/shard_map/ppermute | solution.py:23
  32.2 3.8 %collective-permute-done.16 = f32[2,6,64,128]{3,2,1,0:T(8,128)S(1)} collective-permute-done((f32[2,6,64,128]{3,2,1,0:T(8,128)}, f32[2,6,64,128]{3,2,1,0:T(8,128)S(1)}, u32[]{:S(2)}, u32[]{:S(2)}) %collective-permute-start.16) | collective-permute-done | bytes 393248 | tf_op jit(solution)/shard_map/ppermute | solution.py:23
  38.3 3.5 %collective-permute-start.13 = (f32[2,6,64,128]{3,2,1,0:T(8,128)S(1)}, f32[2,6,64,128]{3,2,1,0:T(8,128)S(1)}, u32[]{:S(2)}, u32[]{:S(2)}) collective-permute-start(f32[2,6,64,128]{3,2,1,0:T(8,128)S(1)} %collective-permute-done.12), channel_id=1, source_target_pairs={{0,28},{4,0},{8,4},{12,8},{16,12},{20,16},{24,20},{28,24},{1,29},{... | collective-permute-start | bytes 1179656 | tf_op jit(solution)/shard_map/ppermute | solution.py:23
  41.8 3.4 %collective-permute-done.17 = f32[2,6,64,128]{3,2,1,0:T(8,128)S(1)} collective-permute-done((f32[2,6,64,128]{3,2,1,0:T(8,128)S(1)}, f32[2,6,64,128]{3,2,1,0:T(8,128)S(1)}, u32[]{:S(2)}, u32[]{:S(2)}) %collective-permute-start.17) | collective-permute-done | bytes 393248 | tf_op jit(solution)/shard_map/ppermute | solution.py:23
  45.3 2.5 %collective-permute-done.13 = f32[2,6,64,128]{3,2,1,0:T(8,128)S(1)} collective-permute-done((f32[2,6,64,128]{3,2,1,0:T(8,128)S(1)}, f32[2,6,64,128]{3,2,1,0:T(8,128)S(1)}, u32[]{:S(2)}, u32[]{:S(2)}) %collective-permute-start.13) | collective-permute-done | bytes 393248 | tf_op jit(solution)/shard_map/ppermute | solution.py:23
  47.8 3.9 %collective-permute-start.14 = (f32[6,64,128]{2,1,0:T(8,128)S(1)}, f32[6,64,128]{2,1,0:T(8,128)S(1)}, u32[]{:S(2)}, u32[]{:S(2)}) collective-permute-start(f32[6,64,128]{2,1,0:T(8,128)S(1)} %slice_bitcast_fusion.3), channel_id=1, source_target_pairs={{0,28},{4,0},{8,4},{12,8},{16,12},{20,16},{24,20},{28,24},{1,29},{... | collective-permute-start | bytes 589832 | tf_op jit(solution)/shard_map/ppermute | solution.py:23
  52.2 2.8 %collective-permute-done.14 = f32[6,64,128]{2,1,0:T(8,128)S(1)} collective-permute-done((f32[6,64,128]{2,1,0:T(8,128)S(1)}, f32[6,64,128]{2,1,0:T(8,128)S(1)}, u32[]{:S(2)}, u32[]{:S(2)}) %collective-permute-start.14) | collective-permute-done | bytes 196640 | tf_op jit(solution)/shard_map/ppermute | solution.py:23
  58.3 2.1 %pad_maximum_fusion = f32[2,16,64,128]{3,2,1,0:T(8,128)} fusion(f32[1,16,64,128]{3,2,1,0:T(8,128)} %bitcast.17, f32[1,16,64,128]{3,2,1,0:T(8,128)S(1)} %copy-done.1), kind=kLoop, calls=%fused_computation | loop fusion | flops 262144 | bytes 2097152 | tf_op jit(solution)/shard_map/stack | solution.py:31
  60.5 2.5 %collective-permute-start.7 = (f32[2,16,64,128]{3,2,1,0:T(8,128)}, f32[2,16,64,128]{3,2,1,0:T(8,128)}, u32[]{:S(2)}, u32[]{:S(2)}) collective-permute-start(f32[2,16,64,128]{3,2,1,0:T(8,128)} %pad_maximum_fusion), channel_id=1, source_target_pairs={{0,96},{32,0},{64,32},{96,64},{1,97},{33,1},{65,33},{97,65},{2,98}... | collective-permute-start | bytes 3145736 | tf_op jit(solution)/shard_map/ppermute | solution.py:23
  63.7 1.9 %constant_dynamic-update-slice_fusion.8 = f32[8,16,64,128]{3,2,1,0:T(8,128)} fusion(f32[8,16,64,128]{3,2,1,0:T(8,128)} %constant_dynamic-update-slice_fusion.9, f32[16,64,128]{2,1,0:T(8,128)} %collective-permute-done.5), kind=kLoop, calls=%fused_computation.25 | loop fusion | bytes 1048576
  65.6 20.2 %collective-permute-done.7 = f32[2,16,64,128]{3,2,1,0:T(8,128)} collective-permute-done((f32[2,16,64,128]{3,2,1,0:T(8,128)}, f32[2,16,64,128]{3,2,1,0:T(8,128)}, u32[]{:S(2)}, u32[]{:S(2)}) %collective-permute-start.7) | collective-permute-done | bytes 1048608 | tf_op jit(solution)/shard_map/ppermute | solution.py:23
  86.8 3.8 %collective-permute-start.8 = (f32[16,64,128]{2,1,0:T(8,128)S(1)}, f32[16,64,128]{2,1,0:T(8,128)S(1)}, u32[]{:S(2)}, u32[]{:S(2)}) collective-permute-start(f32[16,64,128]{2,1,0:T(8,128)S(1)} %slice_bitcast_fusion.1), channel_id=1, source_target_pairs={{0,96},{32,0},{64,32},{96,64},{1,97},{33,1},{65,33},{97,65},{2,98}... | collective-permute-start | bytes 1572872 | tf_op jit(solution)/shard_map/ppermute | solution.py:23
  91.8 2.4 %constant_dynamic-update-slice_fusion.7 = f32[8,16,64,128]{3,2,1,0:T(8,128)} fusion(f32[8,16,64,128]{3,2,1,0:T(8,128)} %constant_dynamic-update-slice_fusion.8, f32[2,16,64,128]{3,2,1,0:T(8,128)} %collective-permute-done.6), kind=kLoop, calls=%fused_computation.24 | loop fusion | bytes 2097152
  94.1 2.3 %constant_dynamic-update-slice_fusion.6 = f32[8,16,64,128]{3,2,1,0:T(8,128)} fusion(f32[8,16,64,128]{3,2,1,0:T(8,128)} %constant_dynamic-update-slice_fusion.7, f32[2,16,64,128]{3,2,1,0:T(8,128)} %collective-permute-done.7), kind=kLoop, calls=%fused_computation.23 | loop fusion | bytes 2097152
  96.5 4.5 %collective-permute-done.8 = f32[16,64,128]{2,1,0:T(8,128)S(1)} collective-permute-done((f32[16,64,128]{2,1,0:T(8,128)S(1)}, f32[16,64,128]{2,1,0:T(8,128)S(1)}, u32[]{:S(2)}, u32[]{:S(2)}) %collective-permute-start.8) | collective-permute-done | bytes 524320 | tf_op jit(solution)/shard_map/ppermute | solution.py:23
  101.8 3.7 %collective-permute-done.9 = f32[16,64,128]{2,1,0:T(8,128)S(1)} collective-permute-done((f32[16,64,128]{2,1,0:T(8,128)S(1)}, f32[16,64,128]{2,1,0:T(8,128)S(1)}, u32[]{:S(2)}, u32[]{:S(2)}) %collective-permute-start.9) | collective-permute-done | bytes 524320 | tf_op jit(solution)/shard_map/ppermute | solution.py:23
  106.4 14.6 %shard_map.46 = f32[32,64,128]{2,1,0:T(8,128)} custom-call(s32[256]{0:T(256)S(1)} %fusion.6.index_ref, s32[256]{0:T(256)S(1)} %reshape_squeeze.6.rows_ref, f32[128,64,128]{2,1,0:T(8,128)} %bitcast.67, f32[96,64,128]{2,1,0:T(8,128)S(1)} %bitcast.66, f32[96,64,128]{2,1,0:T(8,128)} %bitcast.38.other_ref), custom_call_target="tpu_custom_call" | custom-call | flops 268435456 | bytes 11534336 | tf_op jit(solution)/shard_map/pallas_call | solution.py:101
  (74 shorter events, 16.0 us)
Async XLA Ops:
  0.0 8.6 %collective-permute-start.10 = (f32[6,64,128]{2,1,0:T(8,128)}, f32[6,64,128]{2,1,0:T(8,128)S(1)}, u32[]{:S(2)}, u32[]{:S(2)}) collective-permute-start(f32[6,64,128]{2,1,0:T(8,128)} %param.7), channel_id=1, source_target_pairs={{0,2},{2,0},{1,3},{3,1},{4,6},{6,4},{5,7},{7,5},{8,10},{10,8},{9,1... | collective-permute-start | bytes 589832 | tf_op jit(solution)/shard_map/ppermute | solution.py:18
  2.8 22.8 %collective-permute-start = (s32[2,32]{1,0:T(2,128)S(1)}, s32[2,32]{1,0:T(2,128)S(1)}, u32[]{:S(2)}, u32[]{:S(2)}) collective-permute-start(s32[2,32]{1,0:T(2,128)S(1)} %get-tuple-element.12), channel_id=1, source_target_pairs={{0,128},{128,0},{1,129},{129,1},{2,130},{130,2},{3,131},{131,3},{4... | collective-permute-start | bytes 776 | tf_op jit(solution)/shard_map/ppermute | solution.py:18
  5.7 9.7 %copy-start.3 = (s32[1,1,32]{2,1,0:T(1,128)S(1)}, s32[1,1,32]{2,1,0:T(1,128)}, u32[]{:S(2)}) copy-start(s32[1,1,32]{2,1,0:T(1,128)} %param.6) | copy-start | bytes 388
  5.7 9.6 %copy-start.4 = (s32[1,1,32]{2,1,0:T(1,128)S(1)}, s32[1,1,32]{2,1,0:T(1,128)}, u32[]{:S(2)}) copy-start(s32[1,1,32]{2,1,0:T(1,128)} %param.5) | copy-start | bytes 388
  7.9 50.4 %collective-permute-start.5 = (f32[16,64,128]{2,1,0:T(8,128)}, f32[16,64,128]{2,1,0:T(8,128)}, u32[]{:S(2)}, u32[]{:S(2)}) collective-permute-start(f32[16,64,128]{2,1,0:T(8,128)} %reshape.114), channel_id=1, source_target_pairs={{0,128},{128,0},{1,129},{129,1},{2,130},{130,2},{3,131},{131,3},{4... | collective-permute-start | bytes 1572872 | tf_op jit(solution)/shard_map/ppermute | solution.py:18
  8.7 20.3 %collective-permute-start.11 = (f32[2,6,64,128]{3,2,1,0:T(8,128)S(1)}, f32[2,6,64,128]{3,2,1,0:T(8,128)}, u32[]{:S(2)}, u32[]{:S(2)}) collective-permute-start(f32[2,6,64,128]{3,2,1,0:T(8,128)S(1)} %pad_maximum_fusion.1), channel_id=1, source_target_pairs={{0,28},{4,0},{8,4},{12,8},{16,12},{20,16},{24,20},{28,24},{1,29},{... | collective-permute-start | bytes 1179656 | tf_op jit(solution)/shard_map/ppermute | solution.py:23
  14.6 11.1 %collective-permute-start.15 = (f32[2,6,64,128]{3,2,1,0:T(8,128)S(1)}, f32[2,6,64,128]{3,2,1,0:T(8,128)}, u32[]{:S(2)}, u32[]{:S(2)}) collective-permute-start(f32[2,6,64,128]{3,2,1,0:T(8,128)S(1)} %pad_maximum_fusion.1), channel_id=1, source_target_pairs={{0,4},{4,8},{8,12},{12,16},{16,20},{20,24},{24,28},{28,0},{1,5},{5... | collective-permute-start | bytes 1179656 | tf_op jit(solution)/shard_map/ppermute | solution.py:23
  15.2 16.9 %copy-start = (f32[1,16,64,128]{3,2,1,0:T(8,128)}, f32[1,16,64,128]{3,2,1,0:T(8,128)S(1)}, u32[]{:S(2)}) copy-start(f32[1,16,64,128]{3,2,1,0:T(8,128)S(1)} %stack_reshape.4) | copy-start | bytes 1572868
  25.6 10.3 %collective-permute-start.16 = (f32[2,6,64,128]{3,2,1,0:T(8,128)}, f32[2,6,64,128]{3,2,1,0:T(8,128)S(1)}, u32[]{:S(2)}, u32[]{:S(2)}) collective-permute-start(f32[2,6,64,128]{3,2,1,0:T(8,128)} %collective-permute-done.15), channel_id=1, source_target_pairs={{0,4},{4,8},{8,12},{12,16},{16,20},{20,24},{24,28},{28,0},{1,5},{5... | collective-permute-start | bytes 1179656 | tf_op jit(solution)/shard_map/ppermute | solution.py:23
  25.7 32.0 %collective-permute-start.1 = (s32[2,2,32]{2,1,0:T(2,128)S(1)}, s32[2,2,32]{2,1,0:T(2,128)S(1)}, u32[]{:S(2)}, u32[]{:S(2)}) collective-permute-start(s32[2,2,32]{2,1,0:T(2,128)S(1)} %pad_add_fusion), channel_id=1, source_target_pairs={{0,32},{32,64},{64,96},{96,0},{1,33},{33,65},{65,97},{97,1},{2,34}... | collective-permute-start | bytes 1544 | tf_op jit(solution)/shard_map/ppermute | solution.py:23
  27.3 28.9 %collective-permute-start.2 = (s32[2,2,32]{2,1,0:T(2,128)S(1)}, s32[2,2,32]{2,1,0:T(2,128)S(1)}, u32[]{:S(2)}, u32[]{:S(2)}) collective-permute-start(s32[2,2,32]{2,1,0:T(2,128)S(1)} %pad_add_fusion), channel_id=1, source_target_pairs={{0,96},{32,0},{64,32},{96,64},{1,97},{33,1},{65,33},{97,65},{2,98}... | collective-permute-start | bytes 1544 | tf_op jit(solution)/shard_map/ppermute | solution.py:23
  29.0 9.3 %collective-permute-start.12 = (f32[2,6,64,128]{3,2,1,0:T(8,128)}, f32[2,6,64,128]{3,2,1,0:T(8,128)S(1)}, u32[]{:S(2)}, u32[]{:S(2)}) collective-permute-start(f32[2,6,64,128]{3,2,1,0:T(8,128)} %collective-permute-done.11), channel_id=1, source_target_pairs={{0,28},{4,0},{8,4},{12,8},{16,12},{20,16},{24,20},{28,24},{1,29},{... | collective-permute-start | bytes 1179656 | tf_op jit(solution)/shard_map/ppermute | solution.py:23
  32.2 26.2 %copy-start.1 = (f32[1,16,64,128]{3,2,1,0:T(8,128)S(1)}, f32[1,16,64,128]{3,2,1,0:T(8,128)}, u32[]{:S(2)}) copy-start(f32[1,16,64,128]{3,2,1,0:T(8,128)} %copy-done) | copy-start | bytes 1572868
  35.9 9.2 %collective-permute-start.17 = (f32[2,6,64,128]{3,2,1,0:T(8,128)S(1)}, f32[2,6,64,128]{3,2,1,0:T(8,128)S(1)}, u32[]{:S(2)}, u32[]{:S(2)}) collective-permute-start(f32[2,6,64,128]{3,2,1,0:T(8,128)S(1)} %collective-permute-done.16), channel_id=1, source_target_pairs={{0,4},{4,8},{8,12},{12,16},{16,20},{20,24},{24,28},{28,0},{1,5},{5... | collective-permute-start | bytes 1179656 | tf_op jit(solution)/shard_map/ppermute | solution.py:23
  38.3 9.5 %collective-permute-start.13 = (f32[2,6,64,128]{3,2,1,0:T(8,128)S(1)}, f32[2,6,64,128]{3,2,1,0:T(8,128)S(1)}, u32[]{:S(2)}, u32[]{:S(2)}) collective-permute-start(f32[2,6,64,128]{3,2,1,0:T(8,128)S(1)} %collective-permute-done.12), channel_id=1, source_target_pairs={{0,28},{4,0},{8,4},{12,8},{16,12},{20,16},{24,20},{28,24},{1,29},{... | collective-permute-start | bytes 1179656 | tf_op jit(solution)/shard_map/ppermute | solution.py:23
  45.2 7.0 %collective-permute-start.18 = (f32[6,64,128]{2,1,0:T(8,128)S(1)}, f32[6,64,128]{2,1,0:T(8,128)S(1)}, u32[]{:S(2)}, u32[]{:S(2)}) collective-permute-start(f32[6,64,128]{2,1,0:T(8,128)S(1)} %slice_bitcast_fusion.2), channel_id=1, source_target_pairs={{0,4},{4,8},{8,12},{12,16},{16,20},{20,24},{24,28},{28,0},{1,5},{5... | collective-permute-start | bytes 589832 | tf_op jit(solution)/shard_map/ppermute | solution.py:23
  47.8 7.1 %collective-permute-start.14 = (f32[6,64,128]{2,1,0:T(8,128)S(1)}, f32[6,64,128]{2,1,0:T(8,128)S(1)}, u32[]{:S(2)}, u32[]{:S(2)}) collective-permute-start(f32[6,64,128]{2,1,0:T(8,128)S(1)} %slice_bitcast_fusion.3), channel_id=1, source_target_pairs={{0,28},{4,0},{8,4},{12,8},{16,12},{20,16},{24,20},{28,24},{1,29},{... | collective-permute-start | bytes 589832 | tf_op jit(solution)/shard_map/ppermute | solution.py:23
  56.1 50.3 %collective-permute-start.19 = (f32[8,2,6,64,128]{4,3,2,1,0:T(8,128)S(1)}, f32[8,2,6,64,128]{4,3,2,1,0:T(8,128)}, u32[]{:S(2)}, u32[]{:S(2)}) collective-permute-start(f32[8,2,6,64,128]{4,3,2,1,0:T(8,128)S(1)} %bitcast_dynamic-update-slice_fusion.2), channel_id=1, source_target_pairs={{0,1},{1,0},{2,3},{3,2},{4,5},{5,4},{6,7},{7,6},{8,9},{9,8},{10,11... | collective-permute-start | bytes 9437192 | tf_op jit(solution)/shard_map/ppermute | solution.py:18
  56.2 6.8 %collective-permute-start.3 = (s32[2,32]{1,0:T(2,128)S(1)}, s32[2,32]{1,0:T(2,128)S(1)}, u32[]{:S(2)}, u32[]{:S(2)}) collective-permute-start(s32[2,32]{1,0:T(2,128)S(1)} %slice_bitcast_fusion.5), channel_id=1, source_target_pairs={{0,96},{32,0},{64,32},{96,64},{1,97},{33,1},{65,33},{97,65},{2,98}... | collective-permute-start | bytes 776 | tf_op jit(solution)/shard_map/ppermute | solution.py:23
  57.6 5.4 %collective-permute-start.4 = (s32[2,32]{1,0:T(2,128)S(1)}, s32[2,32]{1,0:T(2,128)S(1)}, u32[]{:S(2)}, u32[]{:S(2)}) collective-permute-start(s32[2,32]{1,0:T(2,128)S(1)} %slice_bitcast_fusion.4), channel_id=1, source_target_pairs={{0,32},{32,64},{64,96},{96,0},{1,33},{33,65},{65,97},{97,1},{2,34}... | collective-permute-start | bytes 776 | tf_op jit(solution)/shard_map/ppermute | solution.py:23
  60.5 25.3 %collective-permute-start.7 = (f32[2,16,64,128]{3,2,1,0:T(8,128)}, f32[2,16,64,128]{3,2,1,0:T(8,128)}, u32[]{:S(2)}, u32[]{:S(2)}) collective-permute-start(f32[2,16,64,128]{3,2,1,0:T(8,128)} %pad_maximum_fusion), channel_id=1, source_target_pairs={{0,96},{32,0},{64,32},{96,64},{1,97},{33,1},{65,33},{97,65},{2,98}... | collective-permute-start | bytes 3145736 | tf_op jit(solution)/shard_map/ppermute | solution.py:23
  63.0 27.6 %collective-permute-start.6 = (f32[2,16,64,128]{3,2,1,0:T(8,128)}, f32[2,16,64,128]{3,2,1,0:T(8,128)}, u32[]{:S(2)}, u32[]{:S(2)}) collective-permute-start(f32[2,16,64,128]{3,2,1,0:T(8,128)} %pad_maximum_fusion), channel_id=1, source_target_pairs={{0,32},{32,64},{64,96},{96,0},{1,33},{33,65},{65,97},{97,1},{2,34}... | collective-permute-start | bytes 3145736 | tf_op jit(solution)/shard_map/ppermute | solution.py:23
  86.8 14.1 %collective-permute-start.8 = (f32[16,64,128]{2,1,0:T(8,128)S(1)}, f32[16,64,128]{2,1,0:T(8,128)S(1)}, u32[]{:S(2)}, u32[]{:S(2)}) collective-permute-start(f32[16,64,128]{2,1,0:T(8,128)S(1)} %slice_bitcast_fusion.1), channel_id=1, source_target_pairs={{0,96},{32,0},{64,32},{96,64},{1,97},{33,1},{65,33},{97,65},{2,98}... | collective-permute-start | bytes 1572872 | tf_op jit(solution)/shard_map/ppermute | solution.py:23
  91.7 13.8 %collective-permute-start.9 = (f32[16,64,128]{2,1,0:T(8,128)S(1)}, f32[16,64,128]{2,1,0:T(8,128)S(1)}, u32[]{:S(2)}, u32[]{:S(2)}) collective-permute-start(f32[16,64,128]{2,1,0:T(8,128)S(1)} %slice_bitcast_fusion), channel_id=1, source_target_pairs={{0,32},{32,64},{64,96},{96,0},{1,33},{33,65},{65,97},{97,1},{2,34}... | collective-permute-start | bytes 1572872 | tf_op jit(solution)/shard_map/ppermute | solution.py:23
  (1 other events, 8.6 us)

commit v8 on v7

--- a/solution.py
+++ b/solution.py
@@ -4,6 +4,7 @@
 from jax.experimental import pallas as pl
 from jax.experimental.pallas import tpu as pltpu
 from jax.sharding import Mesh
+
 from jax.sharding import PartitionSpec as P
 
 BLK = 64
@@ -64,7 +65,6 @@
     acc_ref[...] = jnp.zeros_like(acc_ref)
     blocks = out_ref.shape[0]
     stripes = mine_ref.shape[0]
-    blk = a_ref.shape[1]
 
     def one_pair(t, carry):
         pair = a_ref[t]
@@ -119,7 +119,7 @@
     return jnp.swapaxes(blocks, 1, 2).reshape(slots // 2, BLK, 2 * BLK)
 
 
-def shards(a_blocks, a_rows, a_slots, b_stripes):
+def shards_body(a_blocks, a_rows, a_slots, b_stripes):
     n_z = lax.axis_size("z")
     z = lax.axis_index("z")
     columns = b_stripes.shape[2]
@@ -145,7 +145,7 @@
 def solution(mesh):
     fine = Mesh(mesh.devices.reshape(2, 4, 8, 2, 2), AXES)
     return jax.shard_map(
-        shards,
+        shards_body,
         mesh=fine,
         in_specs=(
             P(COL, ROW, None, None),

time: 121 us -> 121 us (level)
  no operation moved by 1% of the time
where the time goes in v8:
time: 121 us
  waiting for transfers between devices  52 us (43%)
  starting transfers between devices  32.6 us (27%)
  local copies, waits for them, and re-layouts  18.4 us (15%)
  Pallas kernels  14.7 us (12%)
  other arithmetic  3.05 us (3%)
    ppermute x16, waiting for transfers between devices, shift(): lax.ppermute(block, axis, [(i, (i + distance) % n) for i in range(n)])  52 us
    ppermute x16, starting transfers between devices, shift(): lax.ppermute(block, axis, [(i, (i + distance) % n) for i in range(n)])  28.4 us
    pallas_call x1, Pallas kernels, product(): pl.pallas_call(product_kernel, out_shape=jax.ShapeDtypeStruct((MB, blk, c...  14.7 us
    unnamed x24, local copies, waits for them, and re-layouts  9.42 us
    ppermute x4, starting transfers between devices, swap(): return lax.ppermute(block, axis, [(0, 1), (1, 0)])  4.24 us
  transfers between devices with their start and end apart: 20, of which 10 were waited for; matrix products, arithmetic and copies ran while one was open for 18% of the time, Pallas kernels for 0%

profile of v8, /device:TPU:2, one launch (start us, length us, event | category | flops | bytes accessed | tf_op | source)
XLA Modules:
  0.0 121.0 jit_solution(14879338636552956247)
XLA Ops:
  0.0 2.1 %collective-permute-start.10 = (f32[6,64,128]{2,1,0:T(8,128)}, f32[6,64,128]{2,1,0:T(8,128)S(1)}, u32[]{:S(2)}, u32[]{:S(2)}) collective-permute-start(f32[6,64,128]{2,1,0:T(8,128)} %param.7), channel_id=1, source_target_pairs={{0,2},{2,0},{1,3},{3,1},{4,6},{6,4},{5,7},{7,5},{8,10},{10,8},{9,1... | collective-permute-start | bytes 589832 | tf_op jit(solution)/shard_map/ppermute | solution.py:19
  2.8 1.4 %collective-permute-start = (s32[2,32]{1,0:T(2,128)S(1)}, s32[2,32]{1,0:T(2,128)S(1)}, u32[]{:S(2)}, u32[]{:S(2)}) collective-permute-start(s32[2,32]{1,0:T(2,128)S(1)} %get-tuple-element.12), channel_id=1, source_target_pairs={{0,128},{128,0},{1,129},{129,1},{2,130},{130,2},{3,131},{131,3},{4... | collective-permute-start | bytes 776 | tf_op jit(solution)/shard_map/ppermute | solution.py:19
  4.2 1.5 %reshape_squeeze.7 = f32[16,2,64,64]{3,2,1,0:T(8,128)S(1)} reshape(f32[1,1,32,4096]{3,2,1,0:T(8,128)} %param.4) | data formatting | bytes 1048576 | tf_op jit(solution)/shard_map/reshape;squeeze | solution.py:118
  8.7 5.9 %collective-permute-start.11 = (f32[2,6,64,128]{3,2,1,0:T(8,128)S(1)}, f32[2,6,64,128]{3,2,1,0:T(8,128)}, u32[]{:S(2)}, u32[]{:S(2)}) collective-permute-start(f32[2,6,64,128]{3,2,1,0:T(8,128)S(1)} %pad_maximum_fusion.1), channel_id=1, source_target_pairs={{0,28},{4,0},{8,4},{12,8},{16,12},{20,16},{24,20},{28,24},{1,29},{... | collective-permute-start | bytes 1179656 | tf_op jit(solution)/shard_map/ppermute | solution.py:24
  16.2 9.4 %collective-permute-done.15 = f32[2,6,64,128]{3,2,1,0:T(8,128)} collective-permute-done((f32[2,6,64,128]{3,2,1,0:T(8,128)S(1)}, f32[2,6,64,128]{3,2,1,0:T(8,128)}, u32[]{:S(2)}, u32[]{:S(2)}) %collective-permute-start.15) | collective-permute-done | bytes 393248 | tf_op jit(solution)/shard_map/ppermute | solution.py:24
  25.7 1.7 %collective-permute-start.1 = (s32[2,2,32]{2,1,0:T(2,128)S(1)}, s32[2,2,32]{2,1,0:T(2,128)S(1)}, u32[]{:S(2)}, u32[]{:S(2)}) collective-permute-start(s32[2,2,32]{2,1,0:T(2,128)S(1)} %pad_add_fusion), channel_id=1, source_target_pairs={{0,32},{32,64},{64,96},{96,0},{1,33},{33,65},{65,97},{97,1},{2,34}... | collective-permute-start | bytes 1544 | tf_op jit(solution)/shard_map/ppermute | solution.py:24
  27.3 1.7 %collective-permute-start.2 = (s32[2,2,32]{2,1,0:T(2,128)S(1)}, s32[2,2,32]{2,1,0:T(2,128)S(1)}, u32[]{:S(2)}, u32[]{:S(2)}) collective-permute-start(s32[2,2,32]{2,1,0:T(2,128)S(1)} %pad_add_fusion), channel_id=1, source_target_pairs={{0,96},{32,0},{64,32},{96,64},{1,97},{33,1},{65,33},{97,65},{2,98}... | collective-permute-start | bytes 1544 | tf_op jit(solution)/shard_map/ppermute | solution.py:24
  29.0 3.2 %collective-permute-start.12 = (f32[2,6,64,128]{3,2,1,0:T(8,128)}, f32[2,6,64,128]{3,2,1,0:T(8,128)S(1)}, u32[]{:S(2)}, u32[]{:S(2)}) collective-permute-start(f32[2,6,64,128]{3,2,1,0:T(8,128)} %collective-permute-done.11), channel_id=1, source_target_pairs={{0,28},{4,0},{8,4},{12,8},{16,12},{20,16},{24,20},{28,24},{1,29},{... | collective-permute-start | bytes 1179656 | tf_op jit(solution)/shard_map/ppermute | solution.py:24
  32.2 3.8 %collective-permute-done.16 = f32[2,6,64,128]{3,2,1,0:T(8,128)S(1)} collective-permute-done((f32[2,6,64,128]{3,2,1,0:T(8,128)}, f32[2,6,64,128]{3,2,1,0:T(8,128)S(1)}, u32[]{:S(2)}, u32[]{:S(2)}) %collective-permute-start.16) | collective-permute-done | bytes 393248 | tf_op jit(solution)/shard_map/ppermute | solution.py:24
  38.3 3.5 %collective-permute-start.13 = (f32[2,6,64,128]{3,2,1,0:T(8,128)S(1)}, f32[2,6,64,128]{3,2,1,0:T(8,128)S(1)}, u32[]{:S(2)}, u32[]{:S(2)}) collective-permute-start(f32[2,6,64,128]{3,2,1,0:T(8,128)S(1)} %collective-permute-done.12), channel_id=1, source_target_pairs={{0,28},{4,0},{8,4},{12,8},{16,12},{20,16},{24,20},{28,24},{1,29},{... | collective-permute-start | bytes 1179656 | tf_op jit(solution)/shard_map/ppermute | solution.py:24
  41.8 3.4 %collective-permute-done.17 = f32[2,6,64,128]{3,2,1,0:T(8,128)S(1)} collective-permute-done((f32[2,6,64,128]{3,2,1,0:T(8,128)S(1)}, f32[2,6,64,128]{3,2,1,0:T(8,128)S(1)}, u32[]{:S(2)}, u32[]{:S(2)}) %collective-permute-start.17) | collective-permute-done | bytes 393248 | tf_op jit(solution)/shard_map/ppermute | solution.py:24
  45.3 2.5 %collective-permute-done.13 = f32[2,6,64,128]{3,2,1,0:T(8,128)S(1)} collective-permute-done((f32[2,6,64,128]{3,2,1,0:T(8,128)S(1)}, f32[2,6,64,128]{3,2,1,0:T(8,128)S(1)}, u32[]{:S(2)}, u32[]{:S(2)}) %collective-permute-start.13) | collective-permute-done | bytes 393248 | tf_op jit(solution)/shard_map/ppermute | solution.py:24
  47.8 3.9 %collective-permute-start.14 = (f32[6,64,128]{2,1,0:T(8,128)S(1)}, f32[6,64,128]{2,1,0:T(8,128)S(1)}, u32[]{:S(2)}, u32[]{:S(2)}) collective-permute-start(f32[6,64,128]{2,1,0:T(8,128)S(1)} %slice_bitcast_fusion.3), channel_id=1, source_target_pairs={{0,28},{4,0},{8,4},{12,8},{16,12},{20,16},{24,20},{28,24},{1,29},{... | collective-permute-start | bytes 589832 | tf_op jit(solution)/shard_map/ppermute | solution.py:24
  52.2 2.8 %collective-permute-done.14 = f32[6,64,128]{2,1,0:T(8,128)S(1)} collective-permute-done((f32[6,64,128]{2,1,0:T(8,128)S(1)}, f32[6,64,128]{2,1,0:T(8,128)S(1)}, u32[]{:S(2)}, u32[]{:S(2)}) %collective-permute-start.14) | collective-permute-done | bytes 196640 | tf_op jit(solution)/shard_map/ppermute | solution.py:24
  58.3 2.1 %pad_maximum_fusion = f32[2,16,64,128]{3,2,1,0:T(8,128)} fusion(f32[1,16,64,128]{3,2,1,0:T(8,128)} %bitcast.17, f32[1,16,64,128]{3,2,1,0:T(8,128)S(1)} %copy-done.1), kind=kLoop, calls=%fused_computation | loop fusion | flops 262144 | bytes 2097152 | tf_op jit(solution)/shard_map/stack | solution.py:32
  60.5 2.5 %collective-permute-start.7 = (f32[2,16,64,128]{3,2,1,0:T(8,128)}, f32[2,16,64,128]{3,2,1,0:T(8,128)}, u32[]{:S(2)}, u32[]{:S(2)}) collective-permute-start(f32[2,16,64,128]{3,2,1,0:T(8,128)} %pad_maximum_fusion), channel_id=1, source_target_pairs={{0,96},{32,0},{64,32},{96,64},{1,97},{33,1},{65,33},{97,65},{2,98}... | collective-permute-start | bytes 3145736 | tf_op jit(solution)/shard_map/ppermute | solution.py:24
  63.7 1.9 %constant_dynamic-update-slice_fusion.8 = f32[8,16,64,128]{3,2,1,0:T(8,128)} fusion(f32[8,16,64,128]{3,2,1,0:T(8,128)} %constant_dynamic-update-slice_fusion.9, f32[16,64,128]{2,1,0:T(8,128)} %collective-permute-done.5), kind=kLoop, calls=%fused_computation.25 | loop fusion | bytes 1048576
  65.6 20.2 %collective-permute-done.7 = f32[2,16,64,128]{3,2,1,0:T(8,128)} collective-permute-done((f32[2,16,64,128]{3,2,1,0:T(8,128)}, f32[2,16,64,128]{3,2,1,0:T(8,128)}, u32[]{:S(2)}, u32[]{:S(2)}) %collective-permute-start.7) | collective-permute-done | bytes 1048608 | tf_op jit(solution)/shard_map/ppermute | solution.py:24
  86.8 3.8 %collective-permute-start.8 = (f32[16,64,128]{2,1,0:T(8,128)S(1)}, f32[16,64,128]{2,1,0:T(8,128)S(1)}, u32[]{:S(2)}, u32[]{:S(2)}) collective-permute-start(f32[16,64,128]{2,1,0:T(8,128)S(1)} %slice_bitcast_fusion.1), channel_id=1, source_target_pairs={{0,96},{32,0},{64,32},{96,64},{1,97},{33,1},{65,33},{97,65},{2,98}... | collective-permute-start | bytes 1572872 | tf_op jit(solution)/shard_map/ppermute | solution.py:24
  91.8 2.4 %constant_dynamic-update-slice_fusion.7 = f32[8,16,64,128]{3,2,1,0:T(8,128)} fusion(f32[8,16,64,128]{3,2,1,0:T(8,128)} %constant_dynamic-update-slice_fusion.8, f32[2,16,64,128]{3,2,1,0:T(8,128)} %collective-permute-done.6), kind=kLoop, calls=%fused_computation.24 | loop fusion | bytes 2097152
  94.1 2.3 %constant_dynamic-update-slice_fusion.6 = f32[8,16,64,128]{3,2,1,0:T(8,128)} fusion(f32[8,16,64,128]{3,2,1,0:T(8,128)} %constant_dynamic-update-slice_fusion.7, f32[2,16,64,128]{3,2,1,0:T(8,128)} %collective-permute-done.7), kind=kLoop, calls=%fused_computation.23 | loop fusion | bytes 2097152
  96.5 4.5 %collective-permute-done.8 = f32[16,64,128]{2,1,0:T(8,128)S(1)} collective-permute-done((f32[16,64,128]{2,1,0:T(8,128)S(1)}, f32[16,64,128]{2,1,0:T(8,128)S(1)}, u32[]{:S(2)}, u32[]{:S(2)}) %collective-permute-start.8) | collective-permute-done | bytes 524320 | tf_op jit(solution)/shard_map/ppermute | solution.py:24
  101.8 3.7 %collective-permute-done.9 = f32[16,64,128]{2,1,0:T(8,128)S(1)} collective-permute-done((f32[16,64,128]{2,1,0:T(8,128)S(1)}, f32[16,64,128]{2,1,0:T(8,128)S(1)}, u32[]{:S(2)}, u32[]{:S(2)}) %collective-permute-start.9) | collective-permute-done | bytes 524320 | tf_op jit(solution)/shard_map/ppermute | solution.py:24
  106.4 14.7 %shard_map.46 = f32[32,64,128]{2,1,0:T(8,128)} custom-call(s32[256]{0:T(256)S(1)} %fusion.6.index_ref, s32[256]{0:T(256)S(1)} %reshape_squeeze.6.rows_ref, f32[128,64,128]{2,1,0:T(8,128)} %bitcast.67, f32[96,64,128]{2,1,0:T(8,128)S(1)} %bitcast.66, f32[96,64,128]{2,1,0:T(8,128)} %bitcast.38.other_ref), custom_call_target="tpu_custom_call" | custom-call | flops 268435456 | bytes 11534336 | tf_op jit(solution)/shard_map/pallas_call | solution.py:101
  (74 shorter events, 16.0 us)
Async XLA Ops:
  0.0 8.6 %collective-permute-start.10 = (f32[6,64,128]{2,1,0:T(8,128)}, f32[6,64,128]{2,1,0:T(8,128)S(1)}, u32[]{:S(2)}, u32[]{:S(2)}) collective-permute-start(f32[6,64,128]{2,1,0:T(8,128)} %param.7), channel_id=1, source_target_pairs={{0,2},{2,0},{1,3},{3,1},{4,6},{6,4},{5,7},{7,5},{8,10},{10,8},{9,1... | collective-permute-start | bytes 589832 | tf_op jit(solution)/shard_map/ppermute | solution.py:19
  2.8 22.8 %collective-permute-start = (s32[2,32]{1,0:T(2,128)S(1)}, s32[2,32]{1,0:T(2,128)S(1)}, u32[]{:S(2)}, u32[]{:S(2)}) collective-permute-start(s32[2,32]{1,0:T(2,128)S(1)} %get-tuple-element.12), channel_id=1, source_target_pairs={{0,128},{128,0},{1,129},{129,1},{2,130},{130,2},{3,131},{131,3},{4... | collective-permute-start | bytes 776 | tf_op jit(solution)/shard_map/ppermute | solution.py:19
  5.7 9.7 %copy-start.3 = (s32[1,1,32]{2,1,0:T(1,128)S(1)}, s32[1,1,32]{2,1,0:T(1,128)}, u32[]{:S(2)}) copy-start(s32[1,1,32]{2,1,0:T(1,128)} %param.6) | copy-start | bytes 388
  5.7 9.6 %copy-start.4 = (s32[1,1,32]{2,1,0:T(1,128)S(1)}, s32[1,1,32]{2,1,0:T(1,128)}, u32[]{:S(2)}) copy-start(s32[1,1,32]{2,1,0:T(1,128)} %param.5) | copy-start | bytes 388
  7.9 50.4 %collective-permute-start.5 = (f32[16,64,128]{2,1,0:T(8,128)}, f32[16,64,128]{2,1,0:T(8,128)}, u32[]{:S(2)}, u32[]{:S(2)}) collective-permute-start(f32[16,64,128]{2,1,0:T(8,128)} %reshape.114), channel_id=1, source_target_pairs={{0,128},{128,0},{1,129},{129,1},{2,130},{130,2},{3,131},{131,3},{4... | collective-permute-start | bytes 1572872 | tf_op jit(solution)/shard_map/ppermute | solution.py:19
  8.7 20.3 %collective-permute-start.11 = (f32[2,6,64,128]{3,2,1,0:T(8,128)S(1)}, f32[2,6,64,128]{3,2,1,0:T(8,128)}, u32[]{:S(2)}, u32[]{:S(2)}) collective-permute-start(f32[2,6,64,128]{3,2,1,0:T(8,128)S(1)} %pad_maximum_fusion.1), channel_id=1, source_target_pairs={{0,28},{4,0},{8,4},{12,8},{16,12},{20,16},{24,20},{28,24},{1,29},{... | collective-permute-start | bytes 1179656 | tf_op jit(solution)/shard_map/ppermute | solution.py:24
  14.6 11.1 %collective-permute-start.15 = (f32[2,6,64,128]{3,2,1,0:T(8,128)S(1)}, f32[2,6,64,128]{3,2,1,0:T(8,128)}, u32[]{:S(2)}, u32[]{:S(2)}) collective-permute-start(f32[2,6,64,128]{3,2,1,0:T(8,128)S(1)} %pad_maximum_fusion.1), channel_id=1, source_target_pairs={{0,4},{4,8},{8,12},{12,16},{16,20},{20,24},{24,28},{28,0},{1,5},{5... | collective-permute-start | bytes 1179656 | tf_op jit(solution)/shard_map/ppermute | solution.py:24
  15.2 16.9 %copy-start = (f32[1,16,64,128]{3,2,1,0:T(8,128)}, f32[1,16,64,128]{3,2,1,0:T(8,128)S(1)}, u32[]{:S(2)}) copy-start(f32[1,16,64,128]{3,2,1,0:T(8,128)S(1)} %stack_reshape.4) | copy-start | bytes 1572868
  25.6 10.3 %collective-permute-start.16 = (f32[2,6,64,128]{3,2,1,0:T(8,128)}, f32[2,6,64,128]{3,2,1,0:T(8,128)S(1)}, u32[]{:S(2)}, u32[]{:S(2)}) collective-permute-start(f32[2,6,64,128]{3,2,1,0:T(8,128)} %collective-permute-done.15), channel_id=1, source_target_pairs={{0,4},{4,8},{8,12},{12,16},{16,20},{20,24},{24,28},{28,0},{1,5},{5... | collective-permute-start | bytes 1179656 | tf_op jit(solution)/shard_map/ppermute | solution.py:24
  25.7 32.0 %collective-permute-start.1 = (s32[2,2,32]{2,1,0:T(2,128)S(1)}, s32[2,2,32]{2,1,0:T(2,128)S(1)}, u32[]{:S(2)}, u32[]{:S(2)}) collective-permute-start(s32[2,2,32]{2,1,0:T(2,128)S(1)} %pad_add_fusion), channel_id=1, source_target_pairs={{0,32},{32,64},{64,96},{96,0},{1,33},{33,65},{65,97},{97,1},{2,34}... | collective-permute-start | bytes 1544 | tf_op jit(solution)/shard_map/ppermute | solution.py:24
  27.3 28.9 %collective-permute-start.2 = (s32[2,2,32]{2,1,0:T(2,128)S(1)}, s32[2,2,32]{2,1,0:T(2,128)S(1)}, u32[]{:S(2)}, u32[]{:S(2)}) collective-permute-start(s32[2,2,32]{2,1,0:T(2,128)S(1)} %pad_add_fusion), channel_id=1, source_target_pairs={{0,96},{32,0},{64,32},{96,64},{1,97},{33,1},{65,33},{97,65},{2,98}... | collective-permute-start | bytes 1544 | tf_op jit(solution)/shard_map/ppermute | solution.py:24
  29.0 9.3 %collective-permute-start.12 = (f32[2,6,64,128]{3,2,1,0:T(8,128)}, f32[2,6,64,128]{3,2,1,0:T(8,128)S(1)}, u32[]{:S(2)}, u32[]{:S(2)}) collective-permute-start(f32[2,6,64,128]{3,2,1,0:T(8,128)} %collective-permute-done.11), channel_id=1, source_target_pairs={{0,28},{4,0},{8,4},{12,8},{16,12},{20,16},{24,20},{28,24},{1,29},{... | collective-permute-start | bytes 1179656 | tf_op jit(solution)/shard_map/ppermute | solution.py:24
  32.2 26.2 %copy-start.1 = (f32[1,16,64,128]{3,2,1,0:T(8,128)S(1)}, f32[1,16,64,128]{3,2,1,0:T(8,128)}, u32[]{:S(2)}) copy-start(f32[1,16,64,128]{3,2,1,0:T(8,128)} %copy-done) | copy-start | bytes 1572868
  35.9 9.2 %collective-permute-start.17 = (f32[2,6,64,128]{3,2,1,0:T(8,128)S(1)}, f32[2,6,64,128]{3,2,1,0:T(8,128)S(1)}, u32[]{:S(2)}, u32[]{:S(2)}) collective-permute-start(f32[2,6,64,128]{3,2,1,0:T(8,128)S(1)} %collective-permute-done.16), channel_id=1, source_target_pairs={{0,4},{4,8},{8,12},{12,16},{16,20},{20,24},{24,28},{28,0},{1,5},{5... | collective-permute-start | bytes 1179656 | tf_op jit(solution)/shard_map/ppermute | solution.py:24
  38.3 9.5 %collective-permute-start.13 = (f32[2,6,64,128]{3,2,1,0:T(8,128)S(1)}, f32[2,6,64,128]{3,2,1,0:T(8,128)S(1)}, u32[]{:S(2)}, u32[]{:S(2)}) collective-permute-start(f32[2,6,64,128]{3,2,1,0:T(8,128)S(1)} %collective-permute-done.12), channel_id=1, source_target_pairs={{0,28},{4,0},{8,4},{12,8},{16,12},{20,16},{24,20},{28,24},{1,29},{... | collective-permute-start | bytes 1179656 | tf_op jit(solution)/shard_map/ppermute | solution.py:24
  45.2 7.0 %collective-permute-start.18 = (f32[6,64,128]{2,1,0:T(8,128)S(1)}, f32[6,64,128]{2,1,0:T(8,128)S(1)}, u32[]{:S(2)}, u32[]{:S(2)}) collective-permute-start(f32[6,64,128]{2,1,0:T(8,128)S(1)} %slice_bitcast_fusion.2), channel_id=1, source_target_pairs={{0,4},{4,8},{8,12},{12,16},{16,20},{20,24},{24,28},{28,0},{1,5},{5... | collective-permute-start | bytes 589832 | tf_op jit(solution)/shard_map/ppermute | solution.py:24
  47.8 7.1 %collective-permute-start.14 = (f32[6,64,128]{2,1,0:T(8,128)S(1)}, f32[6,64,128]{2,1,0:T(8,128)S(1)}, u32[]{:S(2)}, u32[]{:S(2)}) collective-permute-start(f32[6,64,128]{2,1,0:T(8,128)S(1)} %slice_bitcast_fusion.3), channel_id=1, source_target_pairs={{0,28},{4,0},{8,4},{12,8},{16,12},{20,16},{24,20},{28,24},{1,29},{... | collective-permute-start | bytes 589832 | tf_op jit(solution)/shard_map/ppermute | solution.py:24
  56.1 50.3 %collective-permute-start.19 = (f32[8,2,6,64,128]{4,3,2,1,0:T(8,128)S(1)}, f32[8,2,6,64,128]{4,3,2,1,0:T(8,128)}, u32[]{:S(2)}, u32[]{:S(2)}) collective-permute-start(f32[8,2,6,64,128]{4,3,2,1,0:T(8,128)S(1)} %bitcast_dynamic-update-slice_fusion.2), channel_id=1, source_target_pairs={{0,1},{1,0},{2,3},{3,2},{4,5},{5,4},{6,7},{7,6},{8,9},{9,8},{10,11... | collective-permute-start | bytes 9437192 | tf_op jit(solution)/shard_map/ppermute | solution.py:19
  56.2 6.8 %collective-permute-start.3 = (s32[2,32]{1,0:T(2,128)S(1)}, s32[2,32]{1,0:T(2,128)S(1)}, u32[]{:S(2)}, u32[]{:S(2)}) collective-permute-start(s32[2,32]{1,0:T(2,128)S(1)} %slice_bitcast_fusion.5), channel_id=1, source_target_pairs={{0,96},{32,0},{64,32},{96,64},{1,97},{33,1},{65,33},{97,65},{2,98}... | collective-permute-start | bytes 776 | tf_op jit(solution)/shard_map/ppermute | solution.py:24
  57.6 5.4 %collective-permute-start.4 = (s32[2,32]{1,0:T(2,128)S(1)}, s32[2,32]{1,0:T(2,128)S(1)}, u32[]{:S(2)}, u32[]{:S(2)}) collective-permute-start(s32[2,32]{1,0:T(2,128)S(1)} %slice_bitcast_fusion.4), channel_id=1, source_target_pairs={{0,32},{32,64},{64,96},{96,0},{1,33},{33,65},{65,97},{97,1},{2,34}... | collective-permute-start | bytes 776 | tf_op jit(solution)/shard_map/ppermute | solution.py:24
  60.5 25.3 %collective-permute-start.7 = (f32[2,16,64,128]{3,2,1,0:T(8,128)}, f32[2,16,64,128]{3,2,1,0:T(8,128)}, u32[]{:S(2)}, u32[]{:S(2)}) collective-permute-start(f32[2,16,64,128]{3,2,1,0:T(8,128)} %pad_maximum_fusion), channel_id=1, source_target_pairs={{0,96},{32,0},{64,32},{96,64},{1,97},{33,1},{65,33},{97,65},{2,98}... | collective-permute-start | bytes 3145736 | tf_op jit(solution)/shard_map/ppermute | solution.py:24
  63.0 27.6 %collective-permute-start.6 = (f32[2,16,64,128]{3,2,1,0:T(8,128)}, f32[2,16,64,128]{3,2,1,0:T(8,128)}, u32[]{:S(2)}, u32[]{:S(2)}) collective-permute-start(f32[2,16,64,128]{3,2,1,0:T(8,128)} %pad_maximum_fusion), channel_id=1, source_target_pairs={{0,32},{32,64},{64,96},{96,0},{1,33},{33,65},{65,97},{97,1},{2,34}... | collective-permute-start | bytes 3145736 | tf_op jit(solution)/shard_map/ppermute | solution.py:24
  86.8 14.1 %collective-permute-start.8 = (f32[16,64,128]{2,1,0:T(8,128)S(1)}, f32[16,64,128]{2,1,0:T(8,128)S(1)}, u32[]{:S(2)}, u32[]{:S(2)}) collective-permute-start(f32[16,64,128]{2,1,0:T(8,128)S(1)} %slice_bitcast_fusion.1), channel_id=1, source_target_pairs={{0,96},{32,0},{64,32},{96,64},{1,97},{33,1},{65,33},{97,65},{2,98}... | collective-permute-start | bytes 1572872 | tf_op jit(solution)/shard_map/ppermute | solution.py:24
  91.7 13.8 %collective-permute-start.9 = (f32[16,64,128]{2,1,0:T(8,128)S(1)}, f32[16,64,128]{2,1,0:T(8,128)S(1)}, u32[]{:S(2)}, u32[]{:S(2)}) collective-permute-start(f32[16,64,128]{2,1,0:T(8,128)S(1)} %slice_bitcast_fusion), channel_id=1, source_target_pairs={{0,32},{32,64},{64,96},{96,0},{1,33},{33,65},{65,97},{97,1},{2,34}... | collective-permute-start | bytes 1572872 | tf_op jit(solution)/shard_map/ppermute | solution.py:24
  (1 other events, 8.6 us)
